TPU v7x, 128 devices: a whole 4x4x4 slice. The times are simulated.
128 devices in a mesh: pairs: 16 (over z_hi, x, core), band: 8 (over y, z_lo).
Axes of the slice: x: 4, y: 4, z: 4 (z_hi: 2, z_lo: 2; z = z_hi * 2 + z_lo), core: 2. Of those that a mesh axis runs over, the one named last changes fastest.
Arguments:
- spectra: bfloat16 [8192, 8, 1024], P('pairs', 'band'), may hold values from -15 to 15
- observed: bfloat16 [32768, 8, 1024], P('pairs', 'band'), may hold values from -5 to 5
- pair_owner: int32 [32768, 2], P('pairs'), may hold values from 0 to 15, all different within a row; in each aligned block of 2048 rows (0 to 2047, 2048 to 4095, ...) at most 384 rows name the same one
- pair_slot: int32 [32768, 2], P('pairs'), may hold values from 0 to 511
- win_start: int32 [32768], P('pairs'), may hold values from 0 to 511
- win_end: int32 [32768], P('pairs'), may hold values from 513 to 1024
Outputs:
- noise_kernel: float32 [8192, 8, 512], P('pairs', 'band')
Inputs may be any that keep to these rules, and one draw needn't show every extreme that they name: `pair_owner`: the two stations of a pair have different owners; among the pairs of one index of pairs no owner is named more than 384 times, a bound that some block reaches.
All inputs are finite; a program needn't handle non-finite values.
Results may differ from a plain program's by a relative error of at most 0.006.
Values may be sent and summed in bfloat16 or wider, within the bound.
No kernel may reach another device: no remote copies, remote signals or barrier semaphores. Data moves between devices by JAX's collectives and lax.ppermute only.
A program may use at most 128 MiB of HBM per device.

v0:
```python
import math

import jax
import jax.numpy as jnp
from jax import lax
from jax.sharding import PartitionSpec as P


def lag_basis(half_width, lag_count):
    freqs = jnp.arange(half_width, dtype=jnp.int32)
    lag_index = jnp.arange(lag_count, dtype=jnp.int32)
    phases = (freqs[:, None] * lag_index[None, :] % lag_count).astype(jnp.float32) * (
        2.0 * math.pi / lag_count
    )
    factor = 1.0 / math.sqrt(lag_count)
    return jnp.concatenate([jnp.cos(phases) * factor, -jnp.sin(phases) * factor], axis=0).astype(
        jnp.bfloat16
    )


def owner_positions(owner_flat, owner_count):
    onehot = (owner_flat[:, None] == jnp.arange(owner_count, dtype=jnp.int32)[None, :]).astype(
        jnp.int32
    )
    before = jnp.cumsum(onehot, axis=0) - onehot
    return jnp.sum(before * onehot, axis=1)


def shards(spectra, observed, pair_owner, pair_slot, win_start, win_end):
    owners = lax.axis_size("pairs")
    station_count = spectra.shape[0]
    band_count = spectra.shape[1]
    full_width = spectra.shape[2]
    half_width = full_width // 2
    pair_count = observed.shape[0]
    lag_count = observed.shape[2]
    capacity = 3 * pair_count // owners
    spectrum = spectra.astype(jnp.float32)
    local_power = jnp.sum(spectrum * spectrum, axis=(1, 2))
    total_power = lax.psum(local_power, "band")
    entries = band_count * lax.axis_size("band") * full_width
    whitened = (spectrum * lax.rsqrt(total_power / entries + 1e-05)[:, None, None]).astype(
        jnp.bfloat16
    )
    owner_flat = pair_owner.reshape(-1)
    slot_flat = pair_slot.reshape(-1)
    position = owner_positions(owner_flat, owners)
    request = (
        jnp.full((owners, capacity), station_count, jnp.int32)
        .at[owner_flat, position]
        .set(slot_flat)
    )
    wanted = lax.all_to_all(request, "pairs", split_axis=0, concat_axis=0, tiled=True)
    panel_rows = lax.all_gather(whitened, "pairs", axis=0, tiled=True)
    fetched = panel_rows[owner_flat * station_count + slot_flat]
    fetched = fetched.reshape(pair_count, 2, band_count, full_width)
    near_end = fetched[:, 0].astype(jnp.float32)
    far_end = fetched[:, 1].astype(jnp.float32)
    near_re, near_im = (near_end[..., :half_width], near_end[..., half_width:])
    far_re, far_im = (far_end[..., :half_width], far_end[..., half_width:])
    cross_spec = jnp.concatenate(
        [near_re * far_re + near_im * far_im, near_im * far_re - near_re * far_im], axis=-1
    ).astype(jnp.bfloat16)
    table = lag_basis(half_width, lag_count)
    lagged = jnp.einsum("pbf,ft->pbt", cross_spec, table, preferred_element_type=jnp.float32)
    lag_index = jnp.arange(lag_count, dtype=jnp.int32)
    window = (
        (lag_index[None, :] >= win_start[:, None]) & (lag_index[None, :] < win_end[:, None])
    ).astype(jnp.float32)
    residual = (window[:, None, :] * (lagged - observed.astype(jnp.float32))).astype(jnp.bfloat16)
    adjoint = jnp.einsum("pbt,ft->pbf", residual, table, preferred_element_type=jnp.float32)
    adj_re, adj_im = (adjoint[..., :half_width], adjoint[..., half_width:])
    to_first = jnp.concatenate(
        [adj_re * far_re - adj_im * far_im, adj_re * far_im + adj_im * far_re], axis=-1
    ).astype(jnp.bfloat16)
    to_second = jnp.concatenate(
        [adj_re * near_re + adj_im * near_im, adj_re * near_im - adj_im * near_re], axis=-1
    ).astype(jnp.bfloat16)
    stacked = jnp.stack([to_first, to_second], axis=1).reshape(
        2 * pair_count, band_count, full_width
    )
    outgoing = (
        jnp.zeros((owners, capacity, band_count, full_width), jnp.bfloat16)
        .at[owner_flat, position]
        .set(stacked)
    )
    incoming = lax.all_to_all(outgoing, "pairs", split_axis=0, concat_axis=0, tiled=True)

    def add_source(source, summed):
        block_rows = lax.dynamic_index_in_dim(incoming, source, 0, keepdims=False).astype(
            jnp.float32
        )
        block_ids = lax.dynamic_index_in_dim(wanted, source, 0, keepdims=False)
        return summed.at[block_ids].add(block_rows)

    summed = lax.fori_loop(
        0, owners, add_source, jnp.zeros((station_count + 1, band_count, full_width), jnp.float32)
    )
    summed = summed[:station_count]
    own_spec = whitened.astype(jnp.float32)
    return 0.25 * (
        summed[..., :half_width] * own_spec[..., :half_width]
        + summed[..., half_width:] * own_spec[..., half_width:]
    )


def solution(mesh):
    return jax.shard_map(
        shards,
        mesh=mesh,
        in_specs=(
            P("pairs", "band", None),
            P("pairs", "band", None),
            P("pairs", None),
            P("pairs", None),
            P("pairs"),
            P("pairs"),
        ),
        out_specs=P("pairs", "band", None),
        check_vma=False,
    )
```

profile of v0, /device:TPU:1, one launch (start us, length us, event | category | flops | bytes accessed | tf_op | source)
XLA Modules:
  0.0 617.7 jit_solution(1249536567660089162)
XLA Ops:
  8.1 17.4 %psum.7 = f32[512]{0:T(512)S(1)} all-reduce(f32[512]{0:T(512)S(1)} %fusion.14), channel_id=1, replica_groups=mesh['pairs'=16,'band'=8] {'band'}, use_global_device_ids=true, to_apply=%region_4.5 | all-reduce | flops 512 | bytes 4096 | tf_op jit(solution)/shard_map/psum | solution.py:40
  38.1 16.1 %scatter_custom_fusion.1 = s32[6144]{0:T(1024)} fusion(s32[4096]{0:T(1024)S(1)} %broadcast_select_fusion, s32[4096]{0:T(1024)S(1)} %reshape.381, s32[]{:T(128)} %constant.75.clone.1), kind=kCustom, calls=%fused_computation.74 | custom fusion | bytes 24580
  54.2 12.2 %all-to-all-start = ((s32[16,1,384]{2,1,0:T(1,128)}), s32[16,1,384]{2,1,0:T(1,128)S(1)}, u32[]{:S(2)}, u32[]{:S(2)}) async-start(s32[16,1,384]{2,1,0:T(1,128)} %bitcast.6), calls=%async_computation | async-start | bytes 49152 | tf_op jit(solution)/shard_map/all_to_all | solution.py:53
  66.4 9.2 %multiply_convert_fusion = (bf16[512,1024]{1,0:T(8,128)(2,1)S(1)}, bf16[512,1024]{1,0:T(8,128)(2,1)}) fusion(), kind=kLoop, calls=%fused_computation.49 | loop fusion | flops 9961472 | bytes 2097152 | tf_op jit(solution)/shard_map/convert.12
  75.6 67.5 %all-gather.2.cloned.1.call-done = bf16[8192,1,1024]{2,0,1:T(8,128)(2,1)} async-done(((bf16[512,1,1024]{2,0,1:T(8,128)(2,1)}), bf16[8192,1,1024]{2,0,1:T(8,128)(2,1)}) %all-gather.2.cloned.1.call-update) | async-done | bytes 16777232 | tf_op jit(solution)/shard_map/all_gather | solution.py:54
  143.1 28.8 %gather_fusion = bf16[4096,1024]{1,0:T(8,128)(2,1)} fusion(bf16[8192,1024]{1,0:T(8,128)(2,1)} %bitcast.79, s32[4096]{0:T(1024)S(1)} %broadcast_clamp_fusion), kind=kCustom, calls=%fused_computation | custom fusion | bytes 16793600 | tf_op jit(solution)/shard_map/gather | solution.py:55
  171.9 13.1 %reshape.340 = bf16[2048,2,1,1024]{3,1,0,2:T(2,128)(2,1)} reshape(bf16[4096,1024]{1,0:T(8,128)(2,1)} %gather_fusion) | data formatting | bytes 16777216 | tf_op jit(solution)/shard_map/reshape | solution.py:56
  185.0 17.2 %fusion.45 = (bf16[2048,1,1,1024]{3,1,0,2:T(2,128)(2,1)}, bf16[2048,1,1,1024]{3,1,0,2:T(2,128)(2,1)}) fusion(bf16[2048,2,1,1024]{3,1,0,2:T(2,128)(2,1)} %reshape.340), kind=kLoop, calls=%fused_computation.82 | loop fusion | bytes 16777216 | tf_op jit(solution)/shard_map/slice | solution.py:58
  202.3 20.1 %copy.28 = bf16[2048,1,1,1024]{0,3,2,1:T(8,128)(2,1)} copy(bf16[2048,1,1,1024]{3,1,0,2:T(2,128)(2,1)} %get-tuple-element.103) | data formatting | bytes 8388608
  222.3 6.7 %bitcast_convert_fusion = f32[2048,1,1024]{0,2,1:T(8,128)} fusion(bf16[2048,1,1,1024]{0,3,2,1:T(8,128)(2,1)} %copy.28), kind=kLoop, calls=%fused_computation.24 | loop fusion | flops 2097152 | bytes 12582912 | tf_op jit(solution)/shard_map/convert_element_type | solution.py:58
  229.0 20.0 %copy.27 = bf16[2048,1,1,1024]{0,3,2,1:T(8,128)(2,1)} copy(bf16[2048,1,1,1024]{3,1,0,2:T(2,128)(2,1)} %get-tuple-element.104) | data formatting | bytes 8388608
  258.3 16.3 %convolution_bitcast_fusion = f32[2048,1,1024]{0,2,1:T(8,128)} fusion(bf16[2048,1,1024]{2,0,1:T(8,128)(2,1)} %param.9, bf16[2048,512]{0,1:T(8,128)(2,1)} %get-tuple-element.100, bf16[2048,512]{0,1:T(8,128)(2,1)S(1)} %get-tuple-element.99, s32[2048]{0:T(1024)S(1)} %copy-done.6, s32[2048]{0:T(1024)S(1)} %copy-done.7, ...), kind=kOutput, calls=%fused_computation.19 | convolution fusion | flops 8621391872 | bytes 18890752 | tf_op jit(solution)/shard_map/pbt,ft->pbf/dot_general | solution.py:71
  274.6 10.1 %fusion.21 = (bf16[2048,1,1,512]{0,3,2,1:T(8,128)(2,1)S(1)}, bf16[2048,1,1,512]{0,3,2,1:T(8,128)(2,1)S(1)}, bf16[2048,1,1,512]{0,3,2,1:T(8,128)(2,1)S(1)}, bf16[2048,1,1,512]{0,3,2,1:T(8,128)(2,1)S(1)}) fusion(f32[2048,1,1024]{0,2,1:T(8,128)} %bitcast_convert_fusion, f32[2048,1,1024]{0,2,1:T(8,128)} %convolution_bitcast_fusion, f32[2048,1,1024]{0,2,1:T(8,128)} %copy-done.1), kind=kLoop, calls=%fused_computation.44 | loop fusion | flops 16777216 | bytes 33554432 | tf_op jit(solution)/shard_map/concatenate | solution.py:73
  288.8 21.4 %copy.24 = bf16[2048,2,1,1024]{3,1,0,2:T(2,128)(2,1)} copy(bf16[2048,2,1,1024]{0,3,2,1:T(8,128)(2,1)} %maximum_maximum_fusion) | data formatting | bytes 16777216 | tf_op jit(solution)/shard_map/stack | solution.py:79
  310.1 13.3 %reshape.391 = bf16[4096,1024]{1,0:T(8,128)(2,1)} reshape(bf16[2048,2,1,1024]{3,1,0,2:T(2,128)(2,1)} %copy.24) | data formatting | bytes 16777216 | tf_op jit(solution)/shard_map/reshape | solution.py:79
  323.4 26.5 %scatter_custom_fusion.2 = bf16[6144,1024]{1,0:T(8,128)(2,1)} fusion(s32[4096]{0:T(1024)S(1)} %broadcast_select_fusion, bf16[4096,1024]{1,0:T(8,128)(2,1)} %reshape.391, bf16[]{:T(256)} %constant.70.clone.1), kind=kCustom, calls=%fused_computation.17 | custom fusion | bytes 12583424
  349.9 5.3 all-to-all-start.1
  355.2 168.2 %all-to-all-done.1 = bf16[16,384,1,1024]{3,1,2,0:T(8,128)(2,1)} async-done(((bf16[16,384,1,1024]{3,1,2,0:T(8,128)(2,1)}), bf16[16,384,1,1024]{3,1,2,0:T(8,128)(2,1)}, u32[]{:S(2)}, u32[]{:S(2)}) %all-to-all-start.1) | async-done | bytes 12582944 | tf_op jit(solution)/shard_map/all_to_all | solution.py:87
  523.7 82.8 %while.13 = (s32[]{:T(128)}, f32[513,1,1024]{2,0,1:T(8,128)S(1)}, s32[16,384]{1,0:T(8,128)S(1)}, bf16[16,384,1,1024]{3,1,2,0:T(8,128)(2,1)}, s32[]{:T(128)}, /*index=5*/s32[]{:T(128)}) while((s32[]{:T(128)}, f32[513,1,1024]{2,0,1:T(8,128)S(1)}, s32[16,384]{1,0:T(8,128)S(1)}, bf16[16,384,1,1024]{3,1,2,0:T(8,128)(2,1)}, s32[]{:T(128)}, ...), condition=%wide.region_9.10_spmd, body=%wide.region_7.9_spmd.sunk | while | flops 787586 | bytes 2891849 | solution.py:96
  523.7 5.1 scatter_custom_fusion.9
  528.9 5.1 scatter_custom_fusion.9
  534.1 5.1 scatter_custom_fusion.9
  539.3 5.1 scatter_custom_fusion.9
  601.4 5.1 scatter_custom_fusion.9
  (74 shorter events, 88.5 us)
Async XLA Ops:
  6.5 22.1 %copy-start.2 = (s32[2048,2]{0,1:T(2,128)S(1)}, s32[2048,2]{0,1:T(2,128)}, u32[]{:S(2)}) copy-start(s32[2048,2]{0,1:T(2,128)} %param.10) | copy-start | bytes 49156
  6.5 136.5 %all-gather.2.cloned.1.call-start = ((), (), s32[]{:S(2)}) async-start(), calls=%async_computation.2 | async-start | bytes 17825792 | tf_op jit(solution)/shard_map/all_gather | solution.py:54
  25.4 5.2 copy-start.3
  29.0 8.8 %copy-start.5 = (s32[2]{0:T(128)S(1)}, s32[2]{0:T(128)}, u32[]{:S(2)}) copy-start(s32[2]{0:T(128)} %constant.84) | copy-start | bytes 28
  29.0 8.9 %copy-start.4 = (s32[2]{0:T(128)S(1)}, s32[2]{0:T(128)}, u32[]{:S(2)}) copy-start(s32[2]{0:T(128)} %constant.87) | copy-start | bytes 28
  54.2 295.7 %all-to-all-start = ((s32[16,1,384]{2,1,0:T(1,128)}), s32[16,1,384]{2,1,0:T(1,128)S(1)}, u32[]{:S(2)}, u32[]{:S(2)}) async-start(s32[16,1,384]{2,1,0:T(1,128)} %bitcast.6), calls=%async_computation | async-start | bytes 49152 | tf_op jit(solution)/shard_map/all_to_all | solution.py:53
  249.0 4.6 copy-start
  253.7 4.6 copy-start.1
  253.7 4.6 copy-start.6
  253.7 4.6 copy-start.7
  349.9 173.5 %all-to-all-start.1 = ((bf16[16,384,1,1024]{3,1,2,0:T(8,128)(2,1)}), bf16[16,384,1,1024]{3,1,2,0:T(8,128)(2,1)}, u32[]{:S(2)}, u32[]{:S(2)}) async-start(bf16[16,384,1,1024]{3,1,2,0:T(8,128)(2,1)} %bitcast.80), calls=%async_computation.1 | async-start | bytes 25165824 | tf_op jit(solution)/shard_map/all_to_all | solution.py:87
Sparse Core Ops, SparseCore 0:
  28.8 114.2 all-gather.1
where the time goes:
time: 626 us; the launch traced here: 618 us
  waiting for transfers between devices  236 us (38%)
  local copies, waits for them, and re-layouts  184 us (29%)
  other arithmetic  133 us (21%)
  starting transfers between devices  17.5 us (3%)
  blocking collectives  17.4 us (3%)
  matrix products  16.3 us (3%)
  between operations  13.9 us (2%)
    all_to_all x1, waiting for transfers between devices, shards(): lax.all_to_all(outgoing, 'pairs', split_axis=0, concat_axis=0, tiled=True)  168 us
    unnamed x23, local copies, waits for them, and re-layouts  84.7 us
    scatter-add x16, other arithmetic, add_source(): return summed.at[block_ids].add(block_rows)  82 us
    all_gather x1, waiting for transfers between devices, shards(): panel_rows = lax.all_gather(whitened, 'pairs', axis=0, tiled=True)  67.5 us
    gather x1, local copies, waits for them, and re-layouts, shards(): fetched = panel_rows[owner_flat * station_count + slot_flat]  28.8 us
    another operation x1, local copies, waits for them, and re-layouts, shards(): jnp.stack([to_first, to_second], axis=1)  21.4 us
    psum x1, blocking collectives, shards(): total_power = lax.psum(local_power, 'band')  17.4 us
    slice x1, local copies, waits for them, and re-layouts, shards(): far_end = fetched[:, 1].astype(jnp.float32)  17.2 us
  transfers between devices with their start and end apart: 3, of which 2 were waited for; matrix products, arithmetic and copies ran while one was open for 39% of the time, Pallas kernels for 0%

commit v1 on v0

v1 whole, which is shorter than its diff:
```python
import math

import jax
import jax.numpy as jnp
from jax import lax
from jax.sharding import PartitionSpec as P


def lag_basis(half_width, lag_count):
    freqs = jnp.arange(half_width, dtype=jnp.int32)
    lag_index = jnp.arange(lag_count, dtype=jnp.int32)
    phases = (freqs[:, None] * lag_index[None, :] % lag_count).astype(jnp.float32) * (
        2.0 * math.pi / lag_count
    )
    factor = 1.0 / math.sqrt(lag_count)
    return jnp.concatenate([jnp.cos(phases) * factor, -jnp.sin(phases) * factor], axis=0).astype(
        jnp.bfloat16
    )


def owner_positions(owner_flat, owner_count):
    onehot = (owner_flat[:, None] == jnp.arange(owner_count, dtype=jnp.int32)[None, :]).astype(
        jnp.int32
    )
    before = jnp.cumsum(onehot, axis=0) - onehot
    return jnp.sum(before * onehot, axis=1)


def shards(spectra, observed, pair_owner, pair_slot, win_start, win_end):
    owners = lax.axis_size("pairs")
    station_count = spectra.shape[0]
    band_count = spectra.shape[1]
    full_width = spectra.shape[2]
    half_width = full_width // 2
    pair_count = observed.shape[0]
    lag_count = observed.shape[2]
    capacity = 3 * pair_count // owners
    raw = spectra.reshape(station_count, full_width)
    panel_raw = lax.all_gather(raw, "pairs", axis=0, tiled=True)
    spectrum = raw.astype(jnp.float32)
    local_power = jnp.sum(spectrum * spectrum, axis=1)
    total_power = lax.psum(local_power, "band")
    entries = band_count * lax.axis_size("band") * full_width
    scale = lax.rsqrt(total_power / entries + 1e-05)
    own_spec = (spectrum * scale[:, None]).astype(jnp.bfloat16).astype(jnp.float32)
    panel_scale = lax.all_gather(scale, "pairs", axis=0, tiled=True)

    owner_flat = pair_owner.reshape(-1)
    slot_flat = pair_slot.reshape(-1)
    position = owner_positions(owner_flat, owners)
    flat_slot = owner_flat * capacity + position
    request = (
        jnp.full((owners * capacity,), station_count, jnp.int32)
        .at[flat_slot]
        .set(slot_flat, unique_indices=True)
    )
    wanted = lax.all_to_all(
        request.reshape(owners, capacity), "pairs", split_axis=0, concat_axis=0, tiled=True
    ).reshape(owners * capacity)

    rows0 = pair_owner[:, 0] * station_count + pair_slot[:, 0]
    rows1 = pair_owner[:, 1] * station_count + pair_slot[:, 1]
    near_end = panel_raw[rows0].astype(jnp.float32) * panel_scale[rows0][:, None]
    far_end = panel_raw[rows1].astype(jnp.float32) * panel_scale[rows1][:, None]
    near_end = near_end.astype(jnp.bfloat16).astype(jnp.float32)
    far_end = far_end.astype(jnp.bfloat16).astype(jnp.float32)
    near_re, near_im = (near_end[:, :half_width], near_end[:, half_width:])
    far_re, far_im = (far_end[:, :half_width], far_end[:, half_width:])
    cross_spec = jnp.concatenate(
        [near_re * far_re + near_im * far_im, near_im * far_re - near_re * far_im], axis=-1
    ).astype(jnp.bfloat16)
    table = lag_basis(half_width, lag_count)
    lagged = jnp.dot(cross_spec, table, preferred_element_type=jnp.float32)
    lag_index = jnp.arange(lag_count, dtype=jnp.int32)
    window = (lag_index[None, :] >= win_start[:, None]) & (lag_index[None, :] < win_end[:, None])
    obs = observed.reshape(pair_count, lag_count).astype(jnp.float32)
    residual = jnp.where(window, lagged - obs, 0.0).astype(jnp.bfloat16)
    adjoint = lax.dot_general(
        residual, table, (((1,), (1,)), ((), ())), preferred_element_type=jnp.float32
    )
    adj_re, adj_im = (adjoint[:, :half_width], adjoint[:, half_width:])
    to_first = jnp.concatenate(
        [adj_re * far_re - adj_im * far_im, adj_re * far_im + adj_im * far_re], axis=-1
    ).astype(jnp.bfloat16)
    to_second = jnp.concatenate(
        [adj_re * near_re + adj_im * near_im, adj_re * near_im - adj_im * near_re], axis=-1
    ).astype(jnp.bfloat16)
    stacked = jnp.stack([to_first, to_second], axis=1).reshape(2 * pair_count, full_width)
    outgoing = (
        jnp.zeros((owners * capacity, full_width), jnp.bfloat16)
        .at[flat_slot]
        .set(stacked, unique_indices=True)
    )
    incoming = lax.all_to_all(
        outgoing.reshape(owners, capacity, full_width),
        "pairs",
        split_axis=0,
        concat_axis=0,
        tiled=True,
    ).reshape(owners * capacity, full_width)
    onehot = (
        wanted[None, :] == jnp.arange(station_count, dtype=jnp.int32)[:, None]
    ).astype(jnp.bfloat16)
    summed = jnp.dot(onehot, incoming, preferred_element_type=jnp.float32)
    result = 0.25 * (
        summed[:, :half_width] * own_spec[:, :half_width]
        + summed[:, half_width:] * own_spec[:, half_width:]
    )
    return result.reshape(station_count, band_count, half_width)


def solution(mesh):
    return jax.shard_map(
        shards,
        mesh=mesh,
        in_specs=(
            P("pairs", "band", None),
            P("pairs", "band", None),
            P("pairs", None),
            P("pairs", None),
            P("pairs"),
            P("pairs"),
        ),
        out_specs=P("pairs", "band", None),
        check_vma=False,
    )
```

time: 626 us -> 487 us (0.78)
  other arithmetic: 133 us -> 51.1 us
  waiting for transfers between devices: 236 us -> 172 us
  blocking collectives: 17.4 us -> 45.3 us
  local copies, waits for them, and re-layouts: 184 us -> 158 us
  matrix products: 16.3 us -> 26.4 us
    unnamed x23 -> x14, local copies, waits for them, and re-layouts: 84.7 us -> 1.47 us
    scatter-add x16 -> x0, other arithmetic: 82 us -> none  [add_source(): return summed.at[block_ids].add(block_rows)]
    all_gather x1, waiting for transfers between devices: 67.5 us -> 4.43 us  [shards(): panel_raw = lax.all_gather(raw, 'pairs', axis=0, tiled=True)]
    gather x1 -> x6, local copies, waits for them, and re-layouts: 28.8 us -> 74.4 us  [the longest x3 37.1 us: shards(): far_end = panel_raw[rows1].astype(jnp.float32) * panel_scale[rows1][:, None]]
    scatter x0 -> x2, local copies, waits for them, and re-layouts: none -> 42.6 us  [the longest x1 26.5 us: shards(): outgoing = jnp.zeros((owners * capacity, full_width), jnp.bfloat16).at[fl...]
    all_gather x0 -> x1, blocking collectives: none -> 29.2 us  [shards(): panel_scale = lax.all_gather(scale, 'pairs', axis=0, tiled=True)]
    slice x2 -> x1, local copies, waits for them, and re-layouts: 17.7 us -> 0.46 us  [the longest x1 17.2 us: shards(): far_end = fetched[:, 1].astype(jnp.float32)]
    reshape x3 -> x2, local copies, waits for them, and re-layouts: 27 us -> 15.4 us  [the longest x1 13.3 us: shards(): jnp.stack([to_first, to_second], axis=1).reshape(2 * pair_count, full_width)]
  transfers between devices with their start and end apart: 3 -> 3, of which waited for: 2 -> 2; matrix products, arithmetic and copies ran while one was open for 39% -> 46% of each run, Pallas kernels for 0% -> 0%
where the time goes in v1:
time: 487 us; the launch traced here: 481 us
  waiting for transfers between devices  172 us (35%)
  local copies, waits for them, and re-layouts  158 us (32%)
  other arithmetic  51.1 us (10%)
  blocking collectives  45.3 us (9%)
  matrix products  26.4 us (5%)
  starting transfers between devices  14.5 us (3%)
  between operations  14.1 us (3%)
    all_to_all x1, waiting for transfers between devices, shards(): lax.all_to_all(outgoing.reshape(owners, capacity, full_width), 'pairs', s...  167 us
    gather x3, local copies, waits for them, and re-layouts, shards(): far_end = panel_raw[rows1].astype(jnp.float32) * panel_scale[rows1][:, None]  37.1 us
    all_gather x1, blocking collectives, shards(): panel_scale = lax.all_gather(scale, 'pairs', axis=0, tiled=True)  29.2 us
    scatter x1, local copies, waits for them, and re-layouts, shards(): outgoing = jnp.zeros((owners * capacity, full_width), jnp.bfloat16).at[fl...  26.5 us
    gather x2, local copies, waits for them, and re-layouts, shards(): panel_raw[rows0].astype(jnp.float32) * panel_scale[rows0][:, None]  25.4 us
    another operation x5, other arithmetic  22.6 us
    another operation x1, local copies, waits for them, and re-layouts, shards(): jnp.stack([to_first, to_second], axis=1).reshape(2 * pair_count, full_width)  21.4 us
    dot_general x1, matrix products, shards(): lax.dot_general(residual, table, (((1,), (1,)), ((), ())), preferred_elem...  16.3 us
  transfers between devices with their start and end apart: 3, of which 2 were waited for; matrix products, arithmetic and copies ran while one was open for 46% of the time, Pallas kernels for 0%

profile of v1, /device:TPU:1, one launch (start us, length us, event | category | flops | bytes accessed | tf_op | source)
XLA Modules:
  0.0 481.2 jit_solution(8328400754011136342)
XLA Ops:
  9.3 4.6 reduce-window.6
  16.9 16.1 %scatter_custom_fusion = s32[6144]{0:T(1024)} fusion(s32[4096]{0:T(1024)S(1)} %bitcast.62, s32[4096]{0:T(1024)S(1)} %reshape.184, s32[]{:T(128)} %constant.14.clone.1), kind=kCustom, calls=%fused_computation.75 | custom fusion | bytes 24580 | tf_op jit(solution)/shard_map/scatter | solution.py:55
  33.0 9.1 %all-to-all-start = ((s32[16,1,384]{2,1,0:T(1,128)}), s32[16,1,384]{2,1,0:T(1,128)S(1)}, u32[]{:S(2)}, u32[]{:S(2)}) async-start(s32[16,1,384]{2,1,0:T(1,128)} %bitcast.3), calls=%async_computation | async-start | bytes 49152 | tf_op jit(solution)/shard_map/all_to_all | solution.py:57
  42.4 16.1 %psum.7 = f32[512]{0:T(512)S(1)} all-reduce(f32[512]{0:T(512)S(1)} %fusion.19), channel_id=1, replica_groups=mesh['pairs'=16,'band'=8] {'band'}, use_global_device_ids=true, to_apply=%region_5.6 | all-reduce | flops 512 | bytes 4096 | tf_op jit(solution)/shard_map/psum | solution.py:42
  58.5 29.2 %all-gather.1 = f32[16,1,512]{2,1,0:T(1,128)S(1)} all-gather(f32[1,1,512]{2,1,0:T(1,128)S(1)} %bitcast.61), channel_id=1, replica_groups=mesh['pairs'=16,'band'=8] {'pairs'}, dimensions={0}, use_global_device_ids=true | all-gather | bytes 34816 | tf_op jit(solution)/shard_map/all_gather | solution.py:46
  87.7 11.8 %gather_fusion.1 = f32[2048]{0:T(1024)S(1)} fusion(f32[8192]{0:T(1024)S(1)} %bitcast.50, s32[2048]{0:T(1024)S(1)} %broadcast_clamp_fusion.1), kind=kCustom, calls=%fused_computation.1 | custom fusion | bytes 24576 | tf_op jit(solution)/shard_map/gather | solution.py:63
  99.5 11.8 %gather_fusion.3 = f32[2048]{0:T(1024)S(1)} fusion(f32[8192]{0:T(1024)S(1)} %bitcast.51, s32[2048]{0:T(1024)S(1)} %broadcast_clamp_fusion), kind=kCustom, calls=%fused_computation.3 | custom fusion | bytes 24576 | tf_op jit(solution)/shard_map/gather | solution.py:64
  111.3 8.6 %multiply_convert_fusion.2 = (bf16[512,1024]{1,0:T(8,128)(2,1)S(1)}, bf16[512,1024]{1,0:T(8,128)(2,1)S(1)}) fusion(), kind=kLoop, calls=%fused_computation.52 | loop fusion | flops 9961472 | bytes 2097152 | tf_op jit(solution)/shard_map/convert.10
  119.8 4.4 all-gather.4.cloned.1.call-done
  124.3 18.9 %gather_fusion = bf16[2048,1024]{1,0:T(8,128)(2,1)} fusion(bf16[8192,1024]{1,0:T(8,128)(2,1)} %bitcast.52, s32[2048]{0:T(1024)S(1)} %broadcast_clamp_fusion.1), kind=kCustom, calls=%fused_computation | custom fusion | bytes 8396800 | tf_op jit(solution)/shard_map/gather | solution.py:63
  143.2 18.9 %gather_fusion.2 = bf16[2048,1024]{1,0:T(8,128)(2,1)} fusion(bf16[8192,1024]{1,0:T(8,128)(2,1)} %bitcast.53, s32[2048]{0:T(1024)S(1)} %broadcast_clamp_fusion), kind=kCustom, calls=%fused_computation.2 | custom fusion | bytes 8396800 | tf_op jit(solution)/shard_map/gather | solution.py:64
  162.1 6.5 %copy.22 = bf16[2048,1024]{0,1:T(8,128)(2,1)} copy(bf16[2048,1024]{1,0:T(8,128)(2,1)} %gather_fusion) | data formatting | bytes 8388608 | tf_op jit(solution)/shard_map/gather | solution.py:63
  168.6 6.5 %copy.23 = bf16[2048,1024]{0,1:T(8,128)(2,1)} copy(bf16[2048,1024]{1,0:T(8,128)(2,1)} %gather_fusion.2) | data formatting | bytes 8388608 | tf_op jit(solution)/shard_map/gather | solution.py:64
  175.1 11.6 %fusion.7 = (f32[2048,1024]{0,1:T(8,128)}, f32[2048,1024]{0,1:T(8,128)}) fusion(bf16[2048,1024]{0,1:T(8,128)(2,1)} %copy.22, f32[2048]{0:T(1024)S(1)} %gather_fusion.1, f32[2048]{0:T(1024)S(1)} %gather_fusion.3, bf16[2048,1024]{0,1:T(8,128)(2,1)} %copy.23), kind=kLoop, calls=%fused_computation.20 | loop fusion | flops 16777216 | bytes 25182208 | tf_op jit(solution)/shard_map/convert_element_type | solution.py:65
  186.7 9.1 %add_convert_fusion.2 = (bf16[2048,512]{0,1:T(8,128)(2,1)}, bf16[2048,512]{0,1:T(8,128)(2,1)}) fusion(f32[2048,1024]{0,1:T(8,128)} %get-tuple-element.16, f32[2048,1024]{0,1:T(8,128)} %get-tuple-element.15), kind=kLoop, calls=%fused_computation.34 | loop fusion | flops 8388608 | bytes 20971520 | tf_op jit(solution)/shard_map/convert.11
  195.8 16.3 %fusion.9 = f32[2048,1024]{0,1:T(8,128)} fusion(bf16[2048,1,1024]{2,0,1:T(8,128)(2,1)} %param.7, s32[2048]{0:T(1024)S(1)} %copy-done.4, s32[2048]{0:T(1024)S(1)} %copy-done.5, bf16[2048,512]{0,1:T(8,128)(2,1)} %get-tuple-element.10, bf16[2048,512]{0,1:T(8,128)(2,1)} %get-tuple-element.9, bf16[512,1024]{1,0:T(8,128)(2,1)S(1)} %get-tuple-element.17, ...), kind=kOutput, calls=%fused_computation.22 | convolution fusion | flops 8621391872 | bytes 18890752 | tf_op jit(solution)/shard_map/dot_general | solution.py:78
  212.1 10.1 %fusion.24 = (bf16[2048,1,512]{0,2,1:T(8,128)(2,1)S(1)}, bf16[2048,1,512]{0,2,1:T(8,128)(2,1)S(1)}, bf16[2048,1,512]{0,2,1:T(8,128)(2,1)S(1)}, bf16[2048,1,512]{0,2,1:T(8,128)(2,1)S(1)}) fusion(f32[2048,1024]{0,1:T(8,128)} %get-tuple-element.16, f32[2048,1024]{0,1:T(8,128)} %fusion.9, f32[2048,1024]{0,1:T(8,128)} %get-tuple-element.15), kind=kLoop, calls=%fused_computation.47 | loop fusion | flops 16777216 | bytes 33554432 | tf_op jit(solution)/shard_map/concatenate | solution.py:82
  222.2 4.1 maximum_maximum_fusion
  226.2 21.4 %copy.24 = bf16[2048,2,1024]{2,1,0:T(2,128)(2,1)} copy(bf16[2048,2,1024]{0,2,1:T(8,128)(2,1)} %maximum_maximum_fusion) | data formatting | bytes 16777216 | tf_op jit(solution)/shard_map/stack | solution.py:88
  247.7 13.3 %reshape.192 = bf16[4096,1024]{1,0:T(8,128)(2,1)} reshape(bf16[2048,2,1024]{2,1,0:T(2,128)(2,1)} %copy.24) | data formatting | bytes 16777216 | tf_op jit(solution)/shard_map/reshape | solution.py:88
  261.0 26.5 %scatter_custom_fusion.1 = bf16[6144,1024]{1,0:T(8,128)(2,1)} fusion(s32[4096]{0:T(1024)S(1)} %bitcast.63, bf16[4096,1024]{1,0:T(8,128)(2,1)} %reshape.192, bf16[]{:T(256)} %constant.18.clone.1), kind=kCustom, calls=%fused_computation.17 | custom fusion | bytes 12583424 | tf_op jit(solution)/shard_map/scatter | solution.py:92
  287.5 5.4 %all-to-all-start.1 = ((bf16[16,384,1024]{2,1,0:T(8,128)(2,1)}), bf16[16,384,1024]{2,1,0:T(8,128)(2,1)}, u32[]{:S(2)}, u32[]{:S(2)}) async-start(bf16[16,384,1024]{2,1,0:T(8,128)(2,1)} %bitcast.54), calls=%async_computation.1 | async-start | bytes 25165824 | tf_op jit(solution)/shard_map/all_to_all | solution.py:94
  294.5 166.6 %all-to-all-done.1 = bf16[16,384,1024]{2,1,0:T(8,128)(2,1)} async-done(((bf16[16,384,1024]{2,1,0:T(8,128)(2,1)}), bf16[16,384,1024]{2,1,0:T(8,128)(2,1)}, u32[]{:S(2)}, u32[]{:S(2)}) %all-to-all-start.1) | async-done | bytes 12582944 | tf_op jit(solution)/shard_map/all_to_all | solution.py:94
  461.1 10.1 %fusion = f32[512,1024]{1,0:T(8,128)S(1)} fusion(bf16[6144,1024]{1,0:T(8,128)(2,1)} %bitcast.17, s32[6144]{0:T(1024)S(1)} %bitcast.60), kind=kOutput, calls=%fused_computation.7 | convolution fusion | flops 6445596672 | bytes 14704640 | tf_op jit(solution)/shard_map/dot_general | solution.py:104
  (37 shorter events, 10.1 us)
Async XLA Ops:
  6.5 8.1 %copy-start.2 = (s32[2048,2]{0,1:T(2,128)S(1)}, s32[2048,2]{0,1:T(2,128)}, u32[]{:S(2)}) copy-start(s32[2048,2]{0,1:T(2,128)} %param.8) | copy-start | bytes 49156
  6.5 9.1 %copy-start.3 = (s32[2048,2]{0,1:T(2,128)S(1)}, s32[2048,2]{0,1:T(2,128)}, u32[]{:S(2)}) copy-start(s32[2048,2]{0,1:T(2,128)} %param.9) | copy-start | bytes 49156
  6.5 117.7 %all-gather.4.cloned.1.call-start = ((), (), s32[]{:S(2)}) async-start(), calls=%async_computation.2 | async-start | bytes 17825792 | tf_op jit(solution)/shard_map/all_gather | solution.py:39
  8.3 33.7 %copy-start = (bf16[512,1,1024]{2,0,1:T(8,128)(2,1)S(1)}, bf16[512,1,1024]{2,0,1:T(8,128)(2,1)}, u32[]{:S(2)}) copy-start(bf16[512,1,1024]{2,0,1:T(8,128)(2,1)} %param.6) | copy-start | bytes 3145732
  33.0 254.6 %all-to-all-start = ((s32[16,1,384]{2,1,0:T(1,128)}), s32[16,1,384]{2,1,0:T(1,128)S(1)}, u32[]{:S(2)}, u32[]{:S(2)}) async-start(s32[16,1,384]{2,1,0:T(1,128)} %bitcast.3), calls=%async_computation | async-start | bytes 49152 | tf_op jit(solution)/shard_map/all_to_all | solution.py:57
  186.7 9.1 %copy-start.4 = (s32[2048]{0:T(1024)S(1)}, s32[2048]{0:T(1024)}, u32[]{:S(2)}) copy-start(s32[2048]{0:T(1024)} %param.11) | copy-start | bytes 24580
  186.7 9.2 %copy-start.5 = (s32[2048]{0:T(1024)S(1)}, s32[2048]{0:T(1024)}, u32[]{:S(2)}) copy-start(s32[2048]{0:T(1024)} %param.10) | copy-start | bytes 24580
  287.5 173.6 %all-to-all-start.1 = ((bf16[16,384,1024]{2,1,0:T(8,128)(2,1)}), bf16[16,384,1024]{2,1,0:T(8,128)(2,1)}, u32[]{:S(2)}, u32[]{:S(2)}) async-start(bf16[16,384,1024]{2,1,0:T(8,128)(2,1)} %bitcast.54), calls=%async_computation.1 | async-start | bytes 25165824 | tf_op jit(solution)/shard_map/all_to_all | solution.py:94
  461.1 10.1 %copy-start.1 = (f32[512,1024]{1,0:T(8,128)S(1)}, f32[512,1024]{1,0:T(8,128)}, u32[]{:S(2)}) copy-start(f32[512,1024]{1,0:T(8,128)} %fusion.35) | copy-start | bytes 6291460
Sparse Core Ops, SparseCore 0:
  9.8 114.4 all-gather.3

commit v2 on v1

--- a/solution.py
+++ b/solution.py
@@ -4,6 +4,8 @@
 import jax.numpy as jnp
 from jax import lax
 from jax.sharding import PartitionSpec as P
+from jax.experimental import pallas as pl
+from jax.experimental.pallas import tpu as pltpu
 
 
 def lag_basis(half_width, lag_count):
@@ -26,6 +28,60 @@
     return jnp.sum(before * onehot, axis=1)
 
 
+def round_bf16(x):
+    return x.astype(jnp.bfloat16).astype(jnp.float32)
+
+
+def pair_kernel(near_ref, far_ref, ns_ref, fs_ref, obs_ref, ws_ref, we_ref, table_ref, out_ref):
+    half = near_ref.shape[1] // 2
+    near = round_bf16(near_ref[...].astype(jnp.float32) * ns_ref[...])
+    far = round_bf16(far_ref[...].astype(jnp.float32) * fs_ref[...])
+    near_re, near_im = near[:, :half], near[:, half:]
+    far_re, far_im = far[:, :half], far[:, half:]
+    cross_re = (near_re * far_re + near_im * far_im).astype(jnp.bfloat16)
+    cross_im = (near_im * far_re - near_re * far_im).astype(jnp.bfloat16)
+    tab_re = table_ref[:half, :]
+    tab_im = table_ref[half:, :]
+    lagged = jnp.dot(cross_re, tab_re, preferred_element_type=jnp.float32) + jnp.dot(
+        cross_im, tab_im, preferred_element_type=jnp.float32
+    )
+    lag = lax.broadcasted_iota(jnp.int32, lagged.shape, 1)
+    inside = (lag >= ws_ref[...]) & (lag < we_ref[...])
+    residual = jnp.where(inside, lagged - obs_ref[...].astype(jnp.float32), 0.0).astype(
+        jnp.bfloat16
+    )
+    dims = (((1,), (1,)), ((), ()))
+    adj_re = lax.dot_general(residual, tab_re, dims, preferred_element_type=jnp.float32)
+    adj_im = lax.dot_general(residual, tab_im, dims, preferred_element_type=jnp.float32)
+    out_ref[0, :, :half] = (adj_re * far_re - adj_im * far_im).astype(jnp.bfloat16)
+    out_ref[0, :, half:] = (adj_re * far_im + adj_im * far_re).astype(jnp.bfloat16)
+    out_ref[1, :, :half] = (adj_re * near_re + adj_im * near_im).astype(jnp.bfloat16)
+    out_ref[1, :, half:] = (adj_re * near_im - adj_im * near_re).astype(jnp.bfloat16)
+
+
+def pair_contributions(near_raw, far_raw, near_scale, far_scale, obs, ws, we, table, block=256):
+    pairs, width = near_raw.shape
+    lags = obs.shape[1]
+    row = lambda i: (i, 0)
+    return pl.pallas_call(
+        pair_kernel,
+        grid=(pairs // block,),
+        in_specs=[
+            pl.BlockSpec((block, width), row),
+            pl.BlockSpec((block, width), row),
+            pl.BlockSpec((block, 1), row),
+            pl.BlockSpec((block, 1), row),
+            pl.BlockSpec((block, lags), row),
+            pl.BlockSpec((block, 1), row),
+            pl.BlockSpec((block, 1), row),
+            pl.BlockSpec((width, lags), lambda i: (0, 0)),
+        ],
+        out_specs=pl.BlockSpec((2, block, width), lambda i: (0, i, 0)),
+        out_shape=jax.ShapeDtypeStruct((2, pairs, width), jnp.bfloat16),
+        compiler_params=pltpu.CompilerParams(vmem_limit_bytes=48 * 1024 * 1024),
+    )(near_raw, far_raw, near_scale, far_scale, obs, ws, we, table)
+
+
 def shards(spectra, observed, pair_owner, pair_slot, win_start, win_end):
     owners = lax.axis_size("pairs")
     station_count = spectra.shape[0]
@@ -42,11 +98,11 @@
     total_power = lax.psum(local_power, "band")
     entries = band_count * lax.axis_size("band") * full_width
     scale = lax.rsqrt(total_power / entries + 1e-05)
-    own_spec = (spectrum * scale[:, None]).astype(jnp.bfloat16).astype(jnp.float32)
+    own_spec = lax.reduce_precision(spectrum * scale[:, None], exponent_bits=8, mantissa_bits=7)
     panel_scale = lax.all_gather(scale, "pairs", axis=0, tiled=True)
 
-    owner_flat = pair_owner.reshape(-1)
-    slot_flat = pair_slot.reshape(-1)
+    owner_flat = jnp.concatenate([pair_owner[:, 0], pair_owner[:, 1]])
+    slot_flat = jnp.concatenate([pair_slot[:, 0], pair_slot[:, 1]])
     position = owner_positions(owner_flat, owners)
     flat_slot = owner_flat * capacity + position
     request = (
@@ -60,36 +116,20 @@
 
     rows0 = pair_owner[:, 0] * station_count + pair_slot[:, 0]
     rows1 = pair_owner[:, 1] * station_count + pair_slot[:, 1]
-    near_end = panel_raw[rows0].astype(jnp.float32) * panel_scale[rows0][:, None]
-    far_end = panel_raw[rows1].astype(jnp.float32) * panel_scale[rows1][:, None]
-    near_end = near_end.astype(jnp.bfloat16).astype(jnp.float32)
-    far_end = far_end.astype(jnp.bfloat16).astype(jnp.float32)
-    near_re, near_im = (near_end[:, :half_width], near_end[:, half_width:])
-    far_re, far_im = (far_end[:, :half_width], far_end[:, half_width:])
-    cross_spec = jnp.concatenate(
-        [near_re * far_re + near_im * far_im, near_im * far_re - near_re * far_im], axis=-1
-    ).astype(jnp.bfloat16)
+    near_raw = panel_raw[rows0]
+    far_raw = panel_raw[rows1]
+    near_scale = panel_scale[rows0][:, None]
+    far_scale = panel_scale[rows1][:, None]
     table = lag_basis(half_width, lag_count)
-    lagged = jnp.dot(cross_spec, table, preferred_element_type=jnp.float32)
-    lag_index = jnp.arange(lag_count, dtype=jnp.int32)
-    window = (lag_index[None, :] >= win_start[:, None]) & (lag_index[None, :] < win_end[:, None])
-    obs = observed.reshape(pair_count, lag_count).astype(jnp.float32)
-    residual = jnp.where(window, lagged - obs, 0.0).astype(jnp.bfloat16)
-    adjoint = lax.dot_general(
-        residual, table, (((1,), (1,)), ((), ())), preferred_element_type=jnp.float32
-    )
-    adj_re, adj_im = (adjoint[:, :half_width], adjoint[:, half_width:])
-    to_first = jnp.concatenate(
-        [adj_re * far_re - adj_im * far_im, adj_re * far_im + adj_im * far_re], axis=-1
-    ).astype(jnp.bfloat16)
-    to_second = jnp.concatenate(
-        [adj_re * near_re + adj_im * near_im, adj_re * near_im - adj_im * near_re], axis=-1
-    ).astype(jnp.bfloat16)
-    stacked = jnp.stack([to_first, to_second], axis=1).reshape(2 * pair_count, full_width)
+    obs = observed.reshape(pair_count, lag_count)
+    contribs = pair_contributions(
+        near_raw, far_raw, near_scale, far_scale, obs,
+        win_start[:, None], win_end[:, None], table,
+    ).reshape(2 * pair_count, full_width)
     outgoing = (
         jnp.zeros((owners * capacity, full_width), jnp.bfloat16)
         .at[flat_slot]
-        .set(stacked, unique_indices=True)
+        .set(contribs, unique_indices=True)
     )
     incoming = lax.all_to_all(
         outgoing.reshape(owners, capacity, full_width),

time: 487 us -> 402 us (0.83)
  local copies, waits for them, and re-layouts: 158 us -> 110 us
  other arithmetic: 51.1 us -> 17.2 us
  Pallas kernels: 0 us -> 17.9 us
  matrix products: 26.4 us -> 9.99 us
    another operation x1 -> x0, local copies, waits for them, and re-layouts: 21.4 us -> none  [shards(): jnp.stack([to_first, to_second], axis=1).reshape(2 * pair_count, full_width)]
    pallas_call x0 -> x1, Pallas kernels: none -> 17.9 us  [pair_contributions(): pl.pallas_call(pair_kernel, grid=(pairs // block,), in_specs=[pl.BlockSpe...]
    dot_general x1 -> x0, matrix products: 16.3 us -> none  [shards(): lax.dot_general(residual, table, (((1,), (1,)), ((), ())), preferred_elem...]
    reshape x2 -> x0, local copies, waits for them, and re-layouts: 13.8 us -> none  [the longest x1 13.3 us: shards(): jnp.stack([to_first, to_second], axis=1).reshape(2 * pair_count, full_width)]
    convert_element_type x2 -> x0, other arithmetic: 13.2 us -> none  [the longest x1 11.6 us: shards(): near_end = near_end.astype(jnp.bfloat16).astype(jnp.float32)]
    another operation x6 -> x4, other arithmetic: 26.7 us -> 13.5 us
    gather x6 -> x4, local copies, waits for them, and re-layouts: 74.4 us -> 61.4 us  [the longest x1 18.9 us: shards(): far_raw = panel_raw[rows1]]
    concatenate x1 -> x4, other arithmetic: 10.1 us -> 1.54 us  [the longest x1 1.53 us: lag_basis(): jnp.concatenate([jnp.cos(phases) * factor, -jnp.sin(phases) * factor], ax...]
  transfers between devices with their start and end apart: 3 -> 3, of which waited for: 2 -> 2; matrix products, arithmetic and copies ran while one was open for 46% -> 31% of each run, Pallas kernels for 0% -> 4%
where the time goes in v2:
time: 402 us; the launch traced here: 401 us
  waiting for transfers between devices  172 us (43%)
  local copies, waits for them, and re-layouts  110 us (27%)
  blocking collectives  45.2 us (11%)
  Pallas kernels  17.9 us (4%)
  other arithmetic  17.2 us (4%)
  starting transfers between devices  14.2 us (4%)
  between operations  13.5 us (3%)
  matrix products  9.99 us (2%)
    all_to_all x1, waiting for transfers between devices, shards(): lax.all_to_all(outgoing.reshape(owners, capacity, full_width), 'pairs', s...  168 us
    all_gather x1, blocking collectives, shards(): panel_scale = lax.all_gather(scale, 'pairs', axis=0, tiled=True)  29.2 us
    scatter x1, local copies, waits for them, and re-layouts, shards(): outgoing = jnp.zeros((owners * capacity, full_width), jnp.bfloat16).at[fl...  26.7 us
    gather x1, local copies, waits for them, and re-layouts, shards(): far_raw = panel_raw[rows1]  18.9 us
    gather x1, local copies, waits for them, and re-layouts, shards(): near_raw = panel_raw[rows0]  18.9 us
    pallas_call x1, Pallas kernels, pair_contributions(): pl.pallas_call(pair_kernel, grid=(pairs // block,), in_specs=[pl.BlockSpe...  17.9 us
    scatter x1, local copies, waits for them, and re-layouts, shards(): request = jnp.full((owners * capacity,), station_count, jnp.int32).at[fla...  16.1 us
    psum x1, blocking collectives, shards(): total_power = lax.psum(local_power, 'band')  16 us
  transfers between devices with their start and end apart: 3, of which 2 were waited for; matrix products, arithmetic and copies ran while one was open for 31% of the time, Pallas kernels for 4%

profile of v2, /device:TPU:1, one launch (start us, length us, event | category | flops | bytes accessed | tf_op | source)
XLA Modules:
  0.0 400.7 jit_solution(7385537239429514020)
XLA Ops:
  6.5 0.7 all-gather.4.cloned.1.call-update
  7.3 0.8 compare_select_fusion.1
  8.1 4.6 %reduce-window.6 = s32[16,32,128]{2,1,0:T(8,128)S(1)} reduce-window(s32[16,32,128]{2,1,0:T(8,128)S(1)} %fusion.18, s32[]{:T(128)} %constant.16.clone.1), window={size=1x1x128 pad=0_0x0_0x127_0}, to_apply=%region_0.0 | reduce-window | flops 8323072 | bytes 524292 | tf_op jit(solution)/shard_map/reduce-window
  12.8 0.5 slice_reduce_fusion
  13.8 16.1 %scatter_custom_fusion = s32[6144]{0:T(1024)} fusion(s32[4096]{0:T(1024)S(1)} %bitcast.70, s32[4096]{0:T(1024)S(1)} %pad_add_fusion.2, s32[]{:T(128)} %constant.14.clone.1), kind=kCustom, calls=%fused_computation.49 | custom fusion | bytes 24580 | tf_op jit(solution)/shard_map/scatter | solution.py:111
  29.9 9.1 %all-to-all-start = ((s32[16,1,384]{2,1,0:T(1,128)}), s32[16,1,384]{2,1,0:T(1,128)S(1)}, u32[]{:S(2)}, u32[]{:S(2)}) async-start(s32[16,1,384]{2,1,0:T(1,128)} %bitcast.9), calls=%async_computation | async-start | bytes 49152 | tf_op jit(solution)/shard_map/all_to_all | solution.py:113
  39.3 16.0 %psum.7 = f32[512]{0:T(512)S(1)} all-reduce(f32[512]{0:T(512)S(1)} %fusion.4), channel_id=1, replica_groups=mesh['pairs'=16,'band'=8] {'band'}, use_global_device_ids=true, to_apply=%region_5.6 | all-reduce | flops 512 | bytes 4096 | tf_op jit(solution)/shard_map/psum | solution.py:98
  55.3 8.6 %multiply_convert_fusion = (bf16[512,1024]{1,0:T(8,128)(2,1)S(1)}, bf16[512,1024]{1,0:T(8,128)(2,1)S(1)}) fusion(), kind=kLoop, calls=%fused_computation.22 | loop fusion | flops 9961472 | bytes 2097152 | tf_op jit(solution)/shard_map/convert.1
  63.9 1.5 pad_maximum_fusion.table_ref
  65.4 29.2 %all-gather.1 = f32[16,1,512]{2,1,0:T(1,128)S(1)} all-gather(f32[1,1,512]{2,1,0:T(1,128)S(1)} %bitcast.69), channel_id=1, replica_groups=mesh['pairs'=16,'band'=8] {'pairs'}, dimensions={0}, use_global_device_ids=true | all-gather | bytes 34816 | tf_op jit(solution)/shard_map/all_gather | solution.py:102
  94.6 11.8 %gather_fusion.2 = f32[2048]{0:T(1024)S(1)} fusion(f32[8192]{0:T(1024)S(1)} %bitcast.48, s32[2048]{0:T(1024)S(1)} %broadcast_clamp_fusion.1), kind=kCustom, calls=%fused_computation.2 | custom fusion | bytes 24576 | tf_op jit(solution)/shard_map/gather | solution.py:121
  106.8 11.8 %gather_fusion.3 = f32[2048]{0:T(1024)S(1)} fusion(f32[8192]{0:T(1024)S(1)} %bitcast.49, s32[2048]{0:T(1024)S(1)} %broadcast_clamp_fusion), kind=kCustom, calls=%fused_computation.3 | custom fusion | bytes 24576 | tf_op jit(solution)/shard_map/gather | solution.py:122
  119.3 1.3 copy.16.we_ref
  120.7 3.5 all-gather.4.cloned.1.call-done
  124.2 18.9 %gather_fusion = bf16[2048,1024]{1,0:T(8,128)(2,1)} fusion(bf16[8192,1024]{1,0:T(8,128)(2,1)} %bitcast.50, s32[2048]{0:T(1024)S(1)} %broadcast_clamp_fusion.1), kind=kCustom, calls=%fused_computation | custom fusion | bytes 8396800 | tf_op jit(solution)/shard_map/gather | solution.py:119
  143.1 18.9 %gather_fusion.1 = bf16[2048,1024]{1,0:T(8,128)(2,1)} fusion(bf16[8192,1024]{1,0:T(8,128)(2,1)} %bitcast.51, s32[2048]{0:T(1024)S(1)} %broadcast_clamp_fusion), kind=kCustom, calls=%fused_computation.1 | custom fusion | bytes 8396800 | tf_op jit(solution)/shard_map/gather | solution.py:120
  162.0 1.2 copy-done
  163.2 17.9 %shard_map.64 = bf16[2,2048,1024]{2,1,0:T(8,128)(2,1)} custom-call(bf16[2048,1024]{1,0:T(8,128)(2,1)} %gather_fusion, bf16[2048,1024]{1,0:T(8,128)(2,1)} %gather_fusion.1, f32[2048,1]{1,0:T(8,128)S(1)} %copy.13.ns_ref, f32[2048,1]{1,0:T(8,128)S(1)} %copy.14.fs_ref, bf16[2048,1024]{1,0:T(8,128)(2,1)} %bitcast.54, s32[2048,1]{1,0:T(8,128)S(1)} %copy.15.ws_ref, ...), custom_call_target="tpu_custom_call" | custom-call | tf_op jit(solution)/shard_map/pallas_call | solution.py:66
  181.1 26.7 %scatter_custom_fusion.1 = bf16[6144,1024]{1,0:T(8,128)(2,1)} fusion(s32[4096]{0:T(1024)S(1)} %bitcast.71, bf16[4096,1024]{1,0:T(8,128)(2,1)} %bitcast.53, bf16[]{:T(256)} %constant.18.clone.1), kind=kCustom, calls=%fused_computation.8 | custom fusion | bytes 12583424 | tf_op jit(solution)/shard_map/scatter | solution.py:132
  207.8 5.1 %all-to-all-start.1 = ((bf16[16,384,1024]{2,1,0:T(8,128)(2,1)}), bf16[16,384,1024]{2,1,0:T(8,128)(2,1)}, u32[]{:S(2)}, u32[]{:S(2)}) async-start(bf16[16,384,1024]{2,1,0:T(8,128)(2,1)} %bitcast.52), calls=%async_computation.1 | async-start | bytes 25165824 | tf_op jit(solution)/shard_map/all_to_all | solution.py:134
  213.2 168.1 %all-to-all-done.1 = bf16[16,384,1024]{2,1,0:T(8,128)(2,1)} async-done(((bf16[16,384,1024]{2,1,0:T(8,128)(2,1)}), bf16[16,384,1024]{2,1,0:T(8,128)(2,1)}, u32[]{:S(2)}, u32[]{:S(2)}) %all-to-all-start.1) | async-done | bytes 12582944 | tf_op jit(solution)/shard_map/all_to_all | solution.py:134
  381.3 10.0 %fusion = f32[512,1024]{1,0:T(8,128)S(1)} fusion(bf16[6144,1024]{1,0:T(8,128)(2,1)} %bitcast.24, s32[6144]{0:T(1024)S(1)} %bitcast.68), kind=kOutput, calls=%fused_computation.7 | convolution fusion | flops 6445596672 | bytes 14704640 | tf_op jit(solution)/shard_map/dot_general | solution.py:144
  391.3 0.5 fusion.14
  391.8 2.0 copy.17
  (27 shorter events, 2.3 us)
Async XLA Ops:
  6.5 32.5 %copy-start.1 = (bf16[512,1,1024]{2,0,1:T(8,128)(2,1)S(1)}, bf16[512,1,1024]{2,0,1:T(8,128)(2,1)}, u32[]{:S(2)}) copy-start(bf16[512,1,1024]{2,0,1:T(8,128)(2,1)} %param.6) | copy-start | bytes 3145732
  6.5 117.6 %all-gather.4.cloned.1.call-start = ((), (), s32[]{:S(2)}) async-start(), calls=%async_computation.2 | async-start | bytes 17825792 | tf_op jit(solution)/shard_map/all_gather | solution.py:95
  29.9 177.9 %all-to-all-start = ((s32[16,1,384]{2,1,0:T(1,128)}), s32[16,1,384]{2,1,0:T(1,128)S(1)}, u32[]{:S(2)}, u32[]{:S(2)}) async-start(s32[16,1,384]{2,1,0:T(1,128)} %bitcast.9), calls=%async_computation | async-start | bytes 49152 | tf_op jit(solution)/shard_map/all_to_all | solution.py:113
  106.7 12.2 %copy-start.3 = (s32[2048]{0:T(1024)S(1)}, s32[2048]{0:T(1024)}, u32[]{:S(2)}) copy-start(s32[2048]{0:T(1024)} %param.10) | copy-start | bytes 24580
  118.5 0.8 copy-start.4
  162.0 1.2 copy-start
  207.8 5.1 %copy-start.2 = (bf16[512,1,1024]{2,0,1:T(8,128)(2,1)S(1)}, bf16[512,1,1024]{2,0,1:T(8,128)(2,1)}, u32[]{:S(2)}) copy-start(bf16[512,1,1024]{2,0,1:T(8,128)(2,1)} %param.6) | copy-start | bytes 3145732
  207.8 173.5 %all-to-all-start.1 = ((bf16[16,384,1024]{2,1,0:T(8,128)(2,1)}), bf16[16,384,1024]{2,1,0:T(8,128)(2,1)}, u32[]{:S(2)}, u32[]{:S(2)}) async-start(bf16[16,384,1024]{2,1,0:T(8,128)(2,1)} %bitcast.52), calls=%async_computation.1 | async-start | bytes 25165824 | tf_op jit(solution)/shard_map/all_to_all | solution.py:134
Sparse Core Ops, SparseCore 0:
  9.8 114.3 all-gather.3

commit v3 on v2

--- a/solution.py
+++ b/solution.py
@@ -32,12 +32,15 @@
     return x.astype(jnp.bfloat16).astype(jnp.float32)
 
 
-def pair_kernel(near_ref, far_ref, ns_ref, fs_ref, obs_ref, ws_ref, we_ref, table_ref, out_ref):
-    half = near_ref.shape[1] // 2
-    near = round_bf16(near_ref[...].astype(jnp.float32) * ns_ref[...])
-    far = round_bf16(far_ref[...].astype(jnp.float32) * fs_ref[...])
-    near_re, near_im = near[:, :half], near[:, half:]
-    far_re, far_im = far[:, :half], far[:, half:]
+def pair_kernel(
+    nr_ref, ni_ref, fr_ref, fi_ref, ns_ref, fs_ref, obs_ref, ws_ref, we_ref, table_ref,
+    re_ref, im_ref,
+):
+    half = nr_ref.shape[1]
+    near_re = round_bf16(nr_ref[...].astype(jnp.float32) * ns_ref[...])
+    near_im = round_bf16(ni_ref[...].astype(jnp.float32) * ns_ref[...])
+    far_re = round_bf16(fr_ref[...].astype(jnp.float32) * fs_ref[...])
+    far_im = round_bf16(fi_ref[...].astype(jnp.float32) * fs_ref[...])
     cross_re = (near_re * far_re + near_im * far_im).astype(jnp.bfloat16)
     cross_im = (near_im * far_re - near_re * far_im).astype(jnp.bfloat16)
     tab_re = table_ref[:half, :]
@@ -53,33 +56,30 @@
     dims = (((1,), (1,)), ((), ()))
     adj_re = lax.dot_general(residual, tab_re, dims, preferred_element_type=jnp.float32)
     adj_im = lax.dot_general(residual, tab_im, dims, preferred_element_type=jnp.float32)
-    out_ref[0, :, :half] = (adj_re * far_re - adj_im * far_im).astype(jnp.bfloat16)
-    out_ref[0, :, half:] = (adj_re * far_im + adj_im * far_re).astype(jnp.bfloat16)
-    out_ref[1, :, :half] = (adj_re * near_re + adj_im * near_im).astype(jnp.bfloat16)
-    out_ref[1, :, half:] = (adj_re * near_im - adj_im * near_re).astype(jnp.bfloat16)
+    re_ref[0] = (adj_re * far_re - adj_im * far_im).astype(jnp.bfloat16)
+    im_ref[0] = (adj_re * far_im + adj_im * far_re).astype(jnp.bfloat16)
+    re_ref[1] = (adj_re * near_re + adj_im * near_im).astype(jnp.bfloat16)
+    im_ref[1] = (adj_re * near_im - adj_im * near_re).astype(jnp.bfloat16)
 
 
-def pair_contributions(near_raw, far_raw, near_scale, far_scale, obs, ws, we, table, block=256):
-    pairs, width = near_raw.shape
+def pair_contributions(rows, near_scale, far_scale, obs, ws, we, table, block=256):
+    pairs, half = rows[0].shape
     lags = obs.shape[1]
     row = lambda i: (i, 0)
+    half_spec = pl.BlockSpec((block, half), row)
+    col_spec = pl.BlockSpec((block, 1), row)
+    out_spec = pl.BlockSpec((2, block, half), lambda i: (0, i, 0))
+    out_shape = jax.ShapeDtypeStruct((2, pairs, half), jnp.bfloat16)
     return pl.pallas_call(
         pair_kernel,
         grid=(pairs // block,),
-        in_specs=[
-            pl.BlockSpec((block, width), row),
-            pl.BlockSpec((block, width), row),
-            pl.BlockSpec((block, 1), row),
-            pl.BlockSpec((block, 1), row),
-            pl.BlockSpec((block, lags), row),
-            pl.BlockSpec((block, 1), row),
-            pl.BlockSpec((block, 1), row),
-            pl.BlockSpec((width, lags), lambda i: (0, 0)),
-        ],
-        out_specs=pl.BlockSpec((2, block, width), lambda i: (0, i, 0)),
-        out_shape=jax.ShapeDtypeStruct((2, pairs, width), jnp.bfloat16),
+        in_specs=[half_spec] * 4
+        + [col_spec, col_spec, pl.BlockSpec((block, lags), row), col_spec, col_spec]
+        + [pl.BlockSpec((2 * half, lags), lambda i: (0, 0))],
+        out_specs=[out_spec, out_spec],
+        out_shape=[out_shape, out_shape],
         compiler_params=pltpu.CompilerParams(vmem_limit_bytes=48 * 1024 * 1024),
-    )(near_raw, far_raw, near_scale, far_scale, obs, ws, we, table)
+    )(*rows, near_scale, far_scale, obs, ws, we, table)
 
 
 def shards(spectra, observed, pair_owner, pair_slot, win_start, win_end):
@@ -92,7 +92,8 @@
     lag_count = observed.shape[2]
     capacity = 3 * pair_count // owners
     raw = spectra.reshape(station_count, full_width)
-    panel_raw = lax.all_gather(raw, "pairs", axis=0, tiled=True)
+    panel_re = lax.all_gather(raw[:, :half_width], "pairs", axis=0, tiled=True)
+    panel_im = lax.all_gather(raw[:, half_width:], "pairs", axis=0, tiled=True)
     spectrum = raw.astype(jnp.float32)
     local_power = jnp.sum(spectrum * spectrum, axis=1)
     total_power = lax.psum(local_power, "band")
@@ -116,35 +117,38 @@
 
     rows0 = pair_owner[:, 0] * station_count + pair_slot[:, 0]
     rows1 = pair_owner[:, 1] * station_count + pair_slot[:, 1]
-    near_raw = panel_raw[rows0]
-    far_raw = panel_raw[rows1]
+    rows = (panel_re[rows0], panel_im[rows0], panel_re[rows1], panel_im[rows1])
     near_scale = panel_scale[rows0][:, None]
     far_scale = panel_scale[rows1][:, None]
     table = lag_basis(half_width, lag_count)
     obs = observed.reshape(pair_count, lag_count)
-    contribs = pair_contributions(
-        near_raw, far_raw, near_scale, far_scale, obs,
-        win_start[:, None], win_end[:, None], table,
-    ).reshape(2 * pair_count, full_width)
-    outgoing = (
-        jnp.zeros((owners * capacity, full_width), jnp.bfloat16)
-        .at[flat_slot]
-        .set(contribs, unique_indices=True)
+    contrib_re, contrib_im = pair_contributions(
+        rows, near_scale, far_scale, obs, win_start[:, None], win_end[:, None], table
     )
-    incoming = lax.all_to_all(
-        outgoing.reshape(owners, capacity, full_width),
-        "pairs",
-        split_axis=0,
-        concat_axis=0,
-        tiled=True,
-    ).reshape(owners * capacity, full_width)
+
+    def send(contrib):
+        outgoing = (
+            jnp.zeros((owners * capacity, half_width), jnp.bfloat16)
+            .at[flat_slot]
+            .set(contrib.reshape(2 * pair_count, half_width), unique_indices=True)
+        )
+        return lax.all_to_all(
+            outgoing.reshape(owners, capacity, half_width),
+            "pairs",
+            split_axis=0,
+            concat_axis=0,
+            tiled=True,
+        ).reshape(owners * capacity, half_width)
+
+    incoming_re = send(contrib_re)
+    incoming_im = send(contrib_im)
     onehot = (
         wanted[None, :] == jnp.arange(station_count, dtype=jnp.int32)[:, None]
     ).astype(jnp.bfloat16)
-    summed = jnp.dot(onehot, incoming, preferred_element_type=jnp.float32)
+    summed_re = jnp.dot(onehot, incoming_re, preferred_element_type=jnp.float32)
+    summed_im = jnp.dot(onehot, incoming_im, preferred_element_type=jnp.float32)
     result = 0.25 * (
-        summed[:, :half_width] * own_spec[:, :half_width]
-        + summed[:, half_width:] * own_spec[:, half_width:]
+        summed_re * own_spec[:, :half_width] + summed_im * own_spec[:, half_width:]
     )
     return result.reshape(station_count, band_count, half_width)
 

time: 402 us -> 425 us (1.057)
  local copies, waits for them, and re-layouts: 110 us -> 148 us
  waiting for transfers between devices: 172 us -> 151 us
  starting transfers between devices: 14.2 us -> 20.7 us
    all_to_all x1 -> x2, waiting for transfers between devices: 168 us -> 140 us  [send(): lax.all_to_all(outgoing.reshape(owners, capacity, half_width), 'pairs', s...]
    scatter x1 -> x2, local copies, waits for them, and re-layouts: 26.7 us -> 45 us  [send(): outgoing = jnp.zeros((owners * capacity, half_width), jnp.bfloat16).at[fl...]
    gather x2 -> x4, local copies, waits for them, and re-layouts: 37.8 us -> 54.8 us  [shards(): rows = (panel_re[rows0], panel_im[rows0], panel_re[rows1], panel_im[rows1])]
    all_gather x1 -> x2, waiting for transfers between devices: 3.5 us -> 10.3 us  [the longest x1 10.3 us: shards(): panel_im = lax.all_gather(raw[:, half_width:], 'pairs', axis=0, tiled=True)]
    all_to_all x1 -> x2, starting transfers between devices: 5.09 us -> 11.5 us  [send(): lax.all_to_all(outgoing.reshape(owners, capacity, half_width), 'pairs', s...]
    dot_general x1 -> x2, matrix products: 9.99 us -> 12.1 us  [the longest x1 6.06 us: shards(): summed_im = jnp.dot(onehot, incoming_im, preferred_element_type=jnp.float32)]
  transfers between devices with their start and end apart: 3 -> 5, of which waited for: 2 -> 3; matrix products, arithmetic and copies ran while one was open for 31% -> 39% of each run, Pallas kernels for 4% -> 4%
where the time goes in v3:
time: 425 us; the launch traced here: 424 us
  waiting for transfers between devices  151 us (36%)
  local copies, waits for them, and re-layouts  148 us (35%)
  blocking collectives  44.9 us (11%)
  starting transfers between devices  20.7 us (5%)
  Pallas kernels  17.9 us (4%)
  other arithmetic  15.9 us (4%)
  between operations  13.6 us (3%)
  matrix products  12.1 us (3%)
    all_to_all x2, waiting for transfers between devices, send(): lax.all_to_all(outgoing.reshape(owners, capacity, half_width), 'pairs', s...  140 us
    gather x4, local copies, waits for them, and re-layouts, shards(): rows = (panel_re[rows0], panel_im[rows0], panel_re[rows1], panel_im[rows1])  54.8 us
    scatter x2, local copies, waits for them, and re-layouts, send(): outgoing = jnp.zeros((owners * capacity, half_width), jnp.bfloat16).at[fl...  45 us
    all_gather x1, blocking collectives, shards(): panel_scale = lax.all_gather(scale, 'pairs', axis=0, tiled=True)  28.3 us
    pallas_call x1, Pallas kernels, pair_contributions(): pl.pallas_call(pair_kernel, grid=(pairs // block,), in_specs=[half_spec]...  17.9 us
    psum x1, blocking collectives, shards(): total_power = lax.psum(local_power, 'band')  16.5 us
    scatter x1, local copies, waits for them, and re-layouts, shards(): request = jnp.full((owners * capacity,), station_count, jnp.int32).at[fla...  16.1 us
    another operation x4, other arithmetic  13.5 us
  transfers between devices with their start and end apart: 5, of which 3 were waited for; matrix products, arithmetic and copies ran while one was open for 39% of the time, Pallas kernels for 4%

profile of v3, /device:TPU:1, one launch (start us, length us, event | category | flops | bytes accessed | tf_op | source)
XLA Modules:
  0.0 423.9 jit_solution(6274405821246720474)
XLA Ops:
  6.5 2.3 fusion.28
  9.7 4.6 %reduce-window.6 = s32[16,32,128]{2,1,0:T(8,128)S(1)} reduce-window(s32[16,32,128]{2,1,0:T(8,128)S(1)} %fusion.24, s32[]{:T(128)} %constant.16.clone.1), window={size=1x1x128 pad=0_0x0_0x127_0}, to_apply=%region_0.0 | reduce-window | flops 8323072 | bytes 524292 | tf_op jit(solution)/shard_map/reduce-window
  15.4 16.1 %scatter_custom_fusion = s32[6144]{0:T(1024)} fusion(s32[4096]{0:T(1024)S(1)} %bitcast.72, s32[4096]{0:T(1024)S(1)} %pad_add_fusion.2, s32[]{:T(128)} %constant.14.clone.1), kind=kCustom, calls=%fused_computation.56 | custom fusion | bytes 24580 | tf_op jit(solution)/shard_map/scatter | solution.py:112
  31.5 9.1 %all-to-all-start = ((s32[16,1,384]{2,1,0:T(1,128)}), s32[16,1,384]{2,1,0:T(1,128)S(1)}, u32[]{:S(2)}, u32[]{:S(2)}) async-start(s32[16,1,384]{2,1,0:T(1,128)} %bitcast.9), calls=%async_computation | async-start | bytes 49152 | tf_op jit(solution)/shard_map/all_to_all | solution.py:114
  40.9 16.5 %psum.7 = f32[512]{0:T(512)S(1)} all-reduce(f32[512]{0:T(512)S(1)} %fusion.8), channel_id=1, replica_groups=mesh['pairs'=16,'band'=8] {'band'}, use_global_device_ids=true, to_apply=%region_5.6 | all-reduce | flops 512 | bytes 4096 | tf_op jit(solution)/shard_map/psum | solution.py:99
  57.4 8.6 %multiply_convert_fusion = (bf16[512,1024]{1,0:T(8,128)(2,1)S(1)}, bf16[512,1024]{1,0:T(8,128)(2,1)S(1)}) fusion(), kind=kLoop, calls=%fused_computation.29 | loop fusion | flops 9961472 | bytes 2097152 | tf_op jit(solution)/shard_map/convert.1
  67.5 28.3 %all-gather = f32[16,1,512]{2,1,0:T(1,128)S(1)} all-gather(f32[1,1,512]{2,1,0:T(1,128)S(1)} %bitcast.71), channel_id=1, replica_groups=mesh['pairs'=16,'band'=8] {'pairs'}, dimensions={0}, use_global_device_ids=true | all-gather | bytes 34816 | tf_op jit(solution)/shard_map/all_gather | solution.py:103
  95.9 11.8 %gather_fusion.4 = f32[2048]{0:T(1024)S(1)} fusion(f32[8192]{0:T(1024)S(1)} %bitcast.50, s32[2048]{0:T(1024)S(1)} %broadcast_clamp_fusion.1), kind=kCustom, calls=%fused_computation.4 | custom fusion | bytes 24576 | tf_op jit(solution)/shard_map/gather | solution.py:121
  108.0 11.8 %gather_fusion.5 = f32[2048]{0:T(1024)S(1)} fusion(f32[8192]{0:T(1024)S(1)} %bitcast.51, s32[2048]{0:T(1024)S(1)} %broadcast_clamp_fusion), kind=kCustom, calls=%fused_computation.5 | custom fusion | bytes 24576 | tf_op jit(solution)/shard_map/gather | solution.py:122
  121.9 13.7 %gather_fusion = bf16[2048,512]{1,0:T(8,128)(2,1)} fusion(bf16[8192,512]{1,0:T(8,128)(2,1)} %all-gather.4.cloned.1.call-done, s32[2048]{0:T(1024)S(1)} %broadcast_clamp_fusion.1), kind=kCustom, calls=%fused_computation | custom fusion | bytes 4202496 | tf_op jit(solution)/shard_map/gather | solution.py:120
  135.6 13.8 %gather_fusion.2 = bf16[2048,512]{1,0:T(8,128)(2,1)} fusion(bf16[8192,512]{1,0:T(8,128)(2,1)} %all-gather.4.cloned.1.call-done, s32[2048]{0:T(1024)S(1)} %broadcast_clamp_fusion), kind=kCustom, calls=%fused_computation.2 | custom fusion | bytes 4202496 | tf_op jit(solution)/shard_map/gather | solution.py:120
  149.4 10.3 %all-gather.6.cloned.1.call-done = bf16[8192,512]{1,0:T(8,128)(2,1)} async-done(((bf16[512,512]{1,0:T(8,128)(2,1)}), bf16[8192,512]{1,0:T(8,128)(2,1)}) %all-gather.6.cloned.1.call-update) | async-done | bytes 8388624 | tf_op jit(solution)/shard_map/all_gather | solution.py:96
  159.6 13.7 %gather_fusion.1 = bf16[2048,512]{1,0:T(8,128)(2,1)} fusion(bf16[8192,512]{1,0:T(8,128)(2,1)} %all-gather.6.cloned.1.call-done, s32[2048]{0:T(1024)S(1)} %broadcast_clamp_fusion.1), kind=kCustom, calls=%fused_computation.1 | custom fusion | bytes 4202496 | tf_op jit(solution)/shard_map/gather | solution.py:120
  173.3 13.7 %gather_fusion.3 = bf16[2048,512]{1,0:T(8,128)(2,1)} fusion(bf16[8192,512]{1,0:T(8,128)(2,1)} %all-gather.6.cloned.1.call-done, s32[2048]{0:T(1024)S(1)} %broadcast_clamp_fusion), kind=kCustom, calls=%fused_computation.3 | custom fusion | bytes 4202496 | tf_op jit(solution)/shard_map/gather | solution.py:120
  188.3 17.9 %shard_map.64 = (bf16[2,2048,512]{2,1,0:T(8,128)(2,1)}, bf16[2,2048,512]{2,1,0:T(8,128)(2,1)}) custom-call(bf16[2048,512]{1,0:T(8,128)(2,1)} %gather_fusion, bf16[2048,512]{1,0:T(8,128)(2,1)} %gather_fusion.1, bf16[2048,512]{1,0:T(8,128)(2,1)} %gather_fusion.2, bf16[2048,512]{1,0:T(8,128)(2,1)} %gather_fusion.3, f32[2048,1]{1,0:T(8,128)S(1)} %copy.13.ns_ref, ...), custom_call_target="tpu_custom_call" | custom-call | tf_op jit(solution)/shard_map/pallas_call | solution.py:73
  206.1 22.6 %scatter_custom_fusion.1 = bf16[6144,512]{1,0:T(8,128)(2,1)} fusion(s32[4096]{0:T(1024)S(1)} %bitcast.73, bf16[4096,512]{1,0:T(8,128)(2,1)} %bitcast.78, bf16[]{:T(256)} %constant.18.clone.1), kind=kCustom, calls=%fused_computation.19 | custom fusion | bytes 6291968 | tf_op jit(solution)/shard_map/scatter | solution.py:133
  228.8 4.7 %all-to-all-start.1 = ((bf16[16,384,512]{2,1,0:T(8,128)(2,1)}), bf16[16,384,512]{2,1,0:T(8,128)(2,1)}, u32[]{:S(2)}, u32[]{:S(2)}) async-start(bf16[16,384,512]{2,1,0:T(8,128)(2,1)} %bitcast.53), calls=%async_computation.1 | async-start | bytes 12582912 | tf_op jit(solution)/shard_map/all_to_all | solution.py:135
  233.4 22.4 %scatter_custom_fusion.2 = bf16[6144,512]{1,0:T(8,128)(2,1)} fusion(s32[4096]{0:T(1024)S(1)} %bitcast.74, bf16[4096,512]{1,0:T(8,128)(2,1)} %bitcast.77, bf16[]{:T(256)} %constant.18.clone.1), kind=kCustom, calls=%fused_computation.17 | custom fusion | bytes 6291968 | tf_op jit(solution)/shard_map/scatter | solution.py:133
  255.8 61.9 %all-to-all-done.1 = bf16[16,384,512]{2,1,0:T(8,128)(2,1)} async-done(((bf16[16,384,512]{2,1,0:T(8,128)(2,1)}), bf16[16,384,512]{2,1,0:T(8,128)(2,1)}, u32[]{:S(2)}, u32[]{:S(2)}) %all-to-all-start.1) | async-done | bytes 6291488 | tf_op jit(solution)/shard_map/all_to_all | solution.py:135
  317.7 6.9 %all-to-all-start.2 = ((bf16[16,384,512]{2,1,0:T(8,128)(2,1)}), bf16[16,384,512]{2,1,0:T(8,128)(2,1)}, u32[]{:S(2)}, u32[]{:S(2)}) async-start(bf16[16,384,512]{2,1,0:T(8,128)(2,1)} %bitcast.52), calls=%async_computation.2 | async-start | bytes 12582912 | tf_op jit(solution)/shard_map/all_to_all | solution.py:135
  324.8 6.0 %fusion.16 = f32[512,512]{1,0:T(8,128)S(1)} fusion(bf16[6144,512]{1,0:T(8,128)(2,1)} %bitcast.23, s32[6144]{0:T(1024)S(1)} %bitcast.69, f32[512,1024]{1,0:T(8,128)S(1)} %fusion.9), kind=kOutput, calls=%fused_computation.34 | convolution fusion | flops 3224633344 | bytes 8413184 | tf_op jit(solution)/shard_map/dot_general | solution.py:148
  330.8 78.1 %all-to-all-done.2 = bf16[16,384,512]{2,1,0:T(8,128)(2,1)} async-done(((bf16[16,384,512]{2,1,0:T(8,128)(2,1)}), bf16[16,384,512]{2,1,0:T(8,128)(2,1)}, u32[]{:S(2)}, u32[]{:S(2)}) %all-to-all-start.2) | async-done | bytes 6291488 | tf_op jit(solution)/shard_map/all_to_all | solution.py:135
  408.9 6.1 %fusion.20 = f32[512,1,512]{2,0,1:T(8,128)S(1)} fusion(f32[512,512]{1,0:T(8,128)S(1)} %fusion.16, bf16[6144,512]{1,0:T(8,128)(2,1)} %bitcast.26, s32[6144]{0:T(1024)S(1)} %bitcast.70, f32[512,1024]{1,0:T(8,128)S(1)} %fusion.9), kind=kOutput, calls=%fused_computation.38 | convolution fusion | flops 3225157632 | bytes 9461760 | tf_op jit(solution)/shard_map/dot_general | solution.py:149
  415.0 2.0 copy.17
  (40 shorter events, 7.6 us)
Async XLA Ops:
  6.5 3.1 copy-start.4
  6.5 3.1 copy-start.3
  6.5 115.4 %all-gather.4.cloned.1.call-start = ((), (), s32[]{:S(2)}) async-start(), calls=%async_computation.3 | async-start | bytes 8912896 | tf_op jit(solution)/shard_map/all_gather | solution.py:95
  8.8 31.8 %copy-start.1 = (bf16[512,1,1024]{2,0,1:T(8,128)(2,1)S(1)}, bf16[512,1,1024]{2,0,1:T(8,128)(2,1)}, u32[]{:S(2)}) copy-start(bf16[512,1,1024]{2,0,1:T(8,128)(2,1)} %param.6) | copy-start | bytes 3145732
  8.8 150.8 %all-gather.6.cloned.1.call-start = ((), (), s32[]{:S(2)}) async-start(), calls=%async_computation.4 | async-start | bytes 8912896 | tf_op jit(solution)/shard_map/all_gather | solution.py:96
  31.5 197.3 %all-to-all-start = ((s32[16,1,384]{2,1,0:T(1,128)}), s32[16,1,384]{2,1,0:T(1,128)S(1)}, u32[]{:S(2)}, u32[]{:S(2)}) async-start(s32[16,1,384]{2,1,0:T(1,128)} %bitcast.9), calls=%async_computation | async-start | bytes 49152 | tf_op jit(solution)/shard_map/all_to_all | solution.py:114
  108.0 12.2 %copy-start.5 = (s32[2048]{0:T(1024)S(1)}, s32[2048]{0:T(1024)}, u32[]{:S(2)}) copy-start(s32[2048]{0:T(1024)} %param.10) | copy-start | bytes 24580
  119.8 0.8 copy-start.6
  187.0 1.2 copy-start
  228.8 88.9 %all-to-all-start.1 = ((bf16[16,384,512]{2,1,0:T(8,128)(2,1)}), bf16[16,384,512]{2,1,0:T(8,128)(2,1)}, u32[]{:S(2)}, u32[]{:S(2)}) async-start(bf16[16,384,512]{2,1,0:T(8,128)(2,1)} %bitcast.53), calls=%async_computation.1 | async-start | bytes 12582912 | tf_op jit(solution)/shard_map/all_to_all | solution.py:135
  317.7 6.9 %copy-start.2 = (bf16[512,1,1024]{2,0,1:T(8,128)(2,1)S(1)}, bf16[512,1,1024]{2,0,1:T(8,128)(2,1)}, u32[]{:S(2)}) copy-start(bf16[512,1,1024]{2,0,1:T(8,128)(2,1)} %param.6) | copy-start | bytes 3145732
  317.7 91.2 %all-to-all-start.2 = ((bf16[16,384,512]{2,1,0:T(8,128)(2,1)}), bf16[16,384,512]{2,1,0:T(8,128)(2,1)}, u32[]{:S(2)}, u32[]{:S(2)}) async-start(bf16[16,384,512]{2,1,0:T(8,128)(2,1)} %bitcast.52), calls=%async_computation.2 | async-start | bytes 12582912 | tf_op jit(solution)/shard_map/all_to_all | solution.py:135
Sparse Core Ops, SparseCore 0:
  9.8 76.8 all-gather.3
  89.2 70.4 all-gather.5

commit v4 on v2

--- a/solution.py
+++ b/solution.py
@@ -104,15 +104,16 @@
     owner_flat = jnp.concatenate([pair_owner[:, 0], pair_owner[:, 1]])
     slot_flat = jnp.concatenate([pair_slot[:, 0], pair_slot[:, 1]])
     position = owner_positions(owner_flat, owners)
-    flat_slot = owner_flat * capacity + position
+    part = capacity // 2
+    flat_slot = (position // part) * (owners * part) + owner_flat * part + position % part
     request = (
-        jnp.full((owners * capacity,), station_count, jnp.int32)
+        jnp.full((2 * owners * part,), station_count, jnp.int32)
         .at[flat_slot]
         .set(slot_flat, unique_indices=True)
     )
     wanted = lax.all_to_all(
-        request.reshape(owners, capacity), "pairs", split_axis=0, concat_axis=0, tiled=True
-    ).reshape(owners * capacity)
+        request.reshape(2, owners, part), "pairs", split_axis=1, concat_axis=1, tiled=True
+    ).reshape(2, owners * part)
 
     rows0 = pair_owner[:, 0] * station_count + pair_slot[:, 0]
     rows1 = pair_owner[:, 1] * station_count + pair_slot[:, 1]
@@ -127,21 +128,19 @@
         win_start[:, None], win_end[:, None], table,
     ).reshape(2 * pair_count, full_width)
     outgoing = (
-        jnp.zeros((owners * capacity, full_width), jnp.bfloat16)
+        jnp.zeros((2 * owners * part, full_width), jnp.bfloat16)
         .at[flat_slot]
         .set(contribs, unique_indices=True)
-    )
-    incoming = lax.all_to_all(
-        outgoing.reshape(owners, capacity, full_width),
-        "pairs",
-        split_axis=0,
-        concat_axis=0,
-        tiled=True,
-    ).reshape(owners * capacity, full_width)
-    onehot = (
-        wanted[None, :] == jnp.arange(station_count, dtype=jnp.int32)[:, None]
-    ).astype(jnp.bfloat16)
-    summed = jnp.dot(onehot, incoming, preferred_element_type=jnp.float32)
+    ).reshape(2, owners, part, full_width)
+    station_ids = jnp.arange(station_count, dtype=jnp.int32)[:, None]
+    summed = None
+    for half in range(2):
+        incoming = lax.all_to_all(
+            outgoing[half], "pairs", split_axis=0, concat_axis=0, tiled=True
+        ).reshape(owners * part, full_width)
+        onehot = (wanted[half][None, :] == station_ids).astype(jnp.bfloat16)
+        partial = jnp.dot(onehot, incoming, preferred_element_type=jnp.float32)
+        summed = partial if summed is None else summed + partial
     result = 0.25 * (
         summed[:, :half_width] * own_spec[:, :half_width]
         + summed[:, half_width:] * own_spec[:, half_width:]

time: 402 us -> 403 us (level)
  waiting for transfers between devices: 172 us -> 80 us
  blocking collectives: 45.2 us -> 123 us
  local copies, waits for them, and re-layouts: 110 us -> 121 us
  matrix products: 9.99 us -> 14.3 us
    all_to_all x2, waiting for transfers between devices: 168 us -> 75.8 us  [the longest x1 75.8 us: shards(): lax.all_to_all(outgoing[half], 'pairs', split_axis=0, concat_axis=0, tile...]
    all_to_all x0 -> x1, blocking collectives: none -> 78 us  [shards(): lax.all_to_all(outgoing[half], 'pairs', split_axis=0, concat_axis=0, tile...]
    slice x1 -> x3, local copies, waits for them, and re-layouts: 0.46 us -> 10.9 us  [the longest x1 10.4 us: shards(): outgoing[half]]
    dot_general x1 -> x2, matrix products: 9.99 us -> 14.3 us  [shards(): partial = jnp.dot(onehot, incoming, preferred_element_type=jnp.float32)]
  transfers between devices with their start and end apart: 3 -> 3, of which waited for: 2 -> 2; matrix products, arithmetic and copies ran while one was open for 31% -> 35% of each run, Pallas kernels for 4% -> 4%
where the time goes in v4:
time: 403 us; the launch traced here: 402 us
  blocking collectives  123 us (31%)
  local copies, waits for them, and re-layouts  121 us (30%)
  waiting for transfers between devices  80 us (20%)
  Pallas kernels  17.8 us (4%)
  other arithmetic  17.3 us (4%)
  starting transfers between devices  14.7 us (4%)
  matrix products  14.3 us (4%)
  between operations  13.6 us (3%)
    all_to_all x1, blocking collectives, shards(): lax.all_to_all(outgoing[half], 'pairs', split_axis=0, concat_axis=0, tile...  78 us
    all_to_all x1, waiting for transfers between devices, shards(): lax.all_to_all(outgoing[half], 'pairs', split_axis=0, concat_axis=0, tile...  75.8 us
    all_gather x1, blocking collectives, shards(): panel_scale = lax.all_gather(scale, 'pairs', axis=0, tiled=True)  29 us
    scatter x1, local copies, waits for them, and re-layouts, shards(): outgoing = jnp.zeros((2 * owners * part, full_width), jnp.bfloat16).at[fl...  26.6 us
    gather x1, local copies, waits for them, and re-layouts, shards(): far_raw = panel_raw[rows1]  18.9 us
    gather x1, local copies, waits for them, and re-layouts, shards(): near_raw = panel_raw[rows0]  18.9 us
    pallas_call x1, Pallas kernels, pair_contributions(): pl.pallas_call(pair_kernel, grid=(pairs // block,), in_specs=[pl.BlockSpe...  17.8 us
    psum x1, blocking collectives, shards(): total_power = lax.psum(local_power, 'band')  16 us
  transfers between devices with their start and end apart: 3, of which 2 were waited for; matrix products, arithmetic and copies ran while one was open for 35% of the time, Pallas kernels for 4%

profile of v4, /device:TPU:1, one launch (start us, length us, event | category | flops | bytes accessed | tf_op | source)
XLA Modules:
  0.0 401.8 jit_solution(14565147511477923370)
XLA Ops:
  7.3 0.8 compare_select_fusion.1
  8.1 4.6 %reduce-window.6 = s32[16,32,128]{2,1,0:T(8,128)S(1)} reduce-window(s32[16,32,128]{2,1,0:T(8,128)S(1)} %fusion.21, s32[]{:T(128)} %constant.26.clone.1), window={size=1x1x128 pad=0_0x0_0x127_0}, to_apply=%region_0.0 | reduce-window | flops 8323072 | bytes 524292 | tf_op jit(solution)/shard_map/reduce-window
  13.9 15.5 %scatter_custom_fusion = s32[6144]{0:T(1024)S(1)} fusion(s32[4096]{0:T(1024)S(1)} %bitcast.74, s32[4096]{0:T(1024)S(1)} %pad_add_fusion.2, s32[]{:T(128)} %constant.25.clone.1), kind=kCustom, calls=%fused_computation.59 | custom fusion | bytes 24580 | tf_op jit(solution)/shard_map/scatter | solution.py:112
  30.2 9.1 %all-to-all-start = ((s32[2,16,192]{2,0,1:T(2,128)}), s32[2,16,192]{2,0,1:T(2,128)S(1)}, u32[]{:S(2)}, u32[]{:S(2)}) async-start(s32[2,16,192]{2,0,1:T(2,128)} %copy.18), calls=%async_computation | async-start | bytes 65536 | tf_op jit(solution)/shard_map/all_to_all | solution.py:114
  39.6 16.0 %psum.7 = f32[512]{0:T(512)S(1)} all-reduce(f32[512]{0:T(512)S(1)} %fusion.6), channel_id=1, replica_groups=mesh['pairs'=16,'band'=8] {'band'}, use_global_device_ids=true, to_apply=%region_5.6 | all-reduce | flops 512 | bytes 4096 | tf_op jit(solution)/shard_map/psum | solution.py:98
  55.6 29.0 %all-gather.1 = f32[16,1,512]{2,1,0:T(1,128)S(1)} all-gather(f32[1,1,512]{2,1,0:T(1,128)S(1)} %bitcast.73), channel_id=1, replica_groups=mesh['pairs'=16,'band'=8] {'pairs'}, dimensions={0}, use_global_device_ids=true | all-gather | bytes 34816 | tf_op jit(solution)/shard_map/all_gather | solution.py:102
  84.6 11.8 %gather_fusion.2 = f32[2048]{0:T(1024)S(1)} fusion(f32[8192]{0:T(1024)S(1)} %bitcast.50, s32[2048]{0:T(1024)S(1)} %broadcast_clamp_fusion.1), kind=kCustom, calls=%fused_computation.2 | custom fusion | bytes 24576 | tf_op jit(solution)/shard_map/gather | solution.py:122
  96.8 11.8 %gather_fusion.3 = f32[2048]{0:T(1024)S(1)} fusion(f32[8192]{0:T(1024)S(1)} %bitcast.51, s32[2048]{0:T(1024)S(1)} %broadcast_clamp_fusion), kind=kCustom, calls=%fused_computation.3 | custom fusion | bytes 24576 | tf_op jit(solution)/shard_map/gather | solution.py:123
  109.3 1.3 copy.22.we_ref
  110.7 8.6 %multiply_convert_fusion = (bf16[512,1024]{1,0:T(8,128)(2,1)S(1)}, bf16[512,1024]{1,0:T(8,128)(2,1)S(1)}) fusion(), kind=kLoop, calls=%fused_computation.25 | loop fusion | flops 9961472 | bytes 2097152 | tf_op jit(solution)/shard_map/convert.1
  119.2 1.5 pad_maximum_fusion.table_ref
  120.8 3.5 all-gather.4.cloned.1.call-done
  124.3 18.9 %gather_fusion = bf16[2048,1024]{1,0:T(8,128)(2,1)} fusion(bf16[8192,1024]{1,0:T(8,128)(2,1)} %bitcast.52, s32[2048]{0:T(1024)S(1)} %broadcast_clamp_fusion.1), kind=kCustom, calls=%fused_computation | custom fusion | bytes 8396800 | tf_op jit(solution)/shard_map/gather | solution.py:120
  143.2 18.9 %gather_fusion.1 = bf16[2048,1024]{1,0:T(8,128)(2,1)} fusion(bf16[8192,1024]{1,0:T(8,128)(2,1)} %bitcast.53, s32[2048]{0:T(1024)S(1)} %broadcast_clamp_fusion), kind=kCustom, calls=%fused_computation.1 | custom fusion | bytes 8396800 | tf_op jit(solution)/shard_map/gather | solution.py:121
  162.1 1.2 copy-done
  163.3 17.8 %shard_map.64 = bf16[2,2048,1024]{2,1,0:T(8,128)(2,1)} custom-call(bf16[2048,1024]{1,0:T(8,128)(2,1)} %gather_fusion, bf16[2048,1024]{1,0:T(8,128)(2,1)} %gather_fusion.1, f32[2048,1]{1,0:T(8,128)S(1)} %copy.19.ns_ref, f32[2048,1]{1,0:T(8,128)S(1)} %copy.20.fs_ref, bf16[2048,1024]{1,0:T(8,128)(2,1)} %bitcast.58, s32[2048,1]{1,0:T(8,128)S(1)} %copy.21.ws_ref, ...), custom_call_target="tpu_custom_call" | custom-call | tf_op jit(solution)/shard_map/pallas_call | solution.py:66
  181.1 26.6 %scatter_custom_fusion.1 = bf16[6144,1024]{1,0:T(8,128)(2,1)} fusion(s32[4096]{0:T(1024)S(1)} %bitcast.75, bf16[4096,1024]{1,0:T(8,128)(2,1)} %bitcast.56, bf16[]{:T(256)} %constant.56.clone.1), kind=kCustom, calls=%fused_computation.7 | custom fusion | bytes 12583424 | tf_op jit(solution)/shard_map/scatter | solution.py:133
  207.7 10.4 %fusion.26 = (bf16[3072,1024]{1,0:T(8,128)(2,1)}, bf16[3072,1024]{1,0:T(8,128)(2,1)}) fusion(bf16[6144,1024]{1,0:T(8,128)(2,1)} %scatter_custom_fusion.1), kind=kLoop, calls=%fused_computation.66 | loop fusion | bytes 25165824 | tf_op jit(solution)/shard_map/slice | solution.py:139
  218.1 78.0 %all_to_all.15 = bf16[16,192,1024]{2,1,0:T(8,128)(2,1)} all-to-all(bf16[16,192,1024]{2,1,0:T(8,128)(2,1)} %bitcast.55), channel_id=1, replica_groups=mesh['pairs'=16,'band'=8] {'pairs'}, dimensions={0} | all-to-all | bytes 12582912 | tf_op jit(solution)/shard_map/all_to_all | solution.py:138
  296.1 5.6 %all-to-all-start.2 = ((bf16[16,192,1024]{2,1,0:T(8,128)(2,1)}), bf16[16,192,1024]{2,1,0:T(8,128)(2,1)}, u32[]{:S(2)}, u32[]{:S(2)}) async-start(bf16[16,192,1024]{2,1,0:T(8,128)(2,1)} %bitcast.54), calls=%async_computation.2 | async-start | bytes 12582912 | tf_op jit(solution)/shard_map/all_to_all | solution.py:138
  302.2 7.5 %fusion.2 = f32[512,1024]{1,0:T(8,128)} fusion(bf16[3072,1024]{1,0:T(8,128)(2,1)} %bitcast.57, s32[3072]{0:T(1024)S(1)} %eq.61), kind=kOutput, calls=%fused_computation.10 | convolution fusion | flops 3222798336 | bytes 8400896 | tf_op jit(solution)/shard_map/dot_general | solution.py:142
  309.7 75.8 %all-to-all-done.2 = bf16[16,192,1024]{2,1,0:T(8,128)(2,1)} async-done(((bf16[16,192,1024]{2,1,0:T(8,128)(2,1)}), bf16[16,192,1024]{2,1,0:T(8,128)(2,1)}, u32[]{:S(2)}, u32[]{:S(2)}) %all-to-all-start.2) | async-done | bytes 6291488 | tf_op jit(solution)/shard_map/all_to_all | solution.py:138
  385.5 6.8 %fusion.14 = f32[512,1024]{1,0:T(8,128)S(1)} fusion(f32[512,1024]{1,0:T(8,128)} %fusion.2, bf16[3072,1024]{1,0:T(8,128)(2,1)} %bitcast.25, s32[3072]{0:T(1024)S(1)} %eq.65), kind=kOutput, calls=%fused_computation.30 | convolution fusion | flops 3223322624 | bytes 10498048 | tf_op jit(solution)/shard_map/dot_general | solution.py:142
  392.9 2.0 copy.23
  (37 shorter events, 5.0 us)
Async XLA Ops:
  6.5 32.8 %copy-start.1 = (bf16[512,1,1024]{2,0,1:T(8,128)(2,1)S(1)}, bf16[512,1,1024]{2,0,1:T(8,128)(2,1)}, u32[]{:S(2)}) copy-start(bf16[512,1,1024]{2,0,1:T(8,128)(2,1)} %param.6) | copy-start | bytes 3145732
  6.5 117.7 %all-gather.4.cloned.1.call-start = ((), (), s32[]{:S(2)}) async-start(), calls=%async_computation.3 | async-start | bytes 17825792 | tf_op jit(solution)/shard_map/all_gather | solution.py:95
  30.2 188.0 %all-to-all-start = ((s32[2,16,192]{2,0,1:T(2,128)}), s32[2,16,192]{2,0,1:T(2,128)S(1)}, u32[]{:S(2)}, u32[]{:S(2)}) async-start(s32[2,16,192]{2,0,1:T(2,128)} %copy.18), calls=%async_computation | async-start | bytes 65536 | tf_op jit(solution)/shard_map/all_to_all | solution.py:114
  96.7 12.2 %copy-start.3 = (s32[2048]{0:T(1024)S(1)}, s32[2048]{0:T(1024)}, u32[]{:S(2)}) copy-start(s32[2048]{0:T(1024)} %param.10) | copy-start | bytes 24580
  108.5 0.8 copy-start.4
  162.1 1.2 copy-start
  296.1 5.6 %copy-start.2 = (bf16[512,1,1024]{2,0,1:T(8,128)(2,1)S(1)}, bf16[512,1,1024]{2,0,1:T(8,128)(2,1)}, u32[]{:S(2)}) copy-start(bf16[512,1,1024]{2,0,1:T(8,128)(2,1)} %param.6) | copy-start | bytes 3145732
  296.1 89.4 %all-to-all-start.2 = ((bf16[16,192,1024]{2,1,0:T(8,128)(2,1)}), bf16[16,192,1024]{2,1,0:T(8,128)(2,1)}, u32[]{:S(2)}, u32[]{:S(2)}) async-start(bf16[16,192,1024]{2,1,0:T(8,128)(2,1)} %bitcast.54), calls=%async_computation.2 | async-start | bytes 12582912 | tf_op jit(solution)/shard_map/all_to_all | solution.py:138
Sparse Core Ops, SparseCore 0:
  9.8 114.4 all-gather.3

commit v5 on v4

--- a/solution.py
+++ b/solution.py
@@ -127,16 +127,22 @@
         near_raw, far_raw, near_scale, far_scale, obs,
         win_start[:, None], win_end[:, None], table,
     ).reshape(2 * pair_count, full_width)
-    outgoing = (
-        jnp.zeros((2 * owners * part, full_width), jnp.bfloat16)
-        .at[flat_slot]
-        .set(contribs, unique_indices=True)
-    ).reshape(2, owners, part, full_width)
     station_ids = jnp.arange(station_count, dtype=jnp.int32)[:, None]
     summed = None
     for half in range(2):
+        half_slot = jnp.where(position // part == half, flat_slot - half * owners * part, -1)
+        half_slot = jnp.where(half_slot < 0, owners * part, half_slot)
+        outgoing = (
+            jnp.zeros((owners * part, full_width), jnp.bfloat16)
+            .at[half_slot]
+            .set(contribs, mode="drop")
+        )
         incoming = lax.all_to_all(
-            outgoing[half], "pairs", split_axis=0, concat_axis=0, tiled=True
+            outgoing.reshape(owners, part, full_width),
+            "pairs",
+            split_axis=0,
+            concat_axis=0,
+            tiled=True,
         ).reshape(owners * part, full_width)
         onehot = (wanted[half][None, :] == station_ids).astype(jnp.bfloat16)
         partial = jnp.dot(onehot, incoming, preferred_element_type=jnp.float32)

time: 403 us -> 402 us (level)
  blocking collectives: 123 us -> 45.1 us
  waiting for transfers between devices: 80 us -> 141 us
  local copies, waits for them, and re-layouts: 121 us -> 130 us
  starting transfers between devices: 14.7 us -> 20.7 us
    all_to_all x1 -> x0, blocking collectives: 78 us -> none  [shards(): lax.all_to_all(outgoing[half], 'pairs', split_axis=0, concat_axis=0, tile...]
    all_to_all x1 -> x2, waiting for transfers between devices: 75.8 us -> 137 us  [shards(): lax.all_to_all(outgoing.reshape(owners, part, full_width), 'pairs', split...]
    scatter x1 -> x2, local copies, waits for them, and re-layouts: 26.6 us -> 46.4 us  [shards(): outgoing = jnp.zeros((owners * part, full_width), jnp.bfloat16).at[half_s...]
    slice x2 -> x1, local copies, waits for them, and re-layouts: 10.9 us -> 0.46 us  [the longest x1 10.4 us: shards(): outgoing[half]]
    all_to_all x1 -> x2, starting transfers between devices: 5.57 us -> 11.6 us  [shards(): lax.all_to_all(outgoing.reshape(owners, part, full_width), 'pairs', split...]
  transfers between devices with their start and end apart: 3 -> 4, of which waited for: 2 -> 3; matrix products, arithmetic and copies ran while one was open for 35% -> 38% of each run, Pallas kernels for 4% -> 4%
where the time goes in v5:
time: 402 us; the launch traced here: 401 us
  waiting for transfers between devices  141 us (35%)
  local copies, waits for them, and re-layouts  130 us (32%)
  blocking collectives  45.1 us (11%)
  starting transfers between devices  20.7 us (5%)
  Pallas kernels  17.8 us (4%)
  other arithmetic  17.4 us (4%)
  matrix products  14.4 us (4%)
  between operations  13.6 us (3%)
    all_to_all x2, waiting for transfers between devices, shards(): lax.all_to_all(outgoing.reshape(owners, part, full_width), 'pairs', split...  137 us
    scatter x2, local copies, waits for them, and re-layouts, shards(): outgoing = jnp.zeros((owners * part, full_width), jnp.bfloat16).at[half_s...  46.4 us
    all_gather x1, blocking collectives, shards(): panel_scale = lax.all_gather(scale, 'pairs', axis=0, tiled=True)  29.2 us
    gather x1, local copies, waits for them, and re-layouts, shards(): near_raw = panel_raw[rows0]  18.9 us
    gather x1, local copies, waits for them, and re-layouts, shards(): far_raw = panel_raw[rows1]  18.9 us
    pallas_call x1, Pallas kernels, pair_contributions(): pl.pallas_call(pair_kernel, grid=(pairs // block,), in_specs=[pl.BlockSpe...  17.8 us
    psum x1, blocking collectives, shards(): total_power = lax.psum(local_power, 'band')  16 us
    scatter x1, local copies, waits for them, and re-layouts, shards(): request = jnp.full((2 * owners * part,), station_count, jnp.int32).at[fla...  15.5 us
  transfers between devices with their start and end apart: 4, of which 3 were waited for; matrix products, arithmetic and copies ran while one was open for 38% of the time, Pallas kernels for 4%

profile of v5, /device:TPU:1, one launch (start us, length us, event | category | flops | bytes accessed | tf_op | source)
XLA Modules:
  0.0 400.9 jit_solution(8044167654135437500)
XLA Ops:
  8.1 4.6 %reduce-window.6 = s32[16,32,128]{2,1,0:T(8,128)S(1)} reduce-window(s32[16,32,128]{2,1,0:T(8,128)S(1)} %fusion.23, s32[]{:T(128)} %constant.34.clone.1), window={size=1x1x128 pad=0_0x0_0x127_0}, to_apply=%region_0.0 | reduce-window | flops 8323072 | bytes 524292 | tf_op jit(solution)/shard_map/reduce-window
  14.0 15.5 %scatter_custom_fusion = s32[6144]{0:T(1024)S(1)} fusion(s32[4096]{0:T(1024)S(1)} %bitcast.78, s32[4096]{0:T(1024)S(1)} %pad_add_fusion.2, s32[]{:T(128)} %constant.33.clone.1), kind=kCustom, calls=%fused_computation.68 | custom fusion | bytes 24580 | tf_op jit(solution)/shard_map/scatter | solution.py:112
  30.2 9.1 %all-to-all-start = ((s32[2,16,192]{2,0,1:T(2,128)}), s32[2,16,192]{2,0,1:T(2,128)S(1)}, u32[]{:S(2)}, u32[]{:S(2)}) async-start(s32[2,16,192]{2,0,1:T(2,128)} %copy.18), calls=%async_computation | async-start | bytes 65536 | tf_op jit(solution)/shard_map/all_to_all | solution.py:114
  39.7 16.0 %psum.7 = f32[512]{0:T(512)S(1)} all-reduce(f32[512]{0:T(512)S(1)} %fusion.8), channel_id=1, replica_groups=mesh['pairs'=16,'band'=8] {'band'}, use_global_device_ids=true, to_apply=%region_5.6 | all-reduce | flops 512 | bytes 4096 | tf_op jit(solution)/shard_map/psum | solution.py:98
  55.7 8.6 %multiply_convert_fusion = (bf16[512,1024]{1,0:T(8,128)(2,1)S(1)}, bf16[512,1024]{1,0:T(8,128)(2,1)S(1)}) fusion(), kind=kLoop, calls=%fused_computation.28 | loop fusion | flops 9961472 | bytes 2097152 | tf_op jit(solution)/shard_map/convert.1
  64.2 1.6 pad_maximum_fusion.table_ref
  65.8 29.2 %all-gather.1 = f32[16,1,512]{2,1,0:T(1,128)S(1)} all-gather(f32[1,1,512]{2,1,0:T(1,128)S(1)} %bitcast.75), channel_id=1, replica_groups=mesh['pairs'=16,'band'=8] {'pairs'}, dimensions={0}, use_global_device_ids=true | all-gather | bytes 34816 | tf_op jit(solution)/shard_map/all_gather | solution.py:102
  95.0 11.8 %gather_fusion.2 = f32[2048]{0:T(1024)S(1)} fusion(f32[8192]{0:T(1024)S(1)} %bitcast.52, s32[2048]{0:T(1024)S(1)} %broadcast_clamp_fusion.1), kind=kCustom, calls=%fused_computation.2 | custom fusion | bytes 24576 | tf_op jit(solution)/shard_map/gather | solution.py:122
  107.1 11.8 %gather_fusion.3 = f32[2048]{0:T(1024)S(1)} fusion(f32[8192]{0:T(1024)S(1)} %bitcast.53, s32[2048]{0:T(1024)S(1)} %broadcast_clamp_fusion), kind=kCustom, calls=%fused_computation.3 | custom fusion | bytes 24576 | tf_op jit(solution)/shard_map/gather | solution.py:123
  119.7 1.3 copy.22.we_ref
  121.0 3.2 all-gather.4.cloned.1.call-done
  124.3 18.9 %gather_fusion = bf16[2048,1024]{1,0:T(8,128)(2,1)} fusion(bf16[8192,1024]{1,0:T(8,128)(2,1)} %bitcast.54, s32[2048]{0:T(1024)S(1)} %broadcast_clamp_fusion.1), kind=kCustom, calls=%fused_computation | custom fusion | bytes 8396800 | tf_op jit(solution)/shard_map/gather | solution.py:120
  143.2 18.9 %gather_fusion.1 = bf16[2048,1024]{1,0:T(8,128)(2,1)} fusion(bf16[8192,1024]{1,0:T(8,128)(2,1)} %bitcast.55, s32[2048]{0:T(1024)S(1)} %broadcast_clamp_fusion), kind=kCustom, calls=%fused_computation.1 | custom fusion | bytes 8396800 | tf_op jit(solution)/shard_map/gather | solution.py:121
  162.1 1.2 copy-done
  163.3 17.8 %shard_map.64 = bf16[2,2048,1024]{2,1,0:T(8,128)(2,1)} custom-call(bf16[2048,1024]{1,0:T(8,128)(2,1)} %gather_fusion, bf16[2048,1024]{1,0:T(8,128)(2,1)} %gather_fusion.1, f32[2048,1]{1,0:T(8,128)S(1)} %copy.19.ns_ref, f32[2048,1]{1,0:T(8,128)S(1)} %copy.20.fs_ref, bf16[2048,1024]{1,0:T(8,128)(2,1)} %bitcast.60, s32[2048,1]{1,0:T(8,128)S(1)} %copy.21.ws_ref, ...), custom_call_target="tpu_custom_call" | custom-call | tf_op jit(solution)/shard_map/pallas_call | solution.py:66
  181.1 23.4 %scatter_custom_fusion.1 = bf16[3072,1024]{1,0:T(8,128)(2,1)} fusion(s32[4096]{0:T(1024)S(1)} %bitcast.77, bf16[4096,1024]{1,0:T(8,128)(2,1)} %bitcast.58, bf16[]{:T(256)} %constant.64.clone.1), kind=kCustom, calls=%fused_computation.17 | custom fusion | bytes 6291968 | tf_op jit(solution)/shard_map/scatter | solution.py:138
  204.5 4.7 %all-to-all-start.1 = ((bf16[16,192,1024]{2,1,0:T(8,128)(2,1)}), bf16[16,192,1024]{2,1,0:T(8,128)(2,1)}, u32[]{:S(2)}, u32[]{:S(2)}) async-start(bf16[16,192,1024]{2,1,0:T(8,128)(2,1)} %bitcast.57), calls=%async_computation.1 | async-start | bytes 12582912 | tf_op jit(solution)/shard_map/all_to_all | solution.py:140
  209.2 23.1 %scatter_custom_fusion.2 = bf16[3072,1024]{1,0:T(8,128)(2,1)} fusion(s32[4096]{0:T(1024)S(1)} %bitcast.76, bf16[4096,1024]{1,0:T(8,128)(2,1)} %bitcast.59, bf16[]{:T(256)} %constant.64.clone.1), kind=kCustom, calls=%fused_computation.15 | custom fusion | bytes 6291968 | tf_op jit(solution)/shard_map/scatter | solution.py:138
  232.2 61.2 %all-to-all-done.1 = bf16[16,192,1024]{2,1,0:T(8,128)(2,1)} async-done(((bf16[16,192,1024]{2,1,0:T(8,128)(2,1)}), bf16[16,192,1024]{2,1,0:T(8,128)(2,1)}, u32[]{:S(2)}, u32[]{:S(2)}) %all-to-all-start.1) | async-done | bytes 6291488 | tf_op jit(solution)/shard_map/all_to_all | solution.py:140
  293.4 6.9 %all-to-all-start.2 = ((bf16[16,192,1024]{2,1,0:T(8,128)(2,1)}), bf16[16,192,1024]{2,1,0:T(8,128)(2,1)}, u32[]{:S(2)}, u32[]{:S(2)}) async-start(bf16[16,192,1024]{2,1,0:T(8,128)(2,1)} %bitcast.56), calls=%async_computation.2 | async-start | bytes 12582912 | tf_op jit(solution)/shard_map/all_to_all | solution.py:140
  300.8 7.5 %fusion = f32[512,1024]{1,0:T(8,128)} fusion(bf16[3072,1024]{1,0:T(8,128)(2,1)} %bitcast.24, s32[3072]{0:T(1024)S(1)} %eq.82), kind=kOutput, calls=%fused_computation.9 | convolution fusion | flops 3222798336 | bytes 8400896 | tf_op jit(solution)/shard_map/dot_general | solution.py:148
  308.4 76.3 %all-to-all-done.2 = bf16[16,192,1024]{2,1,0:T(8,128)(2,1)} async-done(((bf16[16,192,1024]{2,1,0:T(8,128)(2,1)}), bf16[16,192,1024]{2,1,0:T(8,128)(2,1)}, u32[]{:S(2)}, u32[]{:S(2)}) %all-to-all-start.2) | async-done | bytes 6291488 | tf_op jit(solution)/shard_map/all_to_all | solution.py:140
  384.7 6.8 %fusion.16 = f32[512,1024]{1,0:T(8,128)S(1)} fusion(f32[512,1024]{1,0:T(8,128)} %fusion, bf16[3072,1024]{1,0:T(8,128)(2,1)} %bitcast.27, s32[3072]{0:T(1024)S(1)} %eq.87), kind=kOutput, calls=%fused_computation.33 | convolution fusion | flops 3223322624 | bytes 10498048 | tf_op jit(solution)/shard_map/dot_general | solution.py:148
  392.0 2.0 copy.23
  (39 shorter events, 5.9 us)
Async XLA Ops:
  6.5 32.8 %copy-start.1 = (bf16[512,1,1024]{2,0,1:T(8,128)(2,1)S(1)}, bf16[512,1,1024]{2,0,1:T(8,128)(2,1)}, u32[]{:S(2)}) copy-start(bf16[512,1,1024]{2,0,1:T(8,128)(2,1)} %param.6) | copy-start | bytes 3145732
  6.5 117.7 %all-gather.4.cloned.1.call-start = ((), (), s32[]{:S(2)}) async-start(), calls=%async_computation.3 | async-start | bytes 17825792 | tf_op jit(solution)/shard_map/all_gather | solution.py:95
  30.2 174.3 %all-to-all-start = ((s32[2,16,192]{2,0,1:T(2,128)}), s32[2,16,192]{2,0,1:T(2,128)S(1)}, u32[]{:S(2)}, u32[]{:S(2)}) async-start(s32[2,16,192]{2,0,1:T(2,128)} %copy.18), calls=%async_computation | async-start | bytes 65536 | tf_op jit(solution)/shard_map/all_to_all | solution.py:114
  107.1 12.2 %copy-start.3 = (s32[2048]{0:T(1024)S(1)}, s32[2048]{0:T(1024)}, u32[]{:S(2)}) copy-start(s32[2048]{0:T(1024)} %param.10) | copy-start | bytes 24580
  107.1 12.6 %copy-start.4 = (s32[2048]{0:T(1024)S(1)}, s32[2048]{0:T(1024)}, u32[]{:S(2)}) copy-start(s32[2048]{0:T(1024)} %param.11) | copy-start | bytes 24580
  162.1 1.2 copy-start
  204.5 88.9 %all-to-all-start.1 = ((bf16[16,192,1024]{2,1,0:T(8,128)(2,1)}), bf16[16,192,1024]{2,1,0:T(8,128)(2,1)}, u32[]{:S(2)}, u32[]{:S(2)}) async-start(bf16[16,192,1024]{2,1,0:T(8,128)(2,1)} %bitcast.57), calls=%async_computation.1 | async-start | bytes 12582912 | tf_op jit(solution)/shard_map/all_to_all | solution.py:140
  293.4 6.9 %copy-start.2 = (bf16[512,1,1024]{2,0,1:T(8,128)(2,1)S(1)}, bf16[512,1,1024]{2,0,1:T(8,128)(2,1)}, u32[]{:S(2)}) copy-start(bf16[512,1,1024]{2,0,1:T(8,128)(2,1)} %param.6) | copy-start | bytes 3145732
  293.4 91.2 %all-to-all-start.2 = ((bf16[16,192,1024]{2,1,0:T(8,128)(2,1)}), bf16[16,192,1024]{2,1,0:T(8,128)(2,1)}, u32[]{:S(2)}, u32[]{:S(2)}) async-start(bf16[16,192,1024]{2,1,0:T(8,128)(2,1)} %bitcast.56), calls=%async_computation.2 | async-start | bytes 12582912 | tf_op jit(solution)/shard_map/all_to_all | solution.py:140
Sparse Core Ops, SparseCore 0:
  9.8 114.4 all-gather.3

commit v6 on v2

--- a/solution.py
+++ b/solution.py
@@ -104,16 +104,6 @@
     owner_flat = jnp.concatenate([pair_owner[:, 0], pair_owner[:, 1]])
     slot_flat = jnp.concatenate([pair_slot[:, 0], pair_slot[:, 1]])
     position = owner_positions(owner_flat, owners)
-    flat_slot = owner_flat * capacity + position
-    request = (
-        jnp.full((owners * capacity,), station_count, jnp.int32)
-        .at[flat_slot]
-        .set(slot_flat, unique_indices=True)
-    )
-    wanted = lax.all_to_all(
-        request.reshape(owners, capacity), "pairs", split_axis=0, concat_axis=0, tiled=True
-    ).reshape(owners * capacity)
-
     rows0 = pair_owner[:, 0] * station_count + pair_slot[:, 0]
     rows1 = pair_owner[:, 1] * station_count + pair_slot[:, 1]
     near_raw = panel_raw[rows0]
@@ -126,22 +116,15 @@
         near_raw, far_raw, near_scale, far_scale, obs,
         win_start[:, None], win_end[:, None], table,
     ).reshape(2 * pair_count, full_width)
-    outgoing = (
-        jnp.zeros((owners * capacity, full_width), jnp.bfloat16)
-        .at[flat_slot]
-        .set(contribs, unique_indices=True)
+    endpoint_rows = jnp.concatenate([rows0, rows1])
+    dense = (
+        jnp.zeros((owners * station_count, full_width), jnp.float32)
+        .at[endpoint_rows]
+        .add(contribs.astype(jnp.float32))
+    ).astype(jnp.bfloat16)
+    summed = lax.psum_scatter(dense, "pairs", scatter_dimension=0, tiled=True).astype(
+        jnp.float32
     )
-    incoming = lax.all_to_all(
-        outgoing.reshape(owners, capacity, full_width),
-        "pairs",
-        split_axis=0,
-        concat_axis=0,
-        tiled=True,
-    ).reshape(owners * capacity, full_width)
-    onehot = (
-        wanted[None, :] == jnp.arange(station_count, dtype=jnp.int32)[:, None]
-    ).astype(jnp.bfloat16)
-    summed = jnp.dot(onehot, incoming, preferred_element_type=jnp.float32)
     result = 0.25 * (
         summed[:, :half_width] * own_spec[:, :half_width]
         + summed[:, half_width:] * own_spec[:, half_width:]

time: 402 us -> 402 us (level)
  other arithmetic: 17.2 us -> 79.5 us
  local copies, waits for them, and re-layouts: 110 us -> 68 us
  starting transfers between devices: 14.2 us -> 0.04 us
  matrix products: 9.99 us -> 0 us
    all_to_all x2 -> x0, waiting for transfers between devices: 168 us -> none  [the longest x1 168 us: shards(): lax.all_to_all(outgoing.reshape(owners, capacity, full_width), 'pairs', s...]
    reduce_scatter x0 -> x1, waiting for transfers between devices: none -> 143 us  [shards(): lax.psum_scatter(dense, 'pairs', scatter_dimension=0, tiled=True)]
    scatter-add x0 -> x1, other arithmetic: none -> 48 us  [shards(): dense = jnp.zeros((owners * station_count, full_width), jnp.float32).at[e...]
    scatter x2 -> x0, local copies, waits for them, and re-layouts: 42.8 us -> none  [the longest x1 26.7 us: shards(): outgoing = jnp.zeros((owners * capacity, full_width), jnp.bfloat16).at[fl...]
    all_gather x1, waiting for transfers between devices: 3.5 us -> 32.2 us  [shards(): panel_raw = lax.all_gather(raw, 'pairs', axis=0, tiled=True)]
    convert_element_type x1 -> x2, other arithmetic: 0.02 us -> 19 us  [the longest x1 17.5 us: shards(): dense = jnp.zeros((owners * station_count, full_width), jnp.float32).at[e...]
    all_to_all x2 -> x0, starting transfers between devices: 14.2 us -> none  [the longest x1 9.13 us: shards(): lax.all_to_all(request.reshape(owners, capacity), 'pairs', split_axis=0,...]
    dot_general x1 -> x0, matrix products: 9.99 us -> none  [shards(): summed = jnp.dot(onehot, incoming, preferred_element_type=jnp.float32)]
  transfers between devices with their start and end apart: 3 -> 2, of which waited for: 2 -> 2; matrix products, arithmetic and copies ran while one was open for 31% -> 9% of each run, Pallas kernels for 4% -> 0%
where the time goes in v6:
time: 402 us; the launch traced here: 401 us
  waiting for transfers between devices  176 us (44%)
  other arithmetic  79.5 us (20%)
  local copies, waits for them, and re-layouts  68 us (17%)
  blocking collectives  46.5 us (12%)
  Pallas kernels  17.8 us (4%)
  between operations  13.5 us (3%)
    reduce_scatter x1, waiting for transfers between devices, shards(): lax.psum_scatter(dense, 'pairs', scatter_dimension=0, tiled=True)  143 us
    scatter-add x1, other arithmetic, shards(): dense = jnp.zeros((owners * station_count, full_width), jnp.float32).at[e...  48 us
    all_gather x1, waiting for transfers between devices, shards(): panel_raw = lax.all_gather(raw, 'pairs', axis=0, tiled=True)  32.2 us
    all_gather x1, blocking collectives, shards(): panel_scale = lax.all_gather(scale, 'pairs', axis=0, tiled=True)  29.2 us
    gather x1, local copies, waits for them, and re-layouts, shards(): far_raw = panel_raw[rows1]  19 us
    gather x1, local copies, waits for them, and re-layouts, shards(): near_raw = panel_raw[rows0]  18.9 us
    pallas_call x1, Pallas kernels, pair_contributions(): pl.pallas_call(pair_kernel, grid=(pairs // block,), in_specs=[pl.BlockSpe...  17.8 us
    convert_element_type x1, other arithmetic, shards(): dense = jnp.zeros((owners * station_count, full_width), jnp.float32).at[e...  17.5 us
  transfers between devices with their start and end apart: 2, of which 2 were waited for; matrix products, arithmetic and copies ran while one was open for 9% of the time, Pallas kernels for 0%

profile of v6, /device:TPU:1, one launch (start us, length us, event | category | flops | bytes accessed | tf_op | source)
XLA Modules:
  0.0 401.3 jit_solution(14678895962184887867)
XLA Ops:
  6.5 0.7 all-gather.4.cloned.1.call-update
  7.3 1.5 fusion.3
  8.8 17.4 %psum.7 = f32[512]{0:T(512)S(1)} all-reduce(f32[512]{0:T(512)S(1)} %fusion.3), channel_id=1, replica_groups=mesh['pairs'=16,'band'=8] {'band'}, use_global_device_ids=true, to_apply=%region_1.0 | all-reduce | flops 512 | bytes 4096 | tf_op jit(solution)/shard_map/psum | solution.py:98
  26.2 29.2 %all-gather.1 = f32[16,1,512]{2,1,0:T(1,128)S(1)} all-gather(f32[1,1,512]{2,1,0:T(1,128)S(1)} %bitcast.27), channel_id=1, replica_groups=mesh['pairs'=16,'band'=8] {'pairs'}, dimensions={0}, use_global_device_ids=true | all-gather | bytes 34816 | tf_op jit(solution)/shard_map/all_gather | solution.py:102
  55.4 11.8 %gather_fusion.2 = f32[2048]{0:T(1024)S(1)} fusion(f32[8192]{0:T(1024)S(1)} %bitcast.17, s32[2048]{0:T(1024)S(1)} %broadcast_clamp_fusion.1), kind=kCustom, calls=%fused_computation.2 | custom fusion | bytes 24576 | tf_op jit(solution)/shard_map/gather | solution.py:111
  67.2 0.4 copy.11.ns_ref
  67.6 11.8 %gather_fusion.3 = f32[2048]{0:T(1024)S(1)} fusion(f32[8192]{0:T(1024)S(1)} %bitcast.18, s32[2048]{0:T(1024)S(1)} %broadcast_clamp_fusion), kind=kCustom, calls=%fused_computation.3 | custom fusion | bytes 24576 | tf_op jit(solution)/shard_map/gather | solution.py:112
  79.4 0.4 copy.12.fs_ref
  79.8 0.4 copy.13.ws_ref
  80.2 1.3 copy.14.we_ref
  81.5 8.6 %multiply_convert_fusion = (bf16[512,1024]{1,0:T(8,128)(2,1)S(1)}, bf16[512,1024]{1,0:T(8,128)(2,1)S(1)}) fusion(), kind=kLoop, calls=%fused_computation.19 | loop fusion | flops 9961472 | bytes 2097152 | tf_op jit(solution)/shard_map/convert.2
  90.1 1.5 pad_maximum_fusion.table_ref
  91.6 32.2 %all-gather.4.cloned.1.call-done = bf16[8192,1,1024]{2,0,1:T(8,128)(2,1)} async-done(((bf16[512,1,1024]{2,0,1:T(8,128)(2,1)}), bf16[8192,1,1024]{2,0,1:T(8,128)(2,1)}) %all-gather.4.cloned.1.call-update) | async-done | bytes 16777232 | tf_op jit(solution)/shard_map/all_gather | solution.py:95
  123.9 18.9 %gather_fusion = bf16[2048,1024]{1,0:T(8,128)(2,1)} fusion(bf16[8192,1024]{1,0:T(8,128)(2,1)} %bitcast.19, s32[2048]{0:T(1024)S(1)} %broadcast_clamp_fusion.1), kind=kCustom, calls=%fused_computation | custom fusion | bytes 8396800 | tf_op jit(solution)/shard_map/gather | solution.py:109
  142.8 19.0 %gather_fusion.1 = bf16[2048,1024]{1,0:T(8,128)(2,1)} fusion(bf16[8192,1024]{1,0:T(8,128)(2,1)} %bitcast.20, s32[2048]{0:T(1024)S(1)} %broadcast_clamp_fusion), kind=kCustom, calls=%fused_computation.1 | custom fusion | bytes 8396800 | tf_op jit(solution)/shard_map/gather | solution.py:110
  161.7 1.2 copy-done
  162.9 17.8 %shard_map.64 = bf16[2,2048,1024]{2,1,0:T(8,128)(2,1)} custom-call(bf16[2048,1024]{1,0:T(8,128)(2,1)} %gather_fusion, bf16[2048,1024]{1,0:T(8,128)(2,1)} %gather_fusion.1, f32[2048,1]{1,0:T(8,128)S(1)} %copy.11.ns_ref, f32[2048,1]{1,0:T(8,128)S(1)} %copy.12.fs_ref, bf16[2048,1024]{1,0:T(8,128)(2,1)} %bitcast.22, s32[2048,1]{1,0:T(8,128)S(1)} %copy.13.ws_ref, ...), custom_call_target="tpu_custom_call" | custom-call | tf_op jit(solution)/shard_map/pallas_call | solution.py:66
  180.8 48.0 %scatter_custom_fusion = f32[8192,1024]{1,0:T(8,128)} fusion(s32[4096]{0:T(1024)S(1)} %bitcast.28, bf16[4096,1024]{1,0:T(8,128)(2,1)} %bitcast.21, f32[]{:T(128)} %constant.11.clone.1), kind=kCustom, calls=%fused_computation.5 | custom fusion | flops 8388608 | bytes 41943044 | tf_op jit(solution)/shard_map/scatter-add | solution.py:123
  228.8 17.5 %convert_element_type.25 = bf16[8192,1024]{1,0:T(8,128)(2,1)} convert(f32[8192,1024]{1,0:T(8,128)} %scatter_custom_fusion) | non-fusion elementwise | flops 8388608 | bytes 50331648 | tf_op jit(solution)/shard_map/convert_element_type | solution.py:124
  246.4 1.2 copy-done.1
  247.8 143.0 %reduce-scatter.2.cloned.1.call-done = bf16[512,1024]{1,0:T(8,128)(2,1)} async-done(((bf16[8192,1024]{1,0:T(8,128)(2,1)}), bf16[512,1024]{1,0:T(8,128)(2,1)}) %reduce-scatter.2.cloned.1.call-update) | async-done | bytes 1048592 | tf_op jit(solution)/shard_map/reduce_scatter | solution.py:125
  390.8 1.5 convert_element_type.26
  392.3 0.5 fusion.12
  392.8 1.7 reshape.80
  (19 shorter events, 0.4 us)
Async XLA Ops:
  6.5 48.8 %copy-start.3 = (s32[2048,2]{0,1:T(2,128)S(1)}, s32[2048,2]{0,1:T(2,128)}, u32[]{:S(2)}) copy-start(s32[2048,2]{0,1:T(2,128)} %param.8) | copy-start | bytes 49156
  6.5 48.8 %copy-start.2 = (s32[2048,2]{0,1:T(2,128)S(1)}, s32[2048,2]{0,1:T(2,128)}, u32[]{:S(2)}) copy-start(s32[2048,2]{0,1:T(2,128)} %param.9) | copy-start | bytes 49156
  6.5 117.3 %all-gather.4.cloned.1.call-start = ((), (), s32[]{:S(2)}) async-start(), calls=%async_computation.2 | async-start | bytes 17825792 | tf_op jit(solution)/shard_map/all_gather | solution.py:95
  7.3 383.5 %reduce-scatter.2.cloned.1.call-start = ((), (), s32[]{:S(2)}) async-start(), calls=%async_computation.1 | async-start | bytes 17825792 | tf_op jit(solution)/shard_map/reduce_scatter | solution.py:125
  67.6 12.2 %copy-start.4 = (s32[2048]{0:T(1024)S(1)}, s32[2048]{0:T(1024)}, u32[]{:S(2)}) copy-start(s32[2048]{0:T(1024)} %param.10) | copy-start | bytes 24580
  79.4 0.8 copy-start.5
  161.7 1.2 copy-start
  246.3 1.2 copy-start.1
Sparse Core Ops, SparseCore 0:
  9.8 114.0 all-gather.3
  246.5 144.2 reduce-scatter.1

commit v7 on v6

--- a/solution.py
+++ b/solution.py
@@ -101,9 +101,6 @@
     own_spec = lax.reduce_precision(spectrum * scale[:, None], exponent_bits=8, mantissa_bits=7)
     panel_scale = lax.all_gather(scale, "pairs", axis=0, tiled=True)
 
-    owner_flat = jnp.concatenate([pair_owner[:, 0], pair_owner[:, 1]])
-    slot_flat = jnp.concatenate([pair_slot[:, 0], pair_slot[:, 1]])
-    position = owner_positions(owner_flat, owners)
     rows0 = pair_owner[:, 0] * station_count + pair_slot[:, 0]
     rows1 = pair_owner[:, 1] * station_count + pair_slot[:, 1]
     near_raw = panel_raw[rows0]
@@ -118,10 +115,10 @@
     ).reshape(2 * pair_count, full_width)
     endpoint_rows = jnp.concatenate([rows0, rows1])
     dense = (
-        jnp.zeros((owners * station_count, full_width), jnp.float32)
+        jnp.zeros((owners * station_count, full_width), jnp.bfloat16)
         .at[endpoint_rows]
-        .add(contribs.astype(jnp.float32))
-    ).astype(jnp.bfloat16)
+        .add(contribs)
+    )
     summed = lax.psum_scatter(dense, "pairs", scatter_dimension=0, tiled=True).astype(
         jnp.float32
     )

time: 402 us -> 381 us (0.948)
  other arithmetic: 79.5 us -> 58.2 us
    convert_element_type x1 -> x0, other arithmetic: 17.5 us -> none  [shards(): dense = jnp.zeros((owners * station_count, full_width), jnp.float32).at[e...]
  transfers between devices with their start and end apart: 2 -> 2, of which waited for: 2 -> 2; matrix products, arithmetic and copies ran while one was open for 9% -> 10% of each run, Pallas kernels for 0% -> 0%
where the time goes in v7:
time: 381 us; the launch traced here: 380 us
  waiting for transfers between devices  176 us (46%)
  local copies, waits for them, and re-layouts  68 us (18%)
  other arithmetic  58.2 us (15%)
  blocking collectives  46.5 us (12%)
  Pallas kernels  17.9 us (5%)
  between operations  13.5 us (4%)
    reduce_scatter x1, waiting for transfers between devices, shards(): lax.psum_scatter(dense, 'pairs', scatter_dimension=0, tiled=True)  143 us
    scatter-add x1, other arithmetic, shards(): dense = jnp.zeros((owners * station_count, full_width), jnp.bfloat16).at[...  44.3 us
    all_gather x1, waiting for transfers between devices, shards(): panel_raw = lax.all_gather(raw, 'pairs', axis=0, tiled=True)  32.3 us
    all_gather x1, blocking collectives, shards(): panel_scale = lax.all_gather(scale, 'pairs', axis=0, tiled=True)  29.2 us
    gather x1, local copies, waits for them, and re-layouts, shards(): near_raw = panel_raw[rows0]  18.9 us
    gather x1, local copies, waits for them, and re-layouts, shards(): far_raw = panel_raw[rows1]  18.9 us
    pallas_call x1, Pallas kernels, pair_contributions(): pl.pallas_call(pair_kernel, grid=(pairs // block,), in_specs=[pl.BlockSpe...  17.9 us
    psum x1, blocking collectives, shards(): total_power = lax.psum(local_power, 'band')  17.4 us
  transfers between devices with their start and end apart: 2, of which 2 were waited for; matrix products, arithmetic and copies ran while one was open for 10% of the time, Pallas kernels for 0%

profile of v7, /device:TPU:1, one launch (start us, length us, event | category | flops | bytes accessed | tf_op | source)
XLA Modules:
  0.0 380.1 jit_solution(15724967439706290556)
XLA Ops:
  6.5 0.7 all-gather.4.cloned.1.call-update
  7.3 1.5 fusion.2
  8.8 17.4 %psum.7 = f32[512]{0:T(512)S(1)} all-reduce(f32[512]{0:T(512)S(1)} %fusion.2), channel_id=1, replica_groups=mesh['pairs'=16,'band'=8] {'band'}, use_global_device_ids=true, to_apply=%region_1.0 | all-reduce | flops 512 | bytes 4096 | tf_op jit(solution)/shard_map/psum | solution.py:98
  26.2 29.2 %all-gather.1 = f32[16,1,512]{2,1,0:T(1,128)S(1)} all-gather(f32[1,1,512]{2,1,0:T(1,128)S(1)} %bitcast.26), channel_id=1, replica_groups=mesh['pairs'=16,'band'=8] {'pairs'}, dimensions={0}, use_global_device_ids=true | all-gather | bytes 34816 | tf_op jit(solution)/shard_map/all_gather | solution.py:102
  55.4 11.8 %gather_fusion.2 = f32[2048]{0:T(1024)S(1)} fusion(f32[8192]{0:T(1024)S(1)} %bitcast.16, s32[2048]{0:T(1024)S(1)} %broadcast_clamp_fusion.1), kind=kCustom, calls=%fused_computation.2 | custom fusion | bytes 24576 | tf_op jit(solution)/shard_map/gather | solution.py:108
  67.2 0.4 copy.11.ns_ref
  67.6 11.8 %gather_fusion.3 = f32[2048]{0:T(1024)S(1)} fusion(f32[8192]{0:T(1024)S(1)} %bitcast.17, s32[2048]{0:T(1024)S(1)} %broadcast_clamp_fusion), kind=kCustom, calls=%fused_computation.3 | custom fusion | bytes 24576 | tf_op jit(solution)/shard_map/gather | solution.py:109
  79.4 0.4 copy.12.fs_ref
  79.8 0.4 copy.13.ws_ref
  80.2 1.3 copy.14.we_ref
  81.5 8.6 %multiply_convert_fusion = (bf16[512,1024]{1,0:T(8,128)(2,1)S(1)}, bf16[512,1024]{1,0:T(8,128)(2,1)S(1)}) fusion(), kind=kLoop, calls=%fused_computation.18 | loop fusion | flops 9961472 | bytes 2097152 | tf_op jit(solution)/shard_map/convert.1
  90.1 1.5 pad_maximum_fusion.table_ref
  91.6 32.3 %all-gather.4.cloned.1.call-done = bf16[8192,1,1024]{2,0,1:T(8,128)(2,1)} async-done(((bf16[512,1,1024]{2,0,1:T(8,128)(2,1)}), bf16[8192,1,1024]{2,0,1:T(8,128)(2,1)}) %all-gather.4.cloned.1.call-update) | async-done | bytes 16777232 | tf_op jit(solution)/shard_map/all_gather | solution.py:95
  123.9 18.9 %gather_fusion = bf16[2048,1024]{1,0:T(8,128)(2,1)} fusion(bf16[8192,1024]{1,0:T(8,128)(2,1)} %bitcast.18, s32[2048]{0:T(1024)S(1)} %broadcast_clamp_fusion.1), kind=kCustom, calls=%fused_computation | custom fusion | bytes 8396800 | tf_op jit(solution)/shard_map/gather | solution.py:106
  142.8 18.9 %gather_fusion.1 = bf16[2048,1024]{1,0:T(8,128)(2,1)} fusion(bf16[8192,1024]{1,0:T(8,128)(2,1)} %bitcast.19, s32[2048]{0:T(1024)S(1)} %broadcast_clamp_fusion), kind=kCustom, calls=%fused_computation.1 | custom fusion | bytes 8396800 | tf_op jit(solution)/shard_map/gather | solution.py:107
  161.7 1.2 copy-done
  162.9 17.9 %shard_map.64 = bf16[2,2048,1024]{2,1,0:T(8,128)(2,1)} custom-call(bf16[2048,1024]{1,0:T(8,128)(2,1)} %gather_fusion, bf16[2048,1024]{1,0:T(8,128)(2,1)} %gather_fusion.1, f32[2048,1]{1,0:T(8,128)S(1)} %copy.11.ns_ref, f32[2048,1]{1,0:T(8,128)S(1)} %copy.12.fs_ref, bf16[2048,1024]{1,0:T(8,128)(2,1)} %bitcast.21, s32[2048,1]{1,0:T(8,128)S(1)} %copy.13.ws_ref, ...), custom_call_target="tpu_custom_call" | custom-call | tf_op jit(solution)/shard_map/pallas_call | solution.py:66
  180.8 44.3 %scatter_custom_fusion = bf16[8192,1024]{1,0:T(8,128)(2,1)} fusion(s32[4096]{0:T(1024)S(1)} %bitcast.27, bf16[4096,1024]{1,0:T(8,128)(2,1)} %bitcast.20, bf16[]{:T(256)} %constant.12.clone.1), kind=kCustom, calls=%fused_computation.5 | custom fusion | flops 4194304 | bytes 16777728 | tf_op jit(solution)/shard_map/scatter-add | solution.py:120
  225.2 1.2 copy-done.1
  226.4 0.3 fusion.3
  226.6 143.0 %reduce-scatter.2.cloned.1.call-done = bf16[512,1024]{1,0:T(8,128)(2,1)} async-done(((bf16[8192,1024]{1,0:T(8,128)(2,1)}), bf16[512,1024]{1,0:T(8,128)(2,1)}) %reduce-scatter.2.cloned.1.call-update) | async-done | bytes 1048592 | tf_op jit(solution)/shard_map/reduce_scatter | solution.py:122
  369.6 1.5 convert_element_type.14
  371.1 0.5 fusion.11
  371.6 1.7 reshape.81
  (18 shorter events, 0.2 us)
Async XLA Ops:
  6.5 48.8 %copy-start.3 = (s32[2048,2]{0,1:T(2,128)S(1)}, s32[2048,2]{0,1:T(2,128)}, u32[]{:S(2)}) copy-start(s32[2048,2]{0,1:T(2,128)} %param.8) | copy-start | bytes 49156
  6.5 48.8 %copy-start.2 = (s32[2048,2]{0,1:T(2,128)S(1)}, s32[2048,2]{0,1:T(2,128)}, u32[]{:S(2)}) copy-start(s32[2048,2]{0,1:T(2,128)} %param.9) | copy-start | bytes 49156
  6.5 117.3 %all-gather.4.cloned.1.call-start = ((), (), s32[]{:S(2)}) async-start(), calls=%async_computation.2 | async-start | bytes 17825792 | tf_op jit(solution)/shard_map/all_gather | solution.py:95
  7.3 362.4 %reduce-scatter.2.cloned.1.call-start = ((), (), s32[]{:S(2)}) async-start(), calls=%async_computation.1 | async-start | bytes 17825792 | tf_op jit(solution)/shard_map/reduce_scatter | solution.py:122
  67.6 12.2 %copy-start.4 = (s32[2048]{0:T(1024)S(1)}, s32[2048]{0:T(1024)}, u32[]{:S(2)}) copy-start(s32[2048]{0:T(1024)} %param.10) | copy-start | bytes 24580
  79.4 0.8 copy-start.5
  161.7 1.2 copy-start
  225.1 1.2 copy-start.1
Sparse Core Ops, SparseCore 0:
  9.8 114.0 all-gather.3
  225.3 144.2 reduce-scatter.1

commit v8 on v7

--- a/solution.py
+++ b/solution.py
@@ -113,12 +113,25 @@
         near_raw, far_raw, near_scale, far_scale, obs,
         win_start[:, None], win_end[:, None], table,
     ).reshape(2 * pair_count, full_width)
-    endpoint_rows = jnp.concatenate([rows0, rows1])
-    dense = (
-        jnp.zeros((owners * station_count, full_width), jnp.bfloat16)
-        .at[endpoint_rows]
-        .add(contribs)
-    )
+    owner_flat = jnp.concatenate([pair_owner[:, 0], pair_owner[:, 1]])
+    slot_flat = jnp.concatenate([pair_slot[:, 0], pair_slot[:, 1]])
+    position = owner_positions(owner_flat, owners)
+    flat_slot = owner_flat * capacity + position
+    slot_station = (
+        jnp.full((owners * capacity,), station_count, jnp.int32)
+        .at[flat_slot]
+        .set(slot_flat, unique_indices=True)
+    ).reshape(owners, 1, capacity)
+    slotted = (
+        jnp.zeros((owners * capacity, full_width), jnp.bfloat16)
+        .at[flat_slot]
+        .set(contribs, unique_indices=True)
+    ).reshape(owners, capacity, full_width)
+    station_ids = jnp.arange(station_count, dtype=jnp.int32)[None, :, None]
+    onehot = (slot_station == station_ids).astype(jnp.bfloat16)
+    dense = jnp.einsum(
+        "osk,okf->osf", onehot, slotted, preferred_element_type=jnp.float32
+    ).astype(jnp.bfloat16).reshape(owners * station_count, full_width)
     summed = lax.psum_scatter(dense, "pairs", scatter_dimension=0, tiled=True).astype(
         jnp.float32
     )

time: 381 us -> 380 us (level)
  local copies, waits for them, and re-layouts: 68 us -> 111 us
  other arithmetic: 58.2 us -> 19.9 us
  waiting for transfers between devices: 176 us -> 153 us
  matrix products: 0 us -> 16.8 us
    scatter-add x1 -> x0, other arithmetic: 44.3 us -> none  [shards(): dense = jnp.zeros((owners * station_count, full_width), jnp.bfloat16).at[...]
    scatter x0 -> x2, local copies, waits for them, and re-layouts: none -> 42.4 us  [the longest x1 26.7 us: shards(): slotted = jnp.zeros((owners * capacity, full_width), jnp.bfloat16).at[fla...]
    all_gather x1, waiting for transfers between devices: 32.3 us -> 9.96 us  [shards(): panel_raw = lax.all_gather(raw, 'pairs', axis=0, tiled=True)]
    dot_general x0 -> x1, matrix products: none -> 16.8 us  [shards(): jnp.einsum('osk,okf->osf', onehot, slotted, preferred_element_type=jnp.fl...]
    another operation x1 -> x4, other arithmetic: 8.55 us -> 13.5 us
  transfers between devices with their start and end apart: 2 -> 2, of which waited for: 2 -> 2; matrix products, arithmetic and copies ran while one was open for 10% -> 16% of each run, Pallas kernels for 0% -> 0%
where the time goes in v8:
time: 380 us; the launch traced here: 379 us
  waiting for transfers between devices  153 us (40%)
  local copies, waits for them, and re-layouts  111 us (29%)
  blocking collectives  46.9 us (12%)
  other arithmetic  19.9 us (5%)
  Pallas kernels  17.8 us (5%)
  matrix products  16.8 us (4%)
  between operations  13.6 us (4%)
    reduce_scatter x1, waiting for transfers between devices, shards(): lax.psum_scatter(dense, 'pairs', scatter_dimension=0, tiled=True)  143 us
    all_gather x1, blocking collectives, shards(): panel_scale = lax.all_gather(scale, 'pairs', axis=0, tiled=True)  28.9 us
    scatter x1, local copies, waits for them, and re-layouts, shards(): slotted = jnp.zeros((owners * capacity, full_width), jnp.bfloat16).at[fla...  26.7 us
    gather x1, local copies, waits for them, and re-layouts, shards(): near_raw = panel_raw[rows0]  18.9 us
    gather x1, local copies, waits for them, and re-layouts, shards(): far_raw = panel_raw[rows1]  18.9 us
    psum x1, blocking collectives, shards(): total_power = lax.psum(local_power, 'band')  18 us
    pallas_call x1, Pallas kernels, pair_contributions(): pl.pallas_call(pair_kernel, grid=(pairs // block,), in_specs=[pl.BlockSpe...  17.8 us
    dot_general x1, matrix products, shards(): jnp.einsum('osk,okf->osf', onehot, slotted, preferred_element_type=jnp.fl...  16.8 us
  transfers between devices with their start and end apart: 2, of which 2 were waited for; matrix products, arithmetic and copies ran while one was open for 16% of the time, Pallas kernels for 0%

profile of v8, /device:TPU:1, one launch (start us, length us, event | category | flops | bytes accessed | tf_op | source)
XLA Modules:
  0.0 379.0 jit_solution(326682592131729378)
XLA Ops:
  6.5 0.7 all-gather.4.cloned.1.call-update
  7.3 0.8 compare_select_fusion.1
  8.2 4.6 %reduce-window.6 = s32[16,32,128]{2,1,0:T(8,128)S(1)} reduce-window(s32[16,32,128]{2,1,0:T(8,128)S(1)} %fusion.18, s32[]{:T(128)} %constant.16.clone.1), window={size=1x1x128 pad=0_0x0_0x127_0}, to_apply=%region_0.0 | reduce-window | flops 8323072 | bytes 524292 | tf_op jit(solution)/shard_map/reduce-window
  13.5 1.5 fusion.5
  15.0 18.0 %psum.7 = f32[512]{0:T(512)S(1)} all-reduce(f32[512]{0:T(512)S(1)} %fusion.5), channel_id=1, replica_groups=mesh['pairs'=16,'band'=8] {'band'}, use_global_device_ids=true, to_apply=%region_5.6 | all-reduce | flops 512 | bytes 4096 | tf_op jit(solution)/shard_map/psum | solution.py:98
  33.0 28.9 %all-gather.1 = f32[16,1,512]{2,1,0:T(1,128)S(1)} all-gather(f32[1,1,512]{2,1,0:T(1,128)S(1)} %bitcast.65), channel_id=1, replica_groups=mesh['pairs'=16,'band'=8] {'pairs'}, dimensions={0}, use_global_device_ids=true | all-gather | bytes 34816 | tf_op jit(solution)/shard_map/all_gather | solution.py:102
  61.8 11.8 %gather_fusion.2 = f32[2048]{0:T(1024)S(1)} fusion(f32[8192]{0:T(1024)S(1)} %bitcast.44, s32[2048]{0:T(1024)S(1)} %broadcast_clamp_fusion.1), kind=kCustom, calls=%fused_computation.2 | custom fusion | bytes 24576 | tf_op jit(solution)/shard_map/gather | solution.py:108
  74.0 11.8 %gather_fusion.3 = f32[2048]{0:T(1024)S(1)} fusion(f32[8192]{0:T(1024)S(1)} %bitcast.45, s32[2048]{0:T(1024)S(1)} %broadcast_clamp_fusion), kind=kCustom, calls=%fused_computation.3 | custom fusion | bytes 24576 | tf_op jit(solution)/shard_map/gather | solution.py:109
  86.6 1.3 copy.14.we_ref
  88.3 15.7 %scatter_custom_fusion = s32[6144]{0:T(1024)S(1)} fusion(s32[4096]{0:T(1024)S(1)} %bitcast.66, s32[4096]{0:T(1024)S(1)} %pad_add_fusion.2, s32[]{:T(128)} %constant.14.clone.1), kind=kCustom, calls=%fused_computation.49 | custom fusion | bytes 24580 | tf_op jit(solution)/shard_map/scatter | solution.py:123
  104.1 8.6 %multiply_convert_fusion = (bf16[512,1024]{1,0:T(8,128)(2,1)S(1)}, bf16[512,1024]{1,0:T(8,128)(2,1)S(1)}) fusion(), kind=kLoop, calls=%fused_computation.23 | loop fusion | flops 9961472 | bytes 2097152 | tf_op jit(solution)/shard_map/convert.1
  112.6 1.6 pad_maximum_fusion.table_ref
  114.2 10.0 %all-gather.4.cloned.1.call-done = bf16[8192,1,1024]{2,0,1:T(8,128)(2,1)} async-done(((bf16[512,1,1024]{2,0,1:T(8,128)(2,1)}), bf16[8192,1,1024]{2,0,1:T(8,128)(2,1)}) %all-gather.4.cloned.1.call-update) | async-done | bytes 16777232 | tf_op jit(solution)/shard_map/all_gather | solution.py:95
  124.2 18.9 %gather_fusion = bf16[2048,1024]{1,0:T(8,128)(2,1)} fusion(bf16[8192,1024]{1,0:T(8,128)(2,1)} %bitcast.46, s32[2048]{0:T(1024)S(1)} %broadcast_clamp_fusion.1), kind=kCustom, calls=%fused_computation | custom fusion | bytes 8396800 | tf_op jit(solution)/shard_map/gather | solution.py:106
  143.1 18.9 %gather_fusion.1 = bf16[2048,1024]{1,0:T(8,128)(2,1)} fusion(bf16[8192,1024]{1,0:T(8,128)(2,1)} %bitcast.47, s32[2048]{0:T(1024)S(1)} %broadcast_clamp_fusion), kind=kCustom, calls=%fused_computation.1 | custom fusion | bytes 8396800 | tf_op jit(solution)/shard_map/gather | solution.py:107
  162.0 1.2 copy-done
  163.2 17.8 %shard_map.64 = bf16[2,2048,1024]{2,1,0:T(8,128)(2,1)} custom-call(bf16[2048,1024]{1,0:T(8,128)(2,1)} %gather_fusion, bf16[2048,1024]{1,0:T(8,128)(2,1)} %gather_fusion.1, f32[2048,1]{1,0:T(8,128)S(1)} %copy.11.ns_ref, f32[2048,1]{1,0:T(8,128)S(1)} %copy.12.fs_ref, bf16[2048,1024]{1,0:T(8,128)(2,1)} %bitcast.51, s32[2048,1]{1,0:T(8,128)S(1)} %copy.13.ws_ref, ...), custom_call_target="tpu_custom_call" | custom-call | tf_op jit(solution)/shard_map/pallas_call | solution.py:66
  181.0 26.7 %scatter_custom_fusion.1 = bf16[6144,1024]{1,0:T(8,128)(2,1)} fusion(s32[4096]{0:T(1024)S(1)} %bitcast.67, bf16[4096,1024]{1,0:T(8,128)(2,1)} %bitcast.50, bf16[]{:T(256)} %constant.18.clone.1), kind=kCustom, calls=%fused_computation.9 | custom fusion | bytes 12583424 | tf_op jit(solution)/shard_map/scatter | solution.py:128
  207.7 16.8 %fusion.1 = bf16[16,512,1024]{2,1,0:T(8,128)(2,1)} fusion(bf16[16,384,1024]{2,1,0:T(8,128)(2,1)} %bitcast.49, s32[16,384]{1,0:T(8,128)S(1)} %eq.44), kind=kOutput, calls=%fused_computation.8 | convolution fusion | flops 6453985280 | bytes 29384704 | tf_op jit(solution)/shard_map/osk,okf->osf/dot_general | solution.py:132
  224.6 1.2 copy-done.1
  226.0 142.5 %reduce-scatter.2.cloned.1.call-done = bf16[512,1024]{1,0:T(8,128)(2,1)} async-done(((bf16[8192,1024]{1,0:T(8,128)(2,1)}), bf16[512,1024]{1,0:T(8,128)(2,1)}) %reduce-scatter.2.cloned.1.call-update) | async-done | bytes 1048592 | tf_op jit(solution)/shard_map/reduce_scatter | solution.py:135
  368.6 1.5 convert_element_type.28
  370.0 0.5 fusion.14
  370.5 1.7 reshape.88
  (26 shorter events, 2.5 us)
Async XLA Ops:
  6.5 117.6 %all-gather.4.cloned.1.call-start = ((), (), s32[]{:S(2)}) async-start(), calls=%async_computation.2 | async-start | bytes 17825792 | tf_op jit(solution)/shard_map/all_gather | solution.py:95
  7.3 361.3 %reduce-scatter.2.cloned.1.call-start = ((), (), s32[]{:S(2)}) async-start(), calls=%async_computation.1 | async-start | bytes 17825792 | tf_op jit(solution)/shard_map/reduce_scatter | solution.py:135
  74.0 12.2 %copy-start.2 = (s32[2048]{0:T(1024)S(1)}, s32[2048]{0:T(1024)}, u32[]{:S(2)}) copy-start(s32[2048]{0:T(1024)} %param.10) | copy-start | bytes 24580
  74.0 12.6 %copy-start.3 = (s32[2048]{0:T(1024)S(1)}, s32[2048]{0:T(1024)}, u32[]{:S(2)}) copy-start(s32[2048]{0:T(1024)} %param.11) | copy-start | bytes 24580
  162.0 1.2 copy-start
  224.5 1.2 copy-start.1
Sparse Core Ops, SparseCore 0:
  9.8 114.3 all-gather.3
  224.7 143.8 reduce-scatter.1

commit v9 on v8

--- a/solution.py
+++ b/solution.py
@@ -127,14 +127,16 @@
         .at[flat_slot]
         .set(contribs, unique_indices=True)
     ).reshape(owners, capacity, full_width)
-    station_ids = jnp.arange(station_count, dtype=jnp.int32)[None, :, None]
-    onehot = (slot_station == station_ids).astype(jnp.bfloat16)
-    dense = jnp.einsum(
-        "osk,okf->osf", onehot, slotted, preferred_element_type=jnp.float32
-    ).astype(jnp.bfloat16).reshape(owners * station_count, full_width)
-    summed = lax.psum_scatter(dense, "pairs", scatter_dimension=0, tiled=True).astype(
-        jnp.float32
-    )
+    part = station_count // 2
+    summed = []
+    for half in range(2):
+        station_ids = half * part + jnp.arange(part, dtype=jnp.int32)[None, :, None]
+        onehot = (slot_station == station_ids).astype(jnp.bfloat16)
+        dense = jnp.einsum(
+            "osk,okf->osf", onehot, slotted, preferred_element_type=jnp.float32
+        ).astype(jnp.bfloat16).reshape(owners * part, full_width)
+        summed.append(lax.psum_scatter(dense, "pairs", scatter_dimension=0, tiled=True))
+    summed = jnp.concatenate(summed, axis=0).astype(jnp.float32)
     result = 0.25 * (
         summed[:, :half_width] * own_spec[:, :half_width]
         + summed[:, half_width:] * own_spec[:, half_width:]

time: 380 us -> 434 us (1.14)
  waiting for transfers between devices: 153 us -> 203 us
  matrix products: 16.8 us -> 23 us
    reduce_scatter x1 -> x2, waiting for transfers between devices: 143 us -> 191 us  [shards(): lax.psum_scatter(dense, 'pairs', scatter_dimension=0, tiled=True)]
    dot_general x1 -> x2, matrix products: 16.8 us -> 23 us  [shards(): jnp.einsum('osk,okf->osf', onehot, slotted, preferred_element_type=jnp.fl...]
  transfers between devices with their start and end apart: 2 -> 3, of which waited for: 2 -> 3; matrix products, arithmetic and copies ran while one was open for 16% -> 16% of each run, Pallas kernels for 0% -> 0%
where the time goes in v9:
time: 434 us
  waiting for transfers between devices  203 us (47%)
  local copies, waits for them, and re-layouts  111 us (26%)
  blocking collectives  46.8 us (11%)
  matrix products  23 us (5%)
  other arithmetic  18.7 us (4%)
  Pallas kernels  17.8 us (4%)
  between operations  13.3 us (3%)
    reduce_scatter x2, waiting for transfers between devices, shards(): lax.psum_scatter(dense, 'pairs', scatter_dimension=0, tiled=True)  191 us
    all_gather x1, blocking collectives, shards(): panel_scale = lax.all_gather(scale, 'pairs', axis=0, tiled=True)  29 us
    scatter x1, local copies, waits for them, and re-layouts, shards(): slotted = jnp.zeros((owners * capacity, full_width), jnp.bfloat16).at[fla...  26.6 us
    dot_general x2, matrix products, shards(): jnp.einsum('osk,okf->osf', onehot, slotted, preferred_element_type=jnp.fl...  23 us
    gather x1, local copies, waits for them, and re-layouts, shards(): near_raw = panel_raw[rows0]  18.9 us
    gather x1, local copies, waits for them, and re-layouts, shards(): far_raw = panel_raw[rows1]  18.9 us
    psum x1, blocking collectives, shards(): total_power = lax.psum(local_power, 'band')  17.9 us
    pallas_call x1, Pallas kernels, pair_contributions(): pl.pallas_call(pair_kernel, grid=(pairs // block,), in_specs=[pl.BlockSpe...  17.8 us
  transfers between devices with their start and end apart: 3, of which 3 were waited for; matrix products, arithmetic and copies ran while one was open for 16% of the time, Pallas kernels for 0%

profile of v9, /device:TPU:1, one launch (start us, length us, event | category | flops | bytes accessed | tf_op | source)
XLA Modules:
  0.0 433.5 jit_solution(13963079579422772040)
XLA Ops:
  6.5 0.7 all-gather.4.cloned.1.call-update
  7.3 0.8 compare_select_fusion.1
  8.2 4.6 %reduce-window.6 = s32[16,32,128]{2,1,0:T(8,128)S(1)} reduce-window(s32[16,32,128]{2,1,0:T(8,128)S(1)} %fusion.19, s32[]{:T(128)} %constant.17.clone.1), window={size=1x1x128 pad=0_0x0_0x127_0}, to_apply=%region_0.0 | reduce-window | flops 8323072 | bytes 524292 | tf_op jit(solution)/shard_map/reduce-window
  13.8 17.9 %psum.7 = f32[512]{0:T(512)S(1)} all-reduce(f32[512]{0:T(512)S(1)} %fusion.6), channel_id=1, replica_groups=mesh['pairs'=16,'band'=8] {'band'}, use_global_device_ids=true, to_apply=%region_5.6 | all-reduce | flops 512 | bytes 4096 | tf_op jit(solution)/shard_map/psum | solution.py:98
  31.7 29.0 %all-gather.1 = f32[16,1,512]{2,1,0:T(1,128)S(1)} all-gather(f32[1,1,512]{2,1,0:T(1,128)S(1)} %bitcast.69), channel_id=1, replica_groups=mesh['pairs'=16,'band'=8] {'pairs'}, dimensions={0}, use_global_device_ids=true | all-gather | bytes 34816 | tf_op jit(solution)/shard_map/all_gather | solution.py:102
  60.6 11.8 %gather_fusion.2 = f32[2048]{0:T(1024)S(1)} fusion(f32[8192]{0:T(1024)S(1)} %bitcast.46, s32[2048]{0:T(1024)S(1)} %broadcast_clamp_fusion.1), kind=kCustom, calls=%fused_computation.2 | custom fusion | bytes 24576 | tf_op jit(solution)/shard_map/gather | solution.py:108
  72.8 11.8 %gather_fusion.3 = f32[2048]{0:T(1024)S(1)} fusion(f32[8192]{0:T(1024)S(1)} %bitcast.47, s32[2048]{0:T(1024)S(1)} %broadcast_clamp_fusion), kind=kCustom, calls=%fused_computation.3 | custom fusion | bytes 24576 | tf_op jit(solution)/shard_map/gather | solution.py:109
  85.4 1.3 copy.14.we_ref
  87.1 15.7 %scatter_custom_fusion = s32[6144]{0:T(1024)S(1)} fusion(s32[4096]{0:T(1024)S(1)} %bitcast.70, s32[4096]{0:T(1024)S(1)} %pad_add_fusion.2, s32[]{:T(128)} %constant.15.clone.1), kind=kCustom, calls=%fused_computation.53 | custom fusion | bytes 24580 | tf_op jit(solution)/shard_map/scatter | solution.py:123
  102.8 8.6 %multiply_convert_fusion = (bf16[512,1024]{1,0:T(8,128)(2,1)S(1)}, bf16[512,1024]{1,0:T(8,128)(2,1)S(1)}) fusion(), kind=kLoop, calls=%fused_computation.26 | loop fusion | flops 9961472 | bytes 2097152 | tf_op jit(solution)/shard_map/convert.1
  111.4 1.6 pad_maximum_fusion.table_ref
  113.0 11.1 %all-gather.4.cloned.1.call-done = bf16[8192,1,1024]{2,0,1:T(8,128)(2,1)} async-done(((bf16[512,1,1024]{2,0,1:T(8,128)(2,1)}), bf16[8192,1,1024]{2,0,1:T(8,128)(2,1)}) %all-gather.4.cloned.1.call-update) | async-done | bytes 16777232 | tf_op jit(solution)/shard_map/all_gather | solution.py:95
  124.1 18.9 %gather_fusion = bf16[2048,1024]{1,0:T(8,128)(2,1)} fusion(bf16[8192,1024]{1,0:T(8,128)(2,1)} %bitcast.48, s32[2048]{0:T(1024)S(1)} %broadcast_clamp_fusion.1), kind=kCustom, calls=%fused_computation | custom fusion | bytes 8396800 | tf_op jit(solution)/shard_map/gather | solution.py:106
  143.0 18.9 %gather_fusion.1 = bf16[2048,1024]{1,0:T(8,128)(2,1)} fusion(bf16[8192,1024]{1,0:T(8,128)(2,1)} %bitcast.49, s32[2048]{0:T(1024)S(1)} %broadcast_clamp_fusion), kind=kCustom, calls=%fused_computation.1 | custom fusion | bytes 8396800 | tf_op jit(solution)/shard_map/gather | solution.py:107
  161.9 1.2 copy-done
  163.1 17.8 %shard_map.64 = bf16[2,2048,1024]{2,1,0:T(8,128)(2,1)} custom-call(bf16[2048,1024]{1,0:T(8,128)(2,1)} %gather_fusion, bf16[2048,1024]{1,0:T(8,128)(2,1)} %gather_fusion.1, f32[2048,1]{1,0:T(8,128)S(1)} %copy.11.ns_ref, f32[2048,1]{1,0:T(8,128)S(1)} %copy.12.fs_ref, bf16[2048,1024]{1,0:T(8,128)(2,1)} %bitcast.55, s32[2048,1]{1,0:T(8,128)S(1)} %copy.13.ws_ref, ...), custom_call_target="tpu_custom_call" | custom-call | tf_op jit(solution)/shard_map/pallas_call | solution.py:66
  180.9 26.6 %scatter_custom_fusion.1 = bf16[6144,1024]{1,0:T(8,128)(2,1)} fusion(s32[4096]{0:T(1024)S(1)} %bitcast.71, bf16[4096,1024]{1,0:T(8,128)(2,1)} %bitcast.54, bf16[]{:T(256)} %constant.19.clone.1), kind=kCustom, calls=%fused_computation.8 | custom fusion | bytes 12583424 | tf_op jit(solution)/shard_map/scatter | solution.py:128
  207.6 11.3 %convolution_convert_fusion.1 = bf16[16,256,1024]{2,1,0:T(8,128)(2,1)} fusion(bf16[16,384,1024]{2,1,0:T(8,128)(2,1)} %bitcast.50, s32[16,384]{1,0:T(8,128)S(1)} %eq.55), kind=kOutput, calls=%fused_computation.7 | convolution fusion | flops 3226992640 | bytes 20996096 | tf_op jit(solution)/shard_map/osk,okf->osf/dot_general | solution.py:135
  219.0 11.7 %convolution_convert_fusion = bf16[16,256,1024]{2,1,0:T(8,128)(2,1)} fusion(bf16[16,384,1024]{2,1,0:T(8,128)(2,1)} %bitcast.51, s32[16,384]{1,0:T(8,128)S(1)} %eq.55, s32[256]{0:T(256)S(1)} %iota_add_fusion), kind=kOutput, calls=%fused_computation.6 | convolution fusion | flops 3226992640 | bytes 20997120 | tf_op jit(solution)/shard_map/osk,okf->osf/dot_general | solution.py:135
  230.7 1.3 copy-done.2
  232.2 85.5 %reduce-scatter.3.cloned.1.call-done = bf16[256,1024]{1,0:T(8,128)(2,1)} async-done(((bf16[4096,1024]{1,0:T(8,128)(2,1)}), bf16[256,1024]{1,0:T(8,128)(2,1)}) %reduce-scatter.3.cloned.1.call-update) | async-done | bytes 524304 | tf_op jit(solution)/shard_map/reduce_scatter | solution.py:138
  317.7 105.6 %reduce-scatter.5.cloned.1.call-done = bf16[256,1024]{1,0:T(8,128)(2,1)} async-done(((bf16[4096,1024]{1,0:T(8,128)(2,1)}), bf16[256,1024]{1,0:T(8,128)(2,1)}) %reduce-scatter.5.cloned.1.call-update) | async-done | bytes 524304 | tf_op jit(solution)/shard_map/reduce_scatter | solution.py:138
  423.3 1.4 maximum_convert_fusion
  425.3 1.7 reshape.97
  (33 shorter events, 3.3 us)
Async XLA Ops:
  6.5 6.9 %copy-start.1 = (bf16[512,1,1024]{2,0,1:T(8,128)(2,1)S(1)}, bf16[512,1,1024]{2,0,1:T(8,128)(2,1)}, u32[]{:S(2)}) copy-start(bf16[512,1,1024]{2,0,1:T(8,128)(2,1)} %param.6) | copy-start | bytes 3145732
  6.5 117.5 %all-gather.4.cloned.1.call-start = ((), (), s32[]{:S(2)}) async-start(), calls=%async_computation.4 | async-start | bytes 17825792 | tf_op jit(solution)/shard_map/all_gather | solution.py:95
  7.3 310.5 %reduce-scatter.3.cloned.1.call-start = ((), (), s32[]{:S(2)}) async-start(), calls=%async_computation.2 | async-start | bytes 8912896 | tf_op jit(solution)/shard_map/reduce_scatter | solution.py:138
  72.8 12.2 %copy-start.3 = (s32[2048]{0:T(1024)S(1)}, s32[2048]{0:T(1024)}, u32[]{:S(2)}) copy-start(s32[2048]{0:T(1024)} %param.10) | copy-start | bytes 24580
  84.6 0.8 copy-start.4
  161.9 1.2 copy-start
  218.9 204.4 %reduce-scatter.5.cloned.1.call-start = ((), (), s32[]{:S(2)}) async-start(), calls=%async_computation.3 | async-start | bytes 8912896 | tf_op jit(solution)/shard_map/reduce_scatter | solution.py:138
  230.6 1.3 copy-start.2
Sparse Core Ops, SparseCore 0:
  9.8 114.2 all-gather.3
  219.0 98.6 reduce-scatter.2
  322.1 101.2 reduce-scatter.4

commit v10 on v8

--- a/solution.py
+++ b/solution.py
@@ -59,7 +59,7 @@
     out_ref[1, :, half:] = (adj_re * near_im - adj_im * near_re).astype(jnp.bfloat16)
 
 
-def pair_contributions(near_raw, far_raw, near_scale, far_scale, obs, ws, we, table, block=256):
+def pair_contributions(near_raw, far_raw, near_scale, far_scale, obs, ws, we, table, block=512):
     pairs, width = near_raw.shape
     lags = obs.shape[1]
     row = lambda i: (i, 0)

time: 380 us -> 379 us (level)
  no operation moved by 1% of the time
where the time goes in v10:
time: 379 us
  waiting for transfers between devices  153 us (40%)
  local copies, waits for them, and re-layouts  111 us (29%)
  blocking collectives  46.9 us (12%)
  other arithmetic  19.9 us (5%)
  Pallas kernels  17.7 us (5%)
  matrix products  16.8 us (4%)
  between operations  13.6 us (4%)
    reduce_scatter x1, waiting for transfers between devices, shards(): lax.psum_scatter(dense, 'pairs', scatter_dimension=0, tiled=True)  143 us
    all_gather x1, blocking collectives, shards(): panel_scale = lax.all_gather(scale, 'pairs', axis=0, tiled=True)  28.9 us
    scatter x1, local copies, waits for them, and re-layouts, shards(): slotted = jnp.zeros((owners * capacity, full_width), jnp.bfloat16).at[fla...  26.7 us
    gather x1, local copies, waits for them, and re-layouts, shards(): near_raw = panel_raw[rows0]  18.9 us
    gather x1, local copies, waits for them, and re-layouts, shards(): far_raw = panel_raw[rows1]  18.9 us
    psum x1, blocking collectives, shards(): total_power = lax.psum(local_power, 'band')  18 us
    pallas_call x1, Pallas kernels, pair_contributions(): pl.pallas_call(pair_kernel, grid=(pairs // block,), in_specs=[pl.BlockSpe...  17.7 us
    dot_general x1, matrix products, shards(): jnp.einsum('osk,okf->osf', onehot, slotted, preferred_element_type=jnp.fl...  16.8 us
  transfers between devices with their start and end apart: 2, of which 2 were waited for; matrix products, arithmetic and copies ran while one was open for 16% of the time, Pallas kernels for 0%

profile of v10, /device:TPU:1, one launch (start us, length us, event | category | flops | bytes accessed | tf_op | source)
XLA Modules:
  0.0 379.0 jit_solution(3441462951831126729)
XLA Ops:
  6.5 0.7 all-gather.4.cloned.1.call-update
  7.3 0.8 compare_select_fusion.1
  8.2 4.6 %reduce-window.6 = s32[16,32,128]{2,1,0:T(8,128)S(1)} reduce-window(s32[16,32,128]{2,1,0:T(8,128)S(1)} %fusion.18, s32[]{:T(128)} %constant.16.clone.1), window={size=1x1x128 pad=0_0x0_0x127_0}, to_apply=%region_0.0 | reduce-window | flops 8323072 | bytes 524292 | tf_op jit(solution)/shard_map/reduce-window
  13.5 1.5 fusion.5
  15.0 18.0 %psum.7 = f32[512]{0:T(512)S(1)} all-reduce(f32[512]{0:T(512)S(1)} %fusion.5), channel_id=1, replica_groups=mesh['pairs'=16,'band'=8] {'band'}, use_global_device_ids=true, to_apply=%region_5.6 | all-reduce | flops 512 | bytes 4096 | tf_op jit(solution)/shard_map/psum | solution.py:98
  33.0 28.9 %all-gather.1 = f32[16,1,512]{2,1,0:T(1,128)S(1)} all-gather(f32[1,1,512]{2,1,0:T(1,128)S(1)} %bitcast.65), channel_id=1, replica_groups=mesh['pairs'=16,'band'=8] {'pairs'}, dimensions={0}, use_global_device_ids=true | all-gather | bytes 34816 | tf_op jit(solution)/shard_map/all_gather | solution.py:102
  61.8 11.8 %gather_fusion.2 = f32[2048]{0:T(1024)S(1)} fusion(f32[8192]{0:T(1024)S(1)} %bitcast.44, s32[2048]{0:T(1024)S(1)} %broadcast_clamp_fusion.1), kind=kCustom, calls=%fused_computation.2 | custom fusion | bytes 24576 | tf_op jit(solution)/shard_map/gather | solution.py:108
  74.0 11.8 %gather_fusion.3 = f32[2048]{0:T(1024)S(1)} fusion(f32[8192]{0:T(1024)S(1)} %bitcast.45, s32[2048]{0:T(1024)S(1)} %broadcast_clamp_fusion), kind=kCustom, calls=%fused_computation.3 | custom fusion | bytes 24576 | tf_op jit(solution)/shard_map/gather | solution.py:109
  86.6 1.3 copy.14.we_ref
  88.3 15.7 %scatter_custom_fusion = s32[6144]{0:T(1024)S(1)} fusion(s32[4096]{0:T(1024)S(1)} %bitcast.66, s32[4096]{0:T(1024)S(1)} %pad_add_fusion.2, s32[]{:T(128)} %constant.14.clone.1), kind=kCustom, calls=%fused_computation.49 | custom fusion | bytes 24580 | tf_op jit(solution)/shard_map/scatter | solution.py:123
  104.1 8.6 %multiply_convert_fusion = (bf16[512,1024]{1,0:T(8,128)(2,1)S(1)}, bf16[512,1024]{1,0:T(8,128)(2,1)S(1)}) fusion(), kind=kLoop, calls=%fused_computation.23 | loop fusion | flops 9961472 | bytes 2097152 | tf_op jit(solution)/shard_map/convert.1
  112.6 1.6 pad_maximum_fusion.table_ref
  114.2 10.0 %all-gather.4.cloned.1.call-done = bf16[8192,1,1024]{2,0,1:T(8,128)(2,1)} async-done(((bf16[512,1,1024]{2,0,1:T(8,128)(2,1)}), bf16[8192,1,1024]{2,0,1:T(8,128)(2,1)}) %all-gather.4.cloned.1.call-update) | async-done | bytes 16777232 | tf_op jit(solution)/shard_map/all_gather | solution.py:95
  124.2 18.9 %gather_fusion = bf16[2048,1024]{1,0:T(8,128)(2,1)} fusion(bf16[8192,1024]{1,0:T(8,128)(2,1)} %bitcast.46, s32[2048]{0:T(1024)S(1)} %broadcast_clamp_fusion.1), kind=kCustom, calls=%fused_computation | custom fusion | bytes 8396800 | tf_op jit(solution)/shard_map/gather | solution.py:106
  143.1 18.9 %gather_fusion.1 = bf16[2048,1024]{1,0:T(8,128)(2,1)} fusion(bf16[8192,1024]{1,0:T(8,128)(2,1)} %bitcast.47, s32[2048]{0:T(1024)S(1)} %broadcast_clamp_fusion), kind=kCustom, calls=%fused_computation.1 | custom fusion | bytes 8396800 | tf_op jit(solution)/shard_map/gather | solution.py:107
  162.0 1.2 copy-done
  163.2 17.7 %shard_map.64 = bf16[2,2048,1024]{2,1,0:T(8,128)(2,1)} custom-call(bf16[2048,1024]{1,0:T(8,128)(2,1)} %gather_fusion, bf16[2048,1024]{1,0:T(8,128)(2,1)} %gather_fusion.1, f32[2048,1]{1,0:T(8,128)S(1)} %copy.11.ns_ref, f32[2048,1]{1,0:T(8,128)S(1)} %copy.12.fs_ref, bf16[2048,1024]{1,0:T(8,128)(2,1)} %bitcast.51, s32[2048,1]{1,0:T(8,128)S(1)} %copy.13.ws_ref, ...), custom_call_target="tpu_custom_call" | custom-call | tf_op jit(solution)/shard_map/pallas_call | solution.py:66
  180.9 26.7 %scatter_custom_fusion.1 = bf16[6144,1024]{1,0:T(8,128)(2,1)} fusion(s32[4096]{0:T(1024)S(1)} %bitcast.67, bf16[4096,1024]{1,0:T(8,128)(2,1)} %bitcast.50, bf16[]{:T(256)} %constant.18.clone.1), kind=kCustom, calls=%fused_computation.9 | custom fusion | bytes 12583424 | tf_op jit(solution)/shard_map/scatter | solution.py:128
  207.6 16.8 %fusion.1 = bf16[16,512,1024]{2,1,0:T(8,128)(2,1)} fusion(bf16[16,384,1024]{2,1,0:T(8,128)(2,1)} %bitcast.49, s32[16,384]{1,0:T(8,128)S(1)} %eq.44), kind=kOutput, calls=%fused_computation.8 | convolution fusion | flops 6453985280 | bytes 29384704 | tf_op jit(solution)/shard_map/osk,okf->osf/dot_general | solution.py:132
  224.4 1.2 copy-done.1
  225.9 142.6 %reduce-scatter.2.cloned.1.call-done = bf16[512,1024]{1,0:T(8,128)(2,1)} async-done(((bf16[8192,1024]{1,0:T(8,128)(2,1)}), bf16[512,1024]{1,0:T(8,128)(2,1)}) %reduce-scatter.2.cloned.1.call-update) | async-done | bytes 1048592 | tf_op jit(solution)/shard_map/reduce_scatter | solution.py:135
  368.5 1.5 convert_element_type.28
  370.0 0.5 fusion.14
  370.5 1.7 reshape.88
  (26 shorter events, 2.5 us)
Async XLA Ops:
  6.5 117.6 %all-gather.4.cloned.1.call-start = ((), (), s32[]{:S(2)}) async-start(), calls=%async_computation.2 | async-start | bytes 17825792 | tf_op jit(solution)/shard_map/all_gather | solution.py:95
  7.3 361.2 %reduce-scatter.2.cloned.1.call-start = ((), (), s32[]{:S(2)}) async-start(), calls=%async_computation.1 | async-start | bytes 17825792 | tf_op jit(solution)/shard_map/reduce_scatter | solution.py:135
  74.0 12.2 %copy-start.2 = (s32[2048]{0:T(1024)S(1)}, s32[2048]{0:T(1024)}, u32[]{:S(2)}) copy-start(s32[2048]{0:T(1024)} %param.10) | copy-start | bytes 24580
  74.0 12.6 %copy-start.3 = (s32[2048]{0:T(1024)S(1)}, s32[2048]{0:T(1024)}, u32[]{:S(2)}) copy-start(s32[2048]{0:T(1024)} %param.11) | copy-start | bytes 24580
  162.0 1.2 copy-start
  224.4 1.2 copy-start.1
Sparse Core Ops, SparseCore 0:
  9.8 114.3 all-gather.3
  224.5 143.9 reduce-scatter.1

commit v11 on v10

--- a/solution.py
+++ b/solution.py
@@ -82,6 +82,22 @@
     )(near_raw, far_raw, near_scale, far_scale, obs, ws, we, table)
 
 
+def finish_kernel(summed_ref, own_ref, out_ref):
+    half = own_ref.shape[1] // 2
+    summed = summed_ref[...].astype(jnp.float32)
+    own = own_ref[...]
+    value = 0.25 * (summed[:, :half] * own[:, :half] + summed[:, half:] * own[:, half:])
+    out_ref[...] = value.reshape(out_ref.shape)
+
+
+def finish(summed, own_spec, band_count):
+    stations, width = own_spec.shape
+    return pl.pallas_call(
+        finish_kernel,
+        out_shape=jax.ShapeDtypeStruct((stations, band_count, width // 2), jnp.float32),
+    )(summed, own_spec)
+
+
 def shards(spectra, observed, pair_owner, pair_slot, win_start, win_end):
     owners = lax.axis_size("pairs")
     station_count = spectra.shape[0]
@@ -132,14 +148,8 @@
     dense = jnp.einsum(
         "osk,okf->osf", onehot, slotted, preferred_element_type=jnp.float32
     ).astype(jnp.bfloat16).reshape(owners * station_count, full_width)
-    summed = lax.psum_scatter(dense, "pairs", scatter_dimension=0, tiled=True).astype(
-        jnp.float32
-    )
-    result = 0.25 * (
-        summed[:, :half_width] * own_spec[:, :half_width]
-        + summed[:, half_width:] * own_spec[:, half_width:]
-    )
-    return result.reshape(station_count, band_count, half_width)
+    summed = lax.psum_scatter(dense, "pairs", scatter_dimension=0, tiled=True)
+    return finish(summed, own_spec, band_count)
 
 
 def solution(mesh):

time: 379 us -> 379 us (level)
  no operation moved by 1% of the time
where the time goes in v11:
time: 379 us
  waiting for transfers between devices  152 us (40%)
  local copies, waits for them, and re-layouts  109 us (29%)
  blocking collectives  46.9 us (12%)
  Pallas kernels  20.9 us (6%)
  other arithmetic  19.3 us (5%)
  matrix products  16.8 us (4%)
  between operations  13.6 us (4%)
    reduce_scatter x1, waiting for transfers between devices, shards(): summed = lax.psum_scatter(dense, 'pairs', scatter_dimension=0, tiled=True)  141 us
    all_gather x1, blocking collectives, shards(): panel_scale = lax.all_gather(scale, 'pairs', axis=0, tiled=True)  28.9 us
    scatter x1, local copies, waits for them, and re-layouts, shards(): slotted = jnp.zeros((owners * capacity, full_width), jnp.bfloat16).at[fla...  26.7 us
    gather x1, local copies, waits for them, and re-layouts, shards(): near_raw = panel_raw[rows0]  18.9 us
    gather x1, local copies, waits for them, and re-layouts, shards(): far_raw = panel_raw[rows1]  18.9 us
    psum x1, blocking collectives, shards(): total_power = lax.psum(local_power, 'band')  18 us
    pallas_call x1, Pallas kernels, pair_contributions(): pl.pallas_call(pair_kernel, grid=(pairs // block,), in_specs=[pl.BlockSpe...  17.7 us
    dot_general x1, matrix products, shards(): jnp.einsum('osk,okf->osf', onehot, slotted, preferred_element_type=jnp.fl...  16.8 us
  transfers between devices with their start and end apart: 2, of which 2 were waited for; matrix products, arithmetic and copies ran while one was open for 16% of the time, Pallas kernels for 0%

profile of v11, /device:TPU:1, one launch (start us, length us, event | category | flops | bytes accessed | tf_op | source)
XLA Modules:
  0.0 378.6 jit_solution(1595006953951187095)
XLA Ops:
  6.5 0.7 all-gather.4.cloned.1.call-update
  7.3 0.8 compare_select_fusion.1
  8.2 4.6 %reduce-window.6 = s32[16,32,128]{2,1,0:T(8,128)S(1)} reduce-window(s32[16,32,128]{2,1,0:T(8,128)S(1)} %fusion.16, s32[]{:T(128)} %constant.15.clone.1), window={size=1x1x128 pad=0_0x0_0x127_0}, to_apply=%region_0.0 | reduce-window | flops 8323072 | bytes 524292 | tf_op jit(solution)/shard_map/reduce-window
  12.8 0.5 slice_reduce_fusion
  13.5 1.5 fusion.5
  15.0 18.0 %psum.7 = f32[512]{0:T(512)S(1)} all-reduce(f32[512]{0:T(512)S(1)} %fusion.5), channel_id=1, replica_groups=mesh['pairs'=16,'band'=8] {'band'}, use_global_device_ids=true, to_apply=%region_5.6 | all-reduce | flops 512 | bytes 4096 | tf_op jit(solution)/shard_map/psum | solution.py:114
  33.0 28.9 %all-gather.1 = f32[16,1,512]{2,1,0:T(1,128)S(1)} all-gather(f32[1,1,512]{2,1,0:T(1,128)S(1)} %bitcast.65), channel_id=1, replica_groups=mesh['pairs'=16,'band'=8] {'pairs'}, dimensions={0}, use_global_device_ids=true | all-gather | bytes 34816 | tf_op jit(solution)/shard_map/all_gather | solution.py:118
  61.8 11.8 %gather_fusion.2 = f32[2048]{0:T(1024)S(1)} fusion(f32[8192]{0:T(1024)S(1)} %bitcast.44, s32[2048]{0:T(1024)S(1)} %broadcast_clamp_fusion.1), kind=kCustom, calls=%fused_computation.2 | custom fusion | bytes 24576 | tf_op jit(solution)/shard_map/gather | solution.py:124
  74.0 11.8 %gather_fusion.3 = f32[2048]{0:T(1024)S(1)} fusion(f32[8192]{0:T(1024)S(1)} %bitcast.45, s32[2048]{0:T(1024)S(1)} %broadcast_clamp_fusion), kind=kCustom, calls=%fused_computation.3 | custom fusion | bytes 24576 | tf_op jit(solution)/shard_map/gather | solution.py:125
  86.6 1.3 copy.14.we_ref
  88.3 15.7 %scatter_custom_fusion = s32[6144]{0:T(1024)S(1)} fusion(s32[4096]{0:T(1024)S(1)} %bitcast.66, s32[4096]{0:T(1024)S(1)} %pad_add_fusion.2, s32[]{:T(128)} %constant.13.clone.1), kind=kCustom, calls=%fused_computation.45 | custom fusion | bytes 24580 | tf_op jit(solution)/shard_map/scatter | solution.py:139
  104.1 8.6 %multiply_convert_fusion = (bf16[512,1024]{1,0:T(8,128)(2,1)S(1)}, bf16[512,1024]{1,0:T(8,128)(2,1)S(1)}) fusion(), kind=kLoop, calls=%fused_computation.23 | loop fusion | flops 9961472 | bytes 2097152 | tf_op jit(solution)/shard_map/convert.1
  112.6 1.6 pad_maximum_fusion.table_ref
  114.2 10.0 %all-gather.4.cloned.1.call-done = bf16[8192,1,1024]{2,0,1:T(8,128)(2,1)} async-done(((bf16[512,1,1024]{2,0,1:T(8,128)(2,1)}), bf16[8192,1,1024]{2,0,1:T(8,128)(2,1)}) %all-gather.4.cloned.1.call-update) | async-done | bytes 16777232 | tf_op jit(solution)/shard_map/all_gather | solution.py:111
  124.2 18.9 %gather_fusion = bf16[2048,1024]{1,0:T(8,128)(2,1)} fusion(bf16[8192,1024]{1,0:T(8,128)(2,1)} %bitcast.46, s32[2048]{0:T(1024)S(1)} %broadcast_clamp_fusion.1), kind=kCustom, calls=%fused_computation | custom fusion | bytes 8396800 | tf_op jit(solution)/shard_map/gather | solution.py:122
  143.1 18.9 %gather_fusion.1 = bf16[2048,1024]{1,0:T(8,128)(2,1)} fusion(bf16[8192,1024]{1,0:T(8,128)(2,1)} %bitcast.47, s32[2048]{0:T(1024)S(1)} %broadcast_clamp_fusion), kind=kCustom, calls=%fused_computation.1 | custom fusion | bytes 8396800 | tf_op jit(solution)/shard_map/gather | solution.py:123
  162.0 1.2 copy-done
  163.2 17.7 %shard_map.64 = bf16[2,2048,1024]{2,1,0:T(8,128)(2,1)} custom-call(bf16[2048,1024]{1,0:T(8,128)(2,1)} %gather_fusion, bf16[2048,1024]{1,0:T(8,128)(2,1)} %gather_fusion.1, f32[2048,1]{1,0:T(8,128)S(1)} %copy.11.ns_ref, f32[2048,1]{1,0:T(8,128)S(1)} %copy.12.fs_ref, bf16[2048,1024]{1,0:T(8,128)(2,1)} %bitcast.51, s32[2048,1]{1,0:T(8,128)S(1)} %copy.13.ws_ref, ...), custom_call_target="tpu_custom_call" | custom-call | tf_op jit(solution)/shard_map/pallas_call | solution.py:66
  180.9 26.7 %scatter_custom_fusion.1 = bf16[6144,1024]{1,0:T(8,128)(2,1)} fusion(s32[4096]{0:T(1024)S(1)} %bitcast.67, bf16[4096,1024]{1,0:T(8,128)(2,1)} %bitcast.50, bf16[]{:T(256)} %constant.17.clone.1), kind=kCustom, calls=%fused_computation.9 | custom fusion | bytes 12583424 | tf_op jit(solution)/shard_map/scatter | solution.py:144
  207.6 16.8 %fusion.1 = bf16[16,512,1024]{2,1,0:T(8,128)(2,1)} fusion(bf16[16,384,1024]{2,1,0:T(8,128)(2,1)} %bitcast.49, s32[16,384]{1,0:T(8,128)S(1)} %eq.44), kind=kOutput, calls=%fused_computation.8 | convolution fusion | flops 6453985280 | bytes 29384704 | tf_op jit(solution)/shard_map/osk,okf->osf/dot_general | solution.py:148
  224.4 1.2 copy-done.1
  225.6 1.6 fusion.6.own_ref
  227.2 141.3 %reduce-scatter.2.cloned.1.call-done.summed_ref = bf16[512,1024]{1,0:T(8,128)(2,1)} async-done(((bf16[8192,1024]{1,0:T(8,128)(2,1)}), bf16[512,1024]{1,0:T(8,128)(2,1)}) %reduce-scatter.2.cloned.1.call-update) | async-done | bytes 1048592 | tf_op jit(solution)/shard_map/reduce_scatter | solution.py:151
  368.5 3.3 shard_map.65
  (24 shorter events, 1.8 us)
Async XLA Ops:
  6.5 117.6 %all-gather.4.cloned.1.call-start = ((), (), s32[]{:S(2)}) async-start(), calls=%async_computation.2 | async-start | bytes 17825792 | tf_op jit(solution)/shard_map/all_gather | solution.py:111
  7.3 361.2 %reduce-scatter.2.cloned.1.call-start = ((), (), s32[]{:S(2)}) async-start(), calls=%async_computation.1 | async-start | bytes 17825792 | tf_op jit(solution)/shard_map/reduce_scatter | solution.py:151
  74.0 12.2 %copy-start.2 = (s32[2048]{0:T(1024)S(1)}, s32[2048]{0:T(1024)}, u32[]{:S(2)}) copy-start(s32[2048]{0:T(1024)} %param.10) | copy-start | bytes 24580
  74.0 12.6 %copy-start.3 = (s32[2048]{0:T(1024)S(1)}, s32[2048]{0:T(1024)}, u32[]{:S(2)}) copy-start(s32[2048]{0:T(1024)} %param.11) | copy-start | bytes 24580
  162.0 1.2 copy-start
  224.4 1.2 copy-start.1
Sparse Core Ops, SparseCore 0:
  9.8 114.3 all-gather.3
  224.5 143.9 reduce-scatter.1

commit v12 on v11

--- a/solution.py
+++ b/solution.py
@@ -99,7 +99,7 @@
 
 
 def shards(spectra, observed, pair_owner, pair_slot, win_start, win_end):
-    owners = lax.axis_size("pairs")
+    owners = lax.axis_size(("z_hi", "x", "core"))
     station_count = spectra.shape[0]
     band_count = spectra.shape[1]
     full_width = spectra.shape[2]
@@ -108,14 +108,14 @@
     lag_count = observed.shape[2]
     capacity = 3 * pair_count // owners
     raw = spectra.reshape(station_count, full_width)
-    panel_raw = lax.all_gather(raw, "pairs", axis=0, tiled=True)
+    panel_raw = lax.all_gather(raw, ("z_hi", "x", "core"), axis=0, tiled=True)
     spectrum = raw.astype(jnp.float32)
     local_power = jnp.sum(spectrum * spectrum, axis=1)
-    total_power = lax.psum(local_power, "band")
-    entries = band_count * lax.axis_size("band") * full_width
+    total_power = lax.psum(local_power, ("y", "z_lo"))
+    entries = band_count * lax.axis_size(("y", "z_lo")) * full_width
     scale = lax.rsqrt(total_power / entries + 1e-05)
     own_spec = lax.reduce_precision(spectrum * scale[:, None], exponent_bits=8, mantissa_bits=7)
-    panel_scale = lax.all_gather(scale, "pairs", axis=0, tiled=True)
+    panel_scale = lax.all_gather(scale, ("z_hi", "x", "core"), axis=0, tiled=True)
 
     rows0 = pair_owner[:, 0] * station_count + pair_slot[:, 0]
     rows1 = pair_owner[:, 1] * station_count + pair_slot[:, 1]
@@ -148,22 +148,38 @@
     dense = jnp.einsum(
         "osk,okf->osf", onehot, slotted, preferred_element_type=jnp.float32
     ).astype(jnp.bfloat16).reshape(owners * station_count, full_width)
-    summed = lax.psum_scatter(dense, "pairs", scatter_dimension=0, tiled=True)
+    core = lax.axis_index("core")
+    by_core = dense.reshape(owners // 2, 2, station_count, full_width)
+    keep = lax.dynamic_index_in_dim(by_core, core, axis=1, keepdims=False)
+    give = lax.dynamic_index_in_dim(by_core, 1 - core, axis=1, keepdims=False)
+    taken = lax.ppermute(give, "core", perm=[(0, 1), (1, 0)])
+    chip_sum = (keep.astype(jnp.float32) + taken.astype(jnp.float32)).astype(jnp.bfloat16)
+    summed = lax.psum_scatter(
+        chip_sum.reshape(owners // 2 * station_count, full_width),
+        ("z_hi", "x"),
+        scatter_dimension=0,
+        tiled=True,
+    )
     return finish(summed, own_spec, band_count)
 
 
 def solution(mesh):
+    fine = jax.sharding.Mesh(
+        mesh.devices.reshape(2, 4, 2, 4, 2), ("z_hi", "x", "core", "y", "z_lo")
+    )
+    pairs = ("z_hi", "x", "core")
+    band = ("y", "z_lo")
     return jax.shard_map(
         shards,
-        mesh=mesh,
+        mesh=fine,
         in_specs=(
-            P("pairs", "band", None),
-            P("pairs", "band", None),
-            P("pairs", None),
-            P("pairs", None),
-            P("pairs"),
-            P("pairs"),
+            P(pairs, band, None),
+            P(pairs, band, None),
+            P(pairs, None),
+            P(pairs, None),
+            P(pairs),
+            P(pairs),
         ),
-        out_specs=P("pairs", "band", None),
+        out_specs=P(pairs, band, None),
         check_vma=False,
     )

time: 379 us -> 378 us (level)
  waiting for transfers between devices: 152 us -> 132 us
  other arithmetic: 19.3 us -> 30 us
  local copies, waits for them, and re-layouts: 109 us -> 117 us
    reduce_scatter x1, waiting for transfers between devices: 141 us -> 109 us  [shards(): lax.psum_scatter(chip_sum.reshape(owners // 2 * station_count, full_width...]
    ppermute x0 -> x1, waiting for transfers between devices: none -> 13.3 us  [shards(): taken = lax.ppermute(give, 'core', perm=[(0, 1), (1, 0)])]
    convert_element_type x0 -> x1, other arithmetic: none -> 10.7 us  [shards(): (keep.astype(jnp.float32) + taken.astype(jnp.float32)).astype(jnp.bfloat16)]
    squeeze x0 -> x1, local copies, waits for them, and re-layouts: none -> 7.58 us  [shards(): give = lax.dynamic_index_in_dim(by_core, 1 - core, axis=1, keepdims=False)]
  transfers between devices with their start and end apart: 2 -> 3, of which waited for: 2 -> 3; matrix products, arithmetic and copies ran while one was open for 16% -> 16% of each run, Pallas kernels for 0% -> 0%
where the time goes in v12:
time: 378 us
  waiting for transfers between devices  132 us (35%)
  local copies, waits for them, and re-layouts  117 us (31%)
  blocking collectives  46.9 us (12%)
  other arithmetic  30 us (8%)
  Pallas kernels  20.9 us (6%)
  matrix products  16.8 us (4%)
  between operations  13.6 us (4%)
    reduce_scatter x1, waiting for transfers between devices, shards(): lax.psum_scatter(chip_sum.reshape(owners // 2 * station_count, full_width...  109 us
    all_gather x1, blocking collectives, shards(): lax.all_gather(scale, ('z_hi', 'x', 'core'), axis=0, tiled=True)  28.9 us
    scatter x1, local copies, waits for them, and re-layouts, shards(): slotted = jnp.zeros((owners * capacity, full_width), jnp.bfloat16).at[fla...  26.7 us
    gather x1, local copies, waits for them, and re-layouts, shards(): near_raw = panel_raw[rows0]  18.9 us
    gather x1, local copies, waits for them, and re-layouts, shards(): far_raw = panel_raw[rows1]  18.9 us
    psum x1, blocking collectives, shards(): total_power = lax.psum(local_power, ('y', 'z_lo'))  18 us
    pallas_call x1, Pallas kernels, pair_contributions(): pl.pallas_call(pair_kernel, grid=(pairs // block,), in_specs=[pl.BlockSpe...  17.7 us
    dot_general x1, matrix products, shards(): jnp.einsum('osk,okf->osf', onehot, slotted, preferred_element_type=jnp.fl...  16.8 us
  transfers between devices with their start and end apart: 3, of which 3 were waited for; matrix products, arithmetic and copies ran while one was open for 16% of the time, Pallas kernels for 0%

profile of v12, /device:TPU:1, one launch (start us, length us, event | category | flops | bytes accessed | tf_op | source)
XLA Modules:
  0.0 377.6 jit_solution(12701903919768911807)
XLA Ops:
  8.2 4.6 %reduce-window.6 = s32[16,32,128]{2,1,0:T(8,128)S(1)} reduce-window(s32[16,32,128]{2,1,0:T(8,128)S(1)} %fusion.17, s32[]{:T(128)} %constant.24.clone.1), window={size=1x1x128 pad=0_0x0_0x127_0}, to_apply=%region_0.0 | reduce-window | flops 8323072 | bytes 524292 | tf_op jit(solution)/shard_map/reduce-window
  13.5 1.5 fusion.6
  15.0 18.0 %psum.7 = f32[512]{0:T(512)S(1)} all-reduce(f32[512]{0:T(512)S(1)} %fusion.6), channel_id=1, replica_groups=mesh['z_hi'=2,'x'=4,'core'=2,'y'=4,'z_lo'=2] {'y','z_lo'}, use_global_device_ids=true, to_apply=%region_5.6 | all-reduce | flops 512 | bytes 4096 | tf_op jit(solution)/shard_map/psum | solution.py:114
  33.0 28.9 %all-gather.1 = f32[16,1,512]{2,1,0:T(1,128)S(1)} all-gather(f32[1,1,512]{2,1,0:T(1,128)S(1)} %bitcast.75), channel_id=1, replica_groups=mesh['z_hi'=2,'x'=4,'core'=2,'y'=4,'z_lo'=2] {'z_hi','x','core'}, dimensions={0}, use_global_device_ids=true | all-gather | bytes 34816 | tf_op jit(solution)/shard_map/all_gather | solution.py:118
  61.8 11.8 %gather_fusion.2 = f32[2048]{0:T(1024)S(1)} fusion(f32[8192]{0:T(1024)S(1)} %bitcast.52, s32[2048]{0:T(1024)S(1)} %broadcast_clamp_fusion.1), kind=kCustom, calls=%fused_computation.2 | custom fusion | bytes 24576 | tf_op jit(solution)/shard_map/gather | solution.py:124
  74.0 11.8 %gather_fusion.3 = f32[2048]{0:T(1024)S(1)} fusion(f32[8192]{0:T(1024)S(1)} %bitcast.53, s32[2048]{0:T(1024)S(1)} %broadcast_clamp_fusion), kind=kCustom, calls=%fused_computation.3 | custom fusion | bytes 24576 | tf_op jit(solution)/shard_map/gather | solution.py:125
  86.6 1.3 copy.16.we_ref
  88.3 15.7 %scatter_custom_fusion = s32[6144]{0:T(1024)S(1)} fusion(s32[4096]{0:T(1024)S(1)} %bitcast.76, s32[4096]{0:T(1024)S(1)} %pad_add_fusion.2, s32[]{:T(128)} %constant.19.clone.1), kind=kCustom, calls=%fused_computation.48 | custom fusion | bytes 24580 | tf_op jit(solution)/shard_map/scatter | solution.py:139
  104.1 8.6 %multiply_convert_fusion = (bf16[512,1024]{1,0:T(8,128)(2,1)S(1)}, bf16[512,1024]{1,0:T(8,128)(2,1)S(1)}) fusion(), kind=kLoop, calls=%fused_computation.26 | loop fusion | flops 9961472 | bytes 2097152 | tf_op jit(solution)/shard_map/convert.2
  112.6 1.6 pad_maximum_fusion.table_ref
  114.2 9.8 %all-gather.4.cloned.1.call-done = bf16[8192,1,1024]{2,0,1:T(8,128)(2,1)} async-done(((bf16[512,1,1024]{2,0,1:T(8,128)(2,1)}), bf16[8192,1,1024]{2,0,1:T(8,128)(2,1)}) %all-gather.4.cloned.1.call-update) | async-done | bytes 16777232 | tf_op jit(solution)/shard_map/all_gather | solution.py:111
  124.0 18.9 %gather_fusion = bf16[2048,1024]{1,0:T(8,128)(2,1)} fusion(bf16[8192,1024]{1,0:T(8,128)(2,1)} %bitcast.54, s32[2048]{0:T(1024)S(1)} %broadcast_clamp_fusion.1), kind=kCustom, calls=%fused_computation | custom fusion | bytes 8396800 | tf_op jit(solution)/shard_map/gather | solution.py:122
  142.9 18.9 %gather_fusion.1 = bf16[2048,1024]{1,0:T(8,128)(2,1)} fusion(bf16[8192,1024]{1,0:T(8,128)(2,1)} %bitcast.55, s32[2048]{0:T(1024)S(1)} %broadcast_clamp_fusion), kind=kCustom, calls=%fused_computation.1 | custom fusion | bytes 8396800 | tf_op jit(solution)/shard_map/gather | solution.py:123
  161.8 1.2 copy-done
  163.1 17.7 %shard_map.64 = bf16[2,2048,1024]{2,1,0:T(8,128)(2,1)} custom-call(bf16[2048,1024]{1,0:T(8,128)(2,1)} %gather_fusion, bf16[2048,1024]{1,0:T(8,128)(2,1)} %gather_fusion.1, f32[2048,1]{1,0:T(8,128)S(1)} %copy.13.ns_ref, f32[2048,1]{1,0:T(8,128)S(1)} %copy.14.fs_ref, bf16[2048,1024]{1,0:T(8,128)(2,1)} %bitcast.61, s32[2048,1]{1,0:T(8,128)S(1)} %copy.15.ws_ref, ...), custom_call_target="tpu_custom_call" | custom-call | tf_op jit(solution)/shard_map/pallas_call | solution.py:66
  180.7 26.7 %scatter_custom_fusion.1 = bf16[6144,1024]{1,0:T(8,128)(2,1)} fusion(s32[4096]{0:T(1024)S(1)} %bitcast.77, bf16[4096,1024]{1,0:T(8,128)(2,1)} %bitcast.60, bf16[]{:T(256)} %constant.27.clone.1), kind=kCustom, calls=%fused_computation.12 | custom fusion | bytes 12583424 | tf_op jit(solution)/shard_map/scatter | solution.py:144
  207.4 16.8 %fusion.2 = bf16[16,512,1024]{2,1,0:T(8,128)(2,1)} fusion(bf16[16,384,1024]{2,1,0:T(8,128)(2,1)} %bitcast.59, s32[16,384]{1,0:T(8,128)S(1)} %eq.44), kind=kOutput, calls=%fused_computation.10 | convolution fusion | flops 6453985280 | bytes 29384704 | tf_op jit(solution)/shard_map/osk,okf->osf/dot_general | solution.py:148
  224.2 7.6 %dynamic-slice_bitcast_fusion = bf16[8,512,1024]{2,1,0:T(8,128)(2,1)} fusion(bf16[8,2,512,1024]{3,2,1,0:T(8,128)(2,1)} %bitcast.57, s32[]{:T(128)S(6)} %select_n.42), kind=kLoop, calls=%fused_computation.11 | loop fusion | bytes 16777220 | tf_op jit(solution)/shard_map/jit(dynamic_index_in_dim)/squeeze | solution.py:154
  232.1 13.3 %collective-permute-done = bf16[8,512,1024]{2,1,0:T(8,128)(2,1)} collective-permute-done((bf16[8,512,1024]{2,1,0:T(8,128)(2,1)}, bf16[8,512,1024]{2,1,0:T(8,128)(2,1)}, u32[]{:S(2)}, u32[]{:S(2)}) %collective-permute-start) | collective-permute-done | bytes 8388640 | tf_op jit(solution)/shard_map/ppermute | solution.py:155
  245.3 10.7 %fusion = bf16[8,512,1024]{2,1,0:T(8,128)(2,1)} fusion(bf16[8,512,1024]{2,1,0:T(8,128)(2,1)} %collective-permute-done, bf16[8,2,512,1024]{3,2,1,0:T(8,128)(2,1)} %bitcast.58, s32[]{:T(128)S(6)} %select_n.41), kind=kLoop, calls=%fused_computation.7 | loop fusion | flops 16777216 | bytes 25165828 | tf_op jit(solution)/shard_map/convert_element_type | solution.py:156
  256.0 1.2 copy-done.1
  257.2 1.6 fusion.7.own_ref
  258.9 108.6 %reduce-scatter.2.cloned.1.call-done.summed_ref = bf16[512,1024]{1,0:T(8,128)(2,1)} async-done(((bf16[4096,1024]{1,0:T(8,128)(2,1)}), bf16[512,1024]{1,0:T(8,128)(2,1)}) %reduce-scatter.2.cloned.1.call-update) | async-done | bytes 1048592 | tf_op jit(solution)/shard_map/reduce_scatter | solution.py:157
  367.5 3.3 shard_map.65
  (28 shorter events, 4.0 us)
Async XLA Ops:
  6.5 117.5 %all-gather.4.cloned.1.call-start = ((), (), s32[]{:S(2)}) async-start(), calls=%async_computation.2 | async-start | bytes 17825792 | tf_op jit(solution)/shard_map/all_gather | solution.py:111
  7.3 360.2 %reduce-scatter.2.cloned.1.call-start = ((), (), s32[]{:S(2)}) async-start(), calls=%async_computation.1 | async-start | bytes 9437184 | tf_op jit(solution)/shard_map/reduce_scatter | solution.py:157
  74.0 12.2 %copy-start.2 = (s32[2048]{0:T(1024)S(1)}, s32[2048]{0:T(1024)}, u32[]{:S(2)}) copy-start(s32[2048]{0:T(1024)} %param.10) | copy-start | bytes 24580
  74.0 12.6 %copy-start.3 = (s32[2048]{0:T(1024)S(1)}, s32[2048]{0:T(1024)}, u32[]{:S(2)}) copy-start(s32[2048]{0:T(1024)} %param.11) | copy-start | bytes 24580
  161.8 1.2 copy-start
  231.8 13.5 %collective-permute-start = (bf16[8,512,1024]{2,1,0:T(8,128)(2,1)}, bf16[8,512,1024]{2,1,0:T(8,128)(2,1)}, u32[]{:S(2)}, u32[]{:S(2)}) collective-permute-start(bf16[8,512,1024]{2,1,0:T(8,128)(2,1)} %dynamic-slice_bitcast_fusion), channel_id=1, source_target_pairs={{0,8},{8,0},{1,9},{9,1},{2,10},{10,2},{3,11},{11,3},{4,12},{12,4},... | collective-permute-start | bytes 25165832 | tf_op jit(solution)/shard_map/ppermute | solution.py:155
  256.0 1.2 copy-start.1
Sparse Core Ops, SparseCore 0:
  9.8 114.1 all-gather.3
  256.2 111.2 reduce-scatter.1

commit v13 on v12

--- a/solution.py
+++ b/solution.py
@@ -129,7 +129,9 @@
         near_raw, far_raw, near_scale, far_scale, obs,
         win_start[:, None], win_end[:, None], table,
     ).reshape(2 * pair_count, full_width)
+    core = lax.axis_index("core")
     owner_flat = jnp.concatenate([pair_owner[:, 0], pair_owner[:, 1]])
+    owner_flat = ((owner_flat % 2) ^ core) * (owners // 2) + owner_flat // 2
     slot_flat = jnp.concatenate([pair_slot[:, 0], pair_slot[:, 1]])
     position = owner_positions(owner_flat, owners)
     flat_slot = owner_flat * capacity + position
@@ -145,15 +147,15 @@
     ).reshape(owners, capacity, full_width)
     station_ids = jnp.arange(station_count, dtype=jnp.int32)[None, :, None]
     onehot = (slot_station == station_ids).astype(jnp.bfloat16)
-    dense = jnp.einsum(
-        "osk,okf->osf", onehot, slotted, preferred_element_type=jnp.float32
-    ).astype(jnp.bfloat16).reshape(owners * station_count, full_width)
-    core = lax.axis_index("core")
-    by_core = dense.reshape(owners // 2, 2, station_count, full_width)
-    keep = lax.dynamic_index_in_dim(by_core, core, axis=1, keepdims=False)
-    give = lax.dynamic_index_in_dim(by_core, 1 - core, axis=1, keepdims=False)
+    half = owners // 2
+    give = jnp.einsum(
+        "osk,okf->osf", onehot[half:], slotted[half:], preferred_element_type=jnp.float32
+    ).astype(jnp.bfloat16)
     taken = lax.ppermute(give, "core", perm=[(0, 1), (1, 0)])
-    chip_sum = (keep.astype(jnp.float32) + taken.astype(jnp.float32)).astype(jnp.bfloat16)
+    keep = jnp.einsum(
+        "osk,okf->osf", onehot[:half], slotted[:half], preferred_element_type=jnp.float32
+    )
+    chip_sum = (keep + taken.astype(jnp.float32)).astype(jnp.bfloat16)
     summed = lax.psum_scatter(
         chip_sum.reshape(owners // 2 * station_count, full_width),
         ("z_hi", "x"),

time: 378 us -> 366 us (0.968)
  other arithmetic: 30 us -> 19.5 us
    convert_element_type x1 -> x0, other arithmetic: 10.7 us -> none  [shards(): (keep.astype(jnp.float32) + taken.astype(jnp.float32)).astype(jnp.bfloat16)]
    squeeze x1 -> x0, local copies, waits for them, and re-layouts: 7.58 us -> none  [shards(): give = lax.dynamic_index_in_dim(by_core, 1 - core, axis=1, keepdims=False)]
    slice x1 -> x2, local copies, waits for them, and re-layouts: 0.46 us -> 6 us  [the longest x1 5.53 us: shards(): slotted[:half]]
    dot_general x1 -> x2, matrix products: 16.8 us -> 16.8 us  [the longest x1 9.69 us: shards(): jnp.einsum('osk,okf->osf', onehot[:half], slotted[:half], preferred_eleme...]
  transfers between devices with their start and end apart: 3 -> 3, of which waited for: 3 -> 3; matrix products, arithmetic and copies ran while one was open for 16% -> 17% of each run, Pallas kernels for 0% -> 0%
where the time goes in v13:
time: 366 us; the launch traced here: 365 us
  waiting for transfers between devices  133 us (36%)
  local copies, waits for them, and re-layouts  115 us (31%)
  blocking collectives  46.9 us (13%)
  Pallas kernels  21 us (6%)
  other arithmetic  19.5 us (5%)
  matrix products  16.8 us (5%)
  between operations  13.6 us (4%)
    reduce_scatter x1, waiting for transfers between devices, shards(): lax.psum_scatter(chip_sum.reshape(owners // 2 * station_count, full_width...  109 us
    all_gather x1, blocking collectives, shards(): lax.all_gather(scale, ('z_hi', 'x', 'core'), axis=0, tiled=True)  28.9 us
    scatter x1, local copies, waits for them, and re-layouts, shards(): slotted = jnp.zeros((owners * capacity, full_width), jnp.bfloat16).at[fla...  26.6 us
    gather x1, local copies, waits for them, and re-layouts, shards(): far_raw = panel_raw[rows1]  19 us
    gather x1, local copies, waits for them, and re-layouts, shards(): near_raw = panel_raw[rows0]  18.9 us
    psum x1, blocking collectives, shards(): total_power = lax.psum(local_power, ('y', 'z_lo'))  18 us
    pallas_call x1, Pallas kernels, pair_contributions(): pl.pallas_call(pair_kernel, grid=(pairs // block,), in_specs=[pl.BlockSpe...  17.8 us
    scatter x1, local copies, waits for them, and re-layouts, shards(): slot_station = jnp.full((owners * capacity,), station_count, jnp.int32).a...  15.7 us
  transfers between devices with their start and end apart: 3, of which 3 were waited for; matrix products, arithmetic and copies ran while one was open for 17% of the time, Pallas kernels for 0%

profile of v13, /device:TPU:1, one launch (start us, length us, event | category | flops | bytes accessed | tf_op | source)
XLA Modules:
  0.0 365.3 jit_solution(13282176158021339912)
XLA Ops:
  8.2 4.6 %reduce-window.6 = s32[16,32,128]{2,1,0:T(8,128)S(1)} reduce-window(s32[16,32,128]{2,1,0:T(8,128)S(1)} %fusion.18, s32[]{:T(128)} %constant.59.clone.1), window={size=1x1x128 pad=0_0x0_0x127_0}, to_apply=%region_0.0 | reduce-window | flops 8323072 | bytes 524292 | tf_op jit(solution)/shard_map/reduce-window
  13.5 1.5 fusion.7
  15.0 18.0 %psum.7 = f32[512]{0:T(512)S(1)} all-reduce(f32[512]{0:T(512)S(1)} %fusion.7), channel_id=1, replica_groups=mesh['z_hi'=2,'x'=4,'core'=2,'y'=4,'z_lo'=2] {'y','z_lo'}, use_global_device_ids=true, to_apply=%region_5.6 | all-reduce | flops 512 | bytes 4096 | tf_op jit(solution)/shard_map/psum | solution.py:114
  33.0 28.9 %all-gather.1 = f32[16,1,512]{2,1,0:T(1,128)S(1)} all-gather(f32[1,1,512]{2,1,0:T(1,128)S(1)} %bitcast.66), channel_id=1, replica_groups=mesh['z_hi'=2,'x'=4,'core'=2,'y'=4,'z_lo'=2] {'z_hi','x','core'}, dimensions={0}, use_global_device_ids=true | all-gather | bytes 34816 | tf_op jit(solution)/shard_map/all_gather | solution.py:118
  61.9 11.8 %gather_fusion.2 = f32[2048]{0:T(1024)S(1)} fusion(f32[8192]{0:T(1024)S(1)} %bitcast.45, s32[2048]{0:T(1024)S(1)} %broadcast_clamp_fusion.1), kind=kCustom, calls=%fused_computation.2 | custom fusion | bytes 24576 | tf_op jit(solution)/shard_map/gather | solution.py:124
  74.1 11.8 %gather_fusion.3 = f32[2048]{0:T(1024)S(1)} fusion(f32[8192]{0:T(1024)S(1)} %bitcast.46, s32[2048]{0:T(1024)S(1)} %broadcast_clamp_fusion), kind=kCustom, calls=%fused_computation.3 | custom fusion | bytes 24576 | tf_op jit(solution)/shard_map/gather | solution.py:125
  86.6 1.3 copy.14.we_ref
  88.5 15.7 %scatter_custom_fusion = s32[6144]{0:T(1024)S(1)} fusion(s32[4096]{0:T(1024)S(1)} %bitcast.67, s32[4096]{0:T(1024)S(1)} %pad_add_fusion.2, s32[]{:T(128)} %constant.58.clone.1), kind=kCustom, calls=%fused_computation.80 | custom fusion | bytes 24580 | tf_op jit(solution)/shard_map/scatter | solution.py:141
  104.3 8.6 %multiply_convert_fusion = (bf16[512,1024]{1,0:T(8,128)(2,1)S(1)}, bf16[512,1024]{1,0:T(8,128)(2,1)S(1)}) fusion(), kind=kLoop, calls=%fused_computation.26 | loop fusion | flops 9961472 | bytes 2097152 | tf_op jit(solution)/shard_map/convert.1
  112.8 1.6 pad_maximum_fusion.table_ref
  114.4 9.7 %all-gather.4.cloned.1.call-done = bf16[8192,1,1024]{2,0,1:T(8,128)(2,1)} async-done(((bf16[512,1,1024]{2,0,1:T(8,128)(2,1)}), bf16[8192,1,1024]{2,0,1:T(8,128)(2,1)}) %all-gather.4.cloned.1.call-update) | async-done | bytes 16777232 | tf_op jit(solution)/shard_map/all_gather | solution.py:111
  124.1 18.9 %gather_fusion = bf16[2048,1024]{1,0:T(8,128)(2,1)} fusion(bf16[8192,1024]{1,0:T(8,128)(2,1)} %bitcast.47, s32[2048]{0:T(1024)S(1)} %broadcast_clamp_fusion.1), kind=kCustom, calls=%fused_computation | custom fusion | bytes 8396800 | tf_op jit(solution)/shard_map/gather | solution.py:122
  143.0 19.0 %gather_fusion.1 = bf16[2048,1024]{1,0:T(8,128)(2,1)} fusion(bf16[8192,1024]{1,0:T(8,128)(2,1)} %bitcast.48, s32[2048]{0:T(1024)S(1)} %broadcast_clamp_fusion), kind=kCustom, calls=%fused_computation.1 | custom fusion | bytes 8396800 | tf_op jit(solution)/shard_map/gather | solution.py:123
  162.0 1.2 copy-done
  163.2 17.8 %shard_map.64 = bf16[2,2048,1024]{2,1,0:T(8,128)(2,1)} custom-call(bf16[2048,1024]{1,0:T(8,128)(2,1)} %gather_fusion, bf16[2048,1024]{1,0:T(8,128)(2,1)} %gather_fusion.1, f32[2048,1]{1,0:T(8,128)S(1)} %copy.11.ns_ref, f32[2048,1]{1,0:T(8,128)S(1)} %copy.12.fs_ref, bf16[2048,1024]{1,0:T(8,128)(2,1)} %bitcast.53, s32[2048,1]{1,0:T(8,128)S(1)} %copy.13.ws_ref, ...), custom_call_target="tpu_custom_call" | custom-call | tf_op jit(solution)/shard_map/pallas_call | solution.py:66
  181.0 26.6 %scatter_custom_fusion.1 = bf16[6144,1024]{1,0:T(8,128)(2,1)} fusion(s32[4096]{0:T(1024)S(1)} %bitcast.68, bf16[4096,1024]{1,0:T(8,128)(2,1)} %bitcast.50, bf16[]{:T(256)} %constant.68.clone.1), kind=kCustom, calls=%fused_computation.11 | custom fusion | bytes 12583424 | tf_op jit(solution)/shard_map/scatter | solution.py:146
  207.6 5.5 %fusion.38 = (bf16[3072,1024]{1,0:T(8,128)(2,1)S(1)}, bf16[3072,1024]{1,0:T(8,128)(2,1)S(1)}) fusion(bf16[6144,1024]{1,0:T(8,128)(2,1)} %scatter_custom_fusion.1), kind=kLoop, calls=%fused_computation.85 | loop fusion | bytes 25165824 | tf_op jit(solution)/shard_map/slice | solution.py:156
  213.1 7.1 %fusion.2 = bf16[8,512,1024]{2,1,0:T(8,128)(2,1)} fusion(bf16[8,384,1024]{2,1,0:T(8,128)(2,1)S(1)} %bitcast.52, s32[16,384]{1,0:T(8,128)S(1)} %eq.46), kind=kOutput, calls=%fused_computation.10 | convolution fusion | flops 3228565504 | bytes 14704640 | tf_op jit(solution)/shard_map/osk,okf->osf/dot_general | solution.py:151
  220.5 13.3 %collective-permute-done = bf16[8,512,1024]{2,1,0:T(8,128)(2,1)} collective-permute-done((bf16[8,512,1024]{2,1,0:T(8,128)(2,1)}, bf16[8,512,1024]{2,1,0:T(8,128)(2,1)}, u32[]{:S(2)}, u32[]{:S(2)}) %collective-permute-start) | collective-permute-done | bytes 8388640 | tf_op jit(solution)/shard_map/ppermute | solution.py:154
  233.7 9.7 %add_convert_fusion = bf16[8,512,1024]{2,1,0:T(8,128)(2,1)} fusion(bf16[8,512,1024]{2,1,0:T(8,128)(2,1)} %collective-permute-done, bf16[8,384,1024]{2,1,0:T(8,128)(2,1)S(1)} %bitcast.51, s32[16,384]{1,0:T(8,128)S(1)} %eq.46), kind=kOutput, calls=%fused_computation.6 | convolution fusion | flops 3236954112 | bytes 23093248 | tf_op jit(solution)/shard_map/osk,okf->osf/dot_general | solution.py:155
  243.5 1.2 copy-done.1
  244.7 1.6 fusion.8.own_ref
  246.3 109.0 %reduce-scatter.2.cloned.1.call-done.summed_ref = bf16[512,1024]{1,0:T(8,128)(2,1)} async-done(((bf16[4096,1024]{1,0:T(8,128)(2,1)}), bf16[512,1024]{1,0:T(8,128)(2,1)}) %reduce-scatter.2.cloned.1.call-update) | async-done | bytes 1048592 | tf_op jit(solution)/shard_map/reduce_scatter | solution.py:159
  355.2 3.3 shard_map.65
  (33 shorter events, 4.2 us)
Async XLA Ops:
  6.5 117.6 %all-gather.4.cloned.1.call-start = ((), (), s32[]{:S(2)}) async-start(), calls=%async_computation.2 | async-start | bytes 17825792 | tf_op jit(solution)/shard_map/all_gather | solution.py:111
  7.3 348.0 %reduce-scatter.2.cloned.1.call-start = ((), (), s32[]{:S(2)}) async-start(), calls=%async_computation.1 | async-start | bytes 9437184 | tf_op jit(solution)/shard_map/reduce_scatter | solution.py:159
  33.0 28.9 %copy-start.2 = (f32[512]{0:T(512)}, f32[512]{0:T(512)S(1)}, u32[]{:S(2)}) copy-start(f32[512]{0:T(512)S(1)} %add_rsqrt_fusion) | copy-start | bytes 6148
  74.1 12.2 %copy-start.4 = (s32[2048]{0:T(1024)S(1)}, s32[2048]{0:T(1024)}, u32[]{:S(2)}) copy-start(s32[2048]{0:T(1024)} %param.10) | copy-start | bytes 24580
  74.1 12.6 %copy-start.5 = (s32[2048]{0:T(1024)S(1)}, s32[2048]{0:T(1024)}, u32[]{:S(2)}) copy-start(s32[2048]{0:T(1024)} %param.11) | copy-start | bytes 24580
  162.0 1.2 copy-start
  220.2 13.5 %collective-permute-start = (bf16[8,512,1024]{2,1,0:T(8,128)(2,1)}, bf16[8,512,1024]{2,1,0:T(8,128)(2,1)}, u32[]{:S(2)}, u32[]{:S(2)}) collective-permute-start(bf16[8,512,1024]{2,1,0:T(8,128)(2,1)} %fusion.2), channel_id=1, source_target_pairs={{0,8},{8,0},{1,9},{9,1},{2,10},{10,2},{3,11},{11,3},{4,12},{12,4},... | collective-permute-start | bytes 25165832 | tf_op jit(solution)/shard_map/ppermute | solution.py:154
  243.4 1.2 copy-start.1
  243.4 1.2 copy-start.3
Sparse Core Ops, SparseCore 0:
  9.8 114.2 all-gather.3
  243.6 111.5 reduce-scatter.1

commit v14 on v13

--- a/solution.py
+++ b/solution.py
@@ -148,10 +148,17 @@
     station_ids = jnp.arange(station_count, dtype=jnp.int32)[None, :, None]
     onehot = (slot_station == station_ids).astype(jnp.bfloat16)
     half = owners // 2
-    give = jnp.einsum(
-        "osk,okf->osf", onehot[half:], slotted[half:], preferred_element_type=jnp.float32
-    ).astype(jnp.bfloat16)
-    taken = lax.ppermute(give, "core", perm=[(0, 1), (1, 0)])
+    quarter = half // 2
+    taken = []
+    for start in (half, half + quarter):
+        give = jnp.einsum(
+            "osk,okf->osf",
+            onehot[start:start + quarter],
+            slotted[start:start + quarter],
+            preferred_element_type=jnp.float32,
+        ).astype(jnp.bfloat16)
+        taken.append(lax.ppermute(give, "core", perm=[(0, 1), (1, 0)]))
+    taken = jnp.concatenate(taken, axis=0)
     keep = jnp.einsum(
         "osk,okf->osf", onehot[:half], slotted[:half], preferred_element_type=jnp.float32
     )

time: 366 us -> 362 us (0.989)
  waiting for transfers between devices: 133 us -> 125 us
    ppermute x1 -> x2, waiting for transfers between devices: 13.3 us -> 5.21 us  [shards(): taken.append(lax.ppermute(give, 'core', perm=[(0, 1), (1, 0)]))]
    dot_general x1 -> x2, matrix products: 7.11 us -> 8.88 us  [shards(): jnp.einsum('osk,okf->osf', onehot[start:start + quarter], slotted[start:s...]
  transfers between devices with their start and end apart: 3 -> 4, of which waited for: 3 -> 3; matrix products, arithmetic and copies ran while one was open for 17% -> 19% of each run, Pallas kernels for 0% -> 0%
where the time goes in v14:
time: 362 us
  waiting for transfers between devices  125 us (35%)
  local copies, waits for them, and re-layouts  116 us (32%)
  blocking collectives  46.9 us (13%)
  Pallas kernels  20.9 us (6%)
  matrix products  19.8 us (5%)
  other arithmetic  19.5 us (5%)
  between operations  13.6 us (4%)
    reduce_scatter x1, waiting for transfers between devices, shards(): lax.psum_scatter(chip_sum.reshape(owners // 2 * station_count, full_width...  109 us
    all_gather x1, blocking collectives, shards(): lax.all_gather(scale, ('z_hi', 'x', 'core'), axis=0, tiled=True)  28.9 us
    scatter x1, local copies, waits for them, and re-layouts, shards(): slotted = jnp.zeros((owners * capacity, full_width), jnp.bfloat16).at[fla...  26.6 us
    gather x1, local copies, waits for them, and re-layouts, shards(): near_raw = panel_raw[rows0]  18.9 us
    gather x1, local copies, waits for them, and re-layouts, shards(): far_raw = panel_raw[rows1]  18.9 us
    psum x1, blocking collectives, shards(): total_power = lax.psum(local_power, ('y', 'z_lo'))  18 us
    pallas_call x1, Pallas kernels, pair_contributions(): pl.pallas_call(pair_kernel, grid=(pairs // block,), in_specs=[pl.BlockSpe...  17.7 us
    scatter x1, local copies, waits for them, and re-layouts, shards(): slot_station = jnp.full((owners * capacity,), station_count, jnp.int32).a...  15.7 us
  transfers between devices with their start and end apart: 4, of which 3 were waited for; matrix products, arithmetic and copies ran while one was open for 19% of the time, Pallas kernels for 0%

profile of v14, /device:TPU:1, one launch (start us, length us, event | category | flops | bytes accessed | tf_op | source)
XLA Modules:
  0.0 361.8 jit_solution(4935695300075430153)
XLA Ops:
  8.2 4.6 %reduce-window.6 = s32[16,32,128]{2,1,0:T(8,128)S(1)} reduce-window(s32[16,32,128]{2,1,0:T(8,128)S(1)} %fusion.21, s32[]{:T(128)} %constant.59.clone.1), window={size=1x1x128 pad=0_0x0_0x127_0}, to_apply=%region_0.0 | reduce-window | flops 8323072 | bytes 524292 | tf_op jit(solution)/shard_map/reduce-window
  13.5 1.5 fusion.10
  15.0 18.0 %psum.7 = f32[512]{0:T(512)S(1)} all-reduce(f32[512]{0:T(512)S(1)} %fusion.10), channel_id=1, replica_groups=mesh['z_hi'=2,'x'=4,'core'=2,'y'=4,'z_lo'=2] {'y','z_lo'}, use_global_device_ids=true, to_apply=%region_5.6 | all-reduce | flops 512 | bytes 4096 | tf_op jit(solution)/shard_map/psum | solution.py:114
  33.0 28.9 %all-gather.1 = f32[16,1,512]{2,1,0:T(1,128)S(1)} all-gather(f32[1,1,512]{2,1,0:T(1,128)S(1)} %bitcast.71), channel_id=1, replica_groups=mesh['z_hi'=2,'x'=4,'core'=2,'y'=4,'z_lo'=2] {'z_hi','x','core'}, dimensions={0}, use_global_device_ids=true | all-gather | bytes 34816 | tf_op jit(solution)/shard_map/all_gather | solution.py:118
  61.9 11.8 %gather_fusion.2 = f32[2048]{0:T(1024)S(1)} fusion(f32[8192]{0:T(1024)S(1)} %bitcast.47, s32[2048]{0:T(1024)S(1)} %broadcast_clamp_fusion.1), kind=kCustom, calls=%fused_computation.2 | custom fusion | bytes 24576 | tf_op jit(solution)/shard_map/gather | solution.py:124
  74.1 11.8 %gather_fusion.3 = f32[2048]{0:T(1024)S(1)} fusion(f32[8192]{0:T(1024)S(1)} %bitcast.48, s32[2048]{0:T(1024)S(1)} %broadcast_clamp_fusion), kind=kCustom, calls=%fused_computation.3 | custom fusion | bytes 24576 | tf_op jit(solution)/shard_map/gather | solution.py:125
  86.6 1.3 copy.14.we_ref
  88.5 15.7 %scatter_custom_fusion = s32[6144]{0:T(1024)S(1)} fusion(s32[4096]{0:T(1024)S(1)} %bitcast.72, s32[4096]{0:T(1024)S(1)} %pad_add_fusion.2, s32[]{:T(128)} %constant.58.clone.1), kind=kCustom, calls=%fused_computation.83 | custom fusion | bytes 24580 | tf_op jit(solution)/shard_map/scatter | solution.py:141
  104.3 8.6 %multiply_convert_fusion = (bf16[512,1024]{1,0:T(8,128)(2,1)S(1)}, bf16[512,1024]{1,0:T(8,128)(2,1)S(1)}) fusion(), kind=kLoop, calls=%fused_computation.29 | loop fusion | flops 9961472 | bytes 2097152 | tf_op jit(solution)/shard_map/convert.1
  112.8 1.6 pad_maximum_fusion.table_ref
  114.4 9.7 %all-gather.4.cloned.1.call-done = bf16[8192,1,1024]{2,0,1:T(8,128)(2,1)} async-done(((bf16[512,1,1024]{2,0,1:T(8,128)(2,1)}), bf16[8192,1,1024]{2,0,1:T(8,128)(2,1)}) %all-gather.4.cloned.1.call-update) | async-done | bytes 16777232 | tf_op jit(solution)/shard_map/all_gather | solution.py:111
  124.1 18.9 %gather_fusion = bf16[2048,1024]{1,0:T(8,128)(2,1)} fusion(bf16[8192,1024]{1,0:T(8,128)(2,1)} %bitcast.49, s32[2048]{0:T(1024)S(1)} %broadcast_clamp_fusion.1), kind=kCustom, calls=%fused_computation | custom fusion | bytes 8396800 | tf_op jit(solution)/shard_map/gather | solution.py:122
  143.0 18.9 %gather_fusion.1 = bf16[2048,1024]{1,0:T(8,128)(2,1)} fusion(bf16[8192,1024]{1,0:T(8,128)(2,1)} %bitcast.50, s32[2048]{0:T(1024)S(1)} %broadcast_clamp_fusion), kind=kCustom, calls=%fused_computation.1 | custom fusion | bytes 8396800 | tf_op jit(solution)/shard_map/gather | solution.py:123
  163.1 17.7 %shard_map.64 = bf16[2,2048,1024]{2,1,0:T(8,128)(2,1)} custom-call(bf16[2048,1024]{1,0:T(8,128)(2,1)} %gather_fusion, bf16[2048,1024]{1,0:T(8,128)(2,1)} %gather_fusion.1, f32[2048,1]{1,0:T(8,128)S(1)} %copy.11.ns_ref, f32[2048,1]{1,0:T(8,128)S(1)} %copy.12.fs_ref, bf16[2048,1024]{1,0:T(8,128)(2,1)} %bitcast.56, s32[2048,1]{1,0:T(8,128)S(1)} %copy.13.ws_ref, ...), custom_call_target="tpu_custom_call" | custom-call | tf_op jit(solution)/shard_map/pallas_call | solution.py:66
  180.8 26.6 %scatter_custom_fusion.1 = bf16[6144,1024]{1,0:T(8,128)(2,1)} fusion(s32[4096]{0:T(1024)S(1)} %bitcast.73, bf16[4096,1024]{1,0:T(8,128)(2,1)} %bitcast.54, bf16[]{:T(256)} %constant.68.clone.1), kind=kCustom, calls=%fused_computation.11 | custom fusion | bytes 12583424 | tf_op jit(solution)/shard_map/scatter | solution.py:146
  207.4 3.6 fusion.41
  211.0 4.4 %fusion.9 = bf16[4,512,1024]{2,1,0:T(8,128)(2,1)} fusion(bf16[4,384,1024]{2,1,0:T(8,128)(2,1)S(1)} %bitcast.58, s32[16,384]{1,0:T(8,128)S(1)} %eq.46), kind=kOutput, calls=%fused_computation.20 | convolution fusion | flops 1615855616 | bytes 7364608 | tf_op jit(solution)/shard_map/osk,okf->osf/dot_general | solution.py:154
  215.7 4.4 %fusion.8 = bf16[4,512,1024]{2,1,0:T(8,128)(2,1)} fusion(bf16[4,384,1024]{2,1,0:T(8,128)(2,1)S(1)} %bitcast.57, s32[16,384]{1,0:T(8,128)S(1)} %eq.46), kind=kOutput, calls=%fused_computation.19 | convolution fusion | flops 1615855616 | bytes 7364608 | tf_op jit(solution)/shard_map/osk,okf->osf/dot_general | solution.py:154
  220.4 3.3 slice.74
  223.7 5.2 %collective-permute-done = bf16[4,512,1024]{2,1,0:T(8,128)(2,1)} collective-permute-done((bf16[4,512,1024]{2,1,0:T(8,128)(2,1)}, bf16[4,512,1024]{2,1,0:T(8,128)(2,1)}, u32[]{:S(2)}, u32[]{:S(2)}) %collective-permute-start) | collective-permute-done | bytes 4194336 | tf_op jit(solution)/shard_map/ppermute | solution.py:160
  228.9 11.0 %add_convert_fusion = bf16[8,512,1024]{2,1,0:T(8,128)(2,1)} fusion(bf16[4,512,1024]{2,1,0:T(8,128)(2,1)S(1)} %collective-permute-done.1, bf16[4,512,1024]{2,1,0:T(8,128)(2,1)} %collective-permute-done, bf16[8,384,1024]{2,1,0:T(8,128)(2,1)} %bitcast.55, s32[16,384]{1,0:T(8,128)S(1)} %eq.46), kind=kOutput, calls=%fused_computation.6 | convolution fusion | flops 3241148416 | bytes 23093248 | tf_op jit(solution)/shard_map/osk,okf->osf/dot_general | solution.py:162
  241.1 1.6 fusion.11.own_ref
  242.7 109.0 %reduce-scatter.2.cloned.1.call-done.summed_ref = bf16[512,1024]{1,0:T(8,128)(2,1)} async-done(((bf16[4096,1024]{1,0:T(8,128)(2,1)}), bf16[512,1024]{1,0:T(8,128)(2,1)}) %reduce-scatter.2.cloned.1.call-update) | async-done | bytes 1048592 | tf_op jit(solution)/shard_map/reduce_scatter | solution.py:166
  351.7 3.3 shard_map.65
  (40 shorter events, 6.9 us)
Async XLA Ops:
  6.5 117.5 %all-gather.4.cloned.1.call-start = ((), (), s32[]{:S(2)}) async-start(), calls=%async_computation.2 | async-start | bytes 17825792 | tf_op jit(solution)/shard_map/all_gather | solution.py:111
  7.3 344.5 %reduce-scatter.2.cloned.1.call-start = ((), (), s32[]{:S(2)}) async-start(), calls=%async_computation.1 | async-start | bytes 9437184 | tf_op jit(solution)/shard_map/reduce_scatter | solution.py:166
  74.0 12.2 %copy-start.2 = (s32[2048]{0:T(1024)S(1)}, s32[2048]{0:T(1024)}, u32[]{:S(2)}) copy-start(s32[2048]{0:T(1024)} %param.10) | copy-start | bytes 24580
  74.1 12.6 %copy-start.3 = (s32[2048]{0:T(1024)S(1)}, s32[2048]{0:T(1024)}, u32[]{:S(2)}) copy-start(s32[2048]{0:T(1024)} %param.11) | copy-start | bytes 24580
  161.9 1.2 copy-start
  211.0 9.4 %slice-start = ((s8[12582912]{0:T(1024)(128)(4,1)}), s8[4194304]{0:T(1024)(128)(4,1)S(1)}, s32[]{:S(2)}) async-start(s8[12582912]{0:T(1024)(128)(4,1)} %bitcast.51), calls=%async_computation.3 | async-start | bytes 8388608
  211.0 9.4 %slice-start.1 = ((s8[12582912]{0:T(1024)(128)(4,1)}), s8[4194304]{0:T(1024)(128)(4,1)S(1)}, s32[]{:S(2)}) async-start(s8[12582912]{0:T(1024)(128)(4,1)} %bitcast.51), calls=%async_computation.4 | async-start | bytes 8388608
  215.4 8.3 %collective-permute-start.1 = (bf16[4,512,1024]{2,1,0:T(8,128)(2,1)}, bf16[4,512,1024]{2,1,0:T(8,128)(2,1)S(1)}, u32[]{:S(2)}, u32[]{:S(2)}) collective-permute-start(bf16[4,512,1024]{2,1,0:T(8,128)(2,1)} %fusion.9), channel_id=1, source_target_pairs={{0,8},{8,0},{1,9},{9,1},{2,10},{10,2},{3,11},{11,3},{4,12},{12,4},... | collective-permute-start | bytes 12582920 | tf_op jit(solution)/shard_map/ppermute | solution.py:160
  215.7 4.7 %slice-start.2 = ((s8[12582912]{0:T(1024)(128)(4,1)}), s8[4194304]{0:T(1024)(128)(4,1)S(1)}, s32[]{:S(2)}) async-start(s8[12582912]{0:T(1024)(128)(4,1)} %bitcast.51), calls=%async_computation.5 | async-start | bytes 8388608
  220.1 8.8 %collective-permute-start = (bf16[4,512,1024]{2,1,0:T(8,128)(2,1)}, bf16[4,512,1024]{2,1,0:T(8,128)(2,1)}, u32[]{:S(2)}, u32[]{:S(2)}) collective-permute-start(bf16[4,512,1024]{2,1,0:T(8,128)(2,1)} %fusion.8), channel_id=1, source_target_pairs={{0,8},{8,0},{1,9},{9,1},{2,10},{10,2},{3,11},{11,3},{4,12},{12,4},... | collective-permute-start | bytes 12582920 | tf_op jit(solution)/shard_map/ppermute | solution.py:160
  239.9 1.2 copy-start.1
Sparse Core Ops, SparseCore 0:
  9.8 114.2 all-gather.3
  240.0 111.6 reduce-scatter.1

commit v15 on v14

--- a/solution.py
+++ b/solution.py
@@ -148,9 +148,9 @@
     station_ids = jnp.arange(station_count, dtype=jnp.int32)[None, :, None]
     onehot = (slot_station == station_ids).astype(jnp.bfloat16)
     half = owners // 2
-    quarter = half // 2
+    quarter = half // 4
     taken = []
-    for start in (half, half + quarter):
+    for start in range(half, owners, quarter):
         give = jnp.einsum(
             "osk,okf->osf",
             onehot[start:start + quarter],

time: 362 us -> 357 us (0.986)
    dot_general x2 -> x4, matrix products: 8.88 us -> 7.87 us  [shards(): jnp.einsum('osk,okf->osf', onehot[start:start + quarter], slotted[start:s...]
  transfers between devices with their start and end apart: 4 -> 6, of which waited for: 3 -> 4; matrix products, arithmetic and copies ran while one was open for 19% -> 19% of each run, Pallas kernels for 0% -> 0%
where the time goes in v15:
time: 357 us
  waiting for transfers between devices  126 us (35%)
  local copies, waits for them, and re-layouts  113 us (32%)
  blocking collectives  46.8 us (13%)
  Pallas kernels  21 us (6%)
  other arithmetic  18.3 us (5%)
  matrix products  16.7 us (5%)
  between operations  13.6 us (4%)
    reduce_scatter x1, waiting for transfers between devices, shards(): lax.psum_scatter(chip_sum.reshape(owners // 2 * station_count, full_width...  109 us
    all_gather x1, blocking collectives, shards(): lax.all_gather(scale, ('z_hi', 'x', 'core'), axis=0, tiled=True)  29 us
    scatter x1, local copies, waits for them, and re-layouts, shards(): slotted = jnp.zeros((owners * capacity, full_width), jnp.bfloat16).at[fla...  26.7 us
    gather x1, local copies, waits for them, and re-layouts, shards(): near_raw = panel_raw[rows0]  18.9 us
    gather x1, local copies, waits for them, and re-layouts, shards(): far_raw = panel_raw[rows1]  18.9 us
    psum x1, blocking collectives, shards(): total_power = lax.psum(local_power, ('y', 'z_lo'))  17.9 us
    pallas_call x1, Pallas kernels, pair_contributions(): pl.pallas_call(pair_kernel, grid=(pairs // block,), in_specs=[pl.BlockSpe...  17.7 us
    scatter x1, local copies, waits for them, and re-layouts, shards(): slot_station = jnp.full((owners * capacity,), station_count, jnp.int32).a...  15.7 us
  transfers between devices with their start and end apart: 6, of which 4 were waited for; matrix products, arithmetic and copies ran while one was open for 19% of the time, Pallas kernels for 0%

profile of v15, /device:TPU:1, one launch (start us, length us, event | category | flops | bytes accessed | tf_op | source)
XLA Modules:
  0.0 356.5 jit_solution(15207498993280702798)
XLA Ops:
  8.2 4.6 %reduce-window.6 = s32[16,32,128]{2,1,0:T(8,128)S(1)} reduce-window(s32[16,32,128]{2,1,0:T(8,128)S(1)} %fusion.27, s32[]{:T(128)} %constant.59.clone.1), window={size=1x1x128 pad=0_0x0_0x127_0}, to_apply=%region_0.0 | reduce-window | flops 8323072 | bytes 524292 | tf_op jit(solution)/shard_map/reduce-window
  13.8 17.9 %psum.7 = f32[512]{0:T(512)S(1)} all-reduce(f32[512]{0:T(512)S(1)} %fusion.12), channel_id=1, replica_groups=mesh['z_hi'=2,'x'=4,'core'=2,'y'=4,'z_lo'=2] {'y','z_lo'}, use_global_device_ids=true, to_apply=%region_5.6 | all-reduce | flops 512 | bytes 4096 | tf_op jit(solution)/shard_map/psum | solution.py:114
  31.7 29.0 %all-gather.1 = f32[16,1,512]{2,1,0:T(1,128)S(1)} all-gather(f32[1,1,512]{2,1,0:T(1,128)S(1)} %bitcast.75), channel_id=1, replica_groups=mesh['z_hi'=2,'x'=4,'core'=2,'y'=4,'z_lo'=2] {'z_hi','x','core'}, dimensions={0}, use_global_device_ids=true | all-gather | bytes 34816 | tf_op jit(solution)/shard_map/all_gather | solution.py:118
  60.6 11.8 %gather_fusion.2 = f32[2048]{0:T(1024)S(1)} fusion(f32[8192]{0:T(1024)S(1)} %bitcast.51, s32[2048]{0:T(1024)S(1)} %broadcast_clamp_fusion.1), kind=kCustom, calls=%fused_computation.2 | custom fusion | bytes 24576 | tf_op jit(solution)/shard_map/gather | solution.py:124
  72.8 11.8 %gather_fusion.3 = f32[2048]{0:T(1024)S(1)} fusion(f32[8192]{0:T(1024)S(1)} %bitcast.52, s32[2048]{0:T(1024)S(1)} %broadcast_clamp_fusion), kind=kCustom, calls=%fused_computation.3 | custom fusion | bytes 24576 | tf_op jit(solution)/shard_map/gather | solution.py:125
  85.4 1.3 copy.14.we_ref
  87.3 15.7 %scatter_custom_fusion = s32[6144]{0:T(1024)S(1)} fusion(s32[4096]{0:T(1024)S(1)} %bitcast.76, s32[4096]{0:T(1024)S(1)} %pad_add_fusion.2, s32[]{:T(128)} %constant.58.clone.1), kind=kCustom, calls=%fused_computation.89 | custom fusion | bytes 24580 | tf_op jit(solution)/shard_map/scatter | solution.py:141
  103.0 8.6 %multiply_convert_fusion = (bf16[512,1024]{1,0:T(8,128)(2,1)S(1)}, bf16[512,1024]{1,0:T(8,128)(2,1)S(1)}) fusion(), kind=kLoop, calls=%fused_computation.31 | loop fusion | flops 9961472 | bytes 2097152 | tf_op jit(solution)/shard_map/convert.1
  111.6 1.6 pad_maximum_fusion.table_ref
  113.2 11.0 %all-gather.4.cloned.1.call-done = bf16[8192,1,1024]{2,0,1:T(8,128)(2,1)} async-done(((bf16[512,1,1024]{2,0,1:T(8,128)(2,1)}), bf16[8192,1,1024]{2,0,1:T(8,128)(2,1)}) %all-gather.4.cloned.1.call-update) | async-done | bytes 16777232 | tf_op jit(solution)/shard_map/all_gather | solution.py:111
  124.2 18.9 %gather_fusion = bf16[2048,1024]{1,0:T(8,128)(2,1)} fusion(bf16[8192,1024]{1,0:T(8,128)(2,1)} %bitcast.53, s32[2048]{0:T(1024)S(1)} %broadcast_clamp_fusion.1), kind=kCustom, calls=%fused_computation | custom fusion | bytes 8396800 | tf_op jit(solution)/shard_map/gather | solution.py:122
  143.1 18.9 %gather_fusion.1 = bf16[2048,1024]{1,0:T(8,128)(2,1)} fusion(bf16[8192,1024]{1,0:T(8,128)(2,1)} %bitcast.54, s32[2048]{0:T(1024)S(1)} %broadcast_clamp_fusion), kind=kCustom, calls=%fused_computation.1 | custom fusion | bytes 8396800 | tf_op jit(solution)/shard_map/gather | solution.py:123
  163.2 17.7 %shard_map.64 = bf16[2,2048,1024]{2,1,0:T(8,128)(2,1)} custom-call(bf16[2048,1024]{1,0:T(8,128)(2,1)} %gather_fusion, bf16[2048,1024]{1,0:T(8,128)(2,1)} %gather_fusion.1, f32[2048,1]{1,0:T(8,128)S(1)} %copy.11.ns_ref, f32[2048,1]{1,0:T(8,128)S(1)} %copy.12.fs_ref, bf16[2048,1024]{1,0:T(8,128)(2,1)} %bitcast.58, s32[2048,1]{1,0:T(8,128)S(1)} %copy.13.ws_ref, ...), custom_call_target="tpu_custom_call" | custom-call | tf_op jit(solution)/shard_map/pallas_call | solution.py:66
  181.0 26.7 %scatter_custom_fusion.1 = bf16[6144,1024]{1,0:T(8,128)(2,1)} fusion(s32[4096]{0:T(1024)S(1)} %bitcast.77, bf16[4096,1024]{1,0:T(8,128)(2,1)} %bitcast.57, bf16[]{:T(256)} %constant.68.clone.1), kind=kCustom, calls=%fused_computation.13 | custom fusion | bytes 12583424 | tf_op jit(solution)/shard_map/scatter | solution.py:146
  207.7 3.5 fusion.47
  211.2 1.3 fusion.23
  214.5 2.6 fusion.21
  217.4 2.7 fusion.20
  220.3 2.7 collective-permute-done.1
  223.0 3.1 collective-permute-done
  226.1 8.8 %add_convert_fusion = bf16[8,512,1024]{2,1,0:T(8,128)(2,1)} fusion(bf16[2,512,1024]{2,1,0:T(8,128)(2,1)S(1)} %collective-permute-done.3, bf16[2,512,1024]{2,1,0:T(8,128)(2,1)S(1)} %collective-permute-done.2, bf16[2,512,1024]{2,1,0:T(8,128)(2,1)S(1)} %collective-permute-done.1, bf16[2,512,1024]{2,1,0:T(8,128)(2,1)} %collective-permute-done, ...), kind=kOutput, calls=%fused_computation.6 | convolution fusion | flops 3249537024 | bytes 23093248 | tf_op jit(solution)/shard_map/osk,okf->osf/dot_general | solution.py:162
  236.1 1.7 fusion.13.own_ref
  237.8 108.6 %reduce-scatter.2.cloned.1.call-done.summed_ref = bf16[512,1024]{1,0:T(8,128)(2,1)} async-done(((bf16[4096,1024]{1,0:T(8,128)(2,1)}), bf16[512,1024]{1,0:T(8,128)(2,1)}) %reduce-scatter.2.cloned.1.call-update) | async-done | bytes 1048592 | tf_op jit(solution)/shard_map/reduce_scatter | solution.py:166
  346.4 3.3 shard_map.65
  (42 shorter events, 9.1 us)
Async XLA Ops:
  6.5 7.0 %copy-start.1 = (bf16[512,1,1024]{2,0,1:T(8,128)(2,1)S(1)}, bf16[512,1,1024]{2,0,1:T(8,128)(2,1)}, u32[]{:S(2)}) copy-start(bf16[512,1,1024]{2,0,1:T(8,128)(2,1)} %param.6) | copy-start | bytes 3145732
  6.5 117.7 %all-gather.4.cloned.1.call-start = ((), (), s32[]{:S(2)}) async-start(), calls=%async_computation.2 | async-start | bytes 17825792 | tf_op jit(solution)/shard_map/all_gather | solution.py:111
  7.3 339.2 %reduce-scatter.2.cloned.1.call-start = ((), (), s32[]{:S(2)}) async-start(), calls=%async_computation.1 | async-start | bytes 9437184 | tf_op jit(solution)/shard_map/reduce_scatter | solution.py:166
  72.8 12.2 %copy-start.3 = (s32[2048]{0:T(1024)S(1)}, s32[2048]{0:T(1024)}, u32[]{:S(2)}) copy-start(s32[2048]{0:T(1024)} %param.10) | copy-start | bytes 24580
  84.6 0.8 copy-start.4
  162.0 1.2 copy-start
  212.5 7.8 %collective-permute-start.3 = (bf16[2,512,1024]{2,1,0:T(8,128)(2,1)S(1)}, bf16[2,512,1024]{2,1,0:T(8,128)(2,1)S(1)}, u32[]{:S(2)}, u32[]{:S(2)}) collective-permute-start(bf16[2,512,1024]{2,1,0:T(8,128)(2,1)S(1)} %fusion.23), channel_id=1, source_target_pairs={{0,8},{8,0},{1,9},{9,1},{2,10},{10,2},{3,11},{11,3},{4,12},{12,4},... | collective-permute-start | bytes 6291464 | tf_op jit(solution)/shard_map/ppermute | solution.py:160
  214.2 6.1 %collective-permute-start.2 = (bf16[2,512,1024]{2,1,0:T(8,128)(2,1)S(1)}, bf16[2,512,1024]{2,1,0:T(8,128)(2,1)S(1)}, u32[]{:S(2)}, u32[]{:S(2)}) collective-permute-start(bf16[2,512,1024]{2,1,0:T(8,128)(2,1)S(1)} %fusion.22), channel_id=1, source_target_pairs={{0,8},{8,0},{1,9},{9,1},{2,10},{10,2},{3,11},{11,3},{4,12},{12,4},... | collective-permute-start | bytes 6291464 | tf_op jit(solution)/shard_map/ppermute | solution.py:160
  217.1 5.8 %collective-permute-start.1 = (bf16[2,512,1024]{2,1,0:T(8,128)(2,1)}, bf16[2,512,1024]{2,1,0:T(8,128)(2,1)S(1)}, u32[]{:S(2)}, u32[]{:S(2)}) collective-permute-start(bf16[2,512,1024]{2,1,0:T(8,128)(2,1)} %fusion.21), channel_id=1, source_target_pairs={{0,8},{8,0},{1,9},{9,1},{2,10},{10,2},{3,11},{11,3},{4,12},{12,4},... | collective-permute-start | bytes 6291464 | tf_op jit(solution)/shard_map/ppermute | solution.py:160
  220.0 6.1 %slice-start = ((bf16[6144,1024]{1,0:T(8,128)(2,1)}), bf16[3072,1024]{1,0:T(8,128)(2,1)S(1)}, s32[]{:S(2)}) async-start(bf16[6144,1024]{1,0:T(8,128)(2,1)} %scatter_custom_fusion.1), calls=%async_computation.3 | async-start | bytes 12582912 | tf_op jit(solution)/shard_map/slice | solution.py:163
  220.0 6.1 %collective-permute-start = (bf16[2,512,1024]{2,1,0:T(8,128)(2,1)}, bf16[2,512,1024]{2,1,0:T(8,128)(2,1)}, u32[]{:S(2)}, u32[]{:S(2)}) collective-permute-start(bf16[2,512,1024]{2,1,0:T(8,128)(2,1)} %fusion.20), channel_id=1, source_target_pairs={{0,8},{8,0},{1,9},{9,1},{2,10},{10,2},{3,11},{11,3},{4,12},{12,4},... | collective-permute-start | bytes 6291464 | tf_op jit(solution)/shard_map/ppermute | solution.py:160
  234.9 1.2 copy-start.2
Sparse Core Ops, SparseCore 0:
  9.8 114.3 all-gather.3
  235.1 111.3 reduce-scatter.1

commit v16 on v15

--- a/solution.py
+++ b/solution.py
@@ -148,7 +148,7 @@
     station_ids = jnp.arange(station_count, dtype=jnp.int32)[None, :, None]
     onehot = (slot_station == station_ids).astype(jnp.bfloat16)
     half = owners // 2
-    quarter = half // 4
+    quarter = half // 8
     taken = []
     for start in range(half, owners, quarter):
         give = jnp.einsum(

time: 357 us -> 374 us (1.048)
  matrix products: 16.7 us -> 28.4 us
  waiting for transfers between devices: 126 us -> 115 us
  local copies, waits for them, and re-layouts: 113 us -> 119 us
  other arithmetic: 18.3 us -> 23 us
    dot_general x4 -> x8, matrix products: 7.87 us -> 18.7 us  [shards(): jnp.einsum('osk,okf->osf', onehot[start:start + quarter], slotted[start:s...]
    unnamed x10 -> x21, local copies, waits for them, and re-layouts: 2.44 us -> 11.5 us
    ppermute x4 -> x8, waiting for transfers between devices: 5.81 us -> 0.02 us  [shards(): taken.append(lax.ppermute(give, 'core', perm=[(0, 1), (1, 0)]))]
    all_gather x1, waiting for transfers between devices: 11 us -> 5.91 us  [shards(): panel_raw = lax.all_gather(raw, ('z_hi', 'x', 'core'), axis=0, tiled=True)]
  transfers between devices with their start and end apart: 6 -> 10, of which waited for: 4 -> 2; matrix products, arithmetic and copies ran while one was open for 19% -> 24% of each run, Pallas kernels for 0% -> 0%
where the time goes in v16:
time: 374 us; the launch traced here: 370 us
  local copies, waits for them, and re-layouts  119 us (32%)
  waiting for transfers between devices  115 us (31%)
  blocking collectives  46.9 us (13%)
  matrix products  28.4 us (8%)
  other arithmetic  23 us (6%)
  Pallas kernels  21.1 us (6%)
  between operations  14 us (4%)
    reduce_scatter x1, waiting for transfers between devices, shards(): lax.psum_scatter(chip_sum.reshape(owners // 2 * station_count, full_width...  109 us
    all_gather x1, blocking collectives, shards(): lax.all_gather(scale, ('z_hi', 'x', 'core'), axis=0, tiled=True)  28.9 us
    scatter x1, local copies, waits for them, and re-layouts, shards(): slotted = jnp.zeros((owners * capacity, full_width), jnp.bfloat16).at[fla...  26.7 us
    gather x1, local copies, waits for them, and re-layouts, shards(): near_raw = panel_raw[rows0]  18.9 us
    gather x1, local copies, waits for them, and re-layouts, shards(): far_raw = panel_raw[rows1]  18.9 us
    dot_general x8, matrix products, shards(): jnp.einsum('osk,okf->osf', onehot[start:start + quarter], slotted[start:s...  18.7 us
    psum x1, blocking collectives, shards(): total_power = lax.psum(local_power, ('y', 'z_lo'))  18 us
    pallas_call x1, Pallas kernels, pair_contributions(): pl.pallas_call(pair_kernel, grid=(pairs // block,), in_specs=[pl.BlockSpe...  17.9 us
  transfers between devices with their start and end apart: 10, of which 2 were waited for; matrix products, arithmetic and copies ran while one was open for 24% of the time, Pallas kernels for 0%

profile of v16, /device:TPU:1, one launch (start us, length us, event | category | flops | bytes accessed | tf_op | source)
XLA Modules:
  0.0 369.9 jit_solution(12712072432763146098)
XLA Ops:
  8.2 4.6 %reduce-window.6 = s32[16,32,128]{2,1,0:T(8,128)S(1)} reduce-window(s32[16,32,128]{2,1,0:T(8,128)S(1)} %fusion.30, s32[]{:T(128)} %constant.59.clone.1), window={size=1x1x128 pad=0_0x0_0x127_0}, to_apply=%region_0.0 | reduce-window | flops 8323072 | bytes 524292 | tf_op jit(solution)/shard_map/reduce-window
  15.0 18.0 %psum.7 = f32[512]{0:T(512)S(1)} all-reduce(f32[512]{0:T(512)S(1)} %fusion.2), channel_id=1, replica_groups=mesh['z_hi'=2,'x'=4,'core'=2,'y'=4,'z_lo'=2] {'y','z_lo'}, use_global_device_ids=true, to_apply=%region_5.6 | all-reduce | flops 512 | bytes 4096 | tf_op jit(solution)/shard_map/psum | solution.py:114
  33.0 28.9 %all-gather.1 = f32[16,1,512]{2,1,0:T(1,128)S(1)} all-gather(f32[1,1,512]{2,1,0:T(1,128)S(1)} %bitcast.103), channel_id=1, replica_groups=mesh['z_hi'=2,'x'=4,'core'=2,'y'=4,'z_lo'=2] {'z_hi','x','core'}, dimensions={0}, use_global_device_ids=true | all-gather | bytes 34816 | tf_op jit(solution)/shard_map/all_gather | solution.py:118
  61.9 11.8 %gather_fusion.2 = f32[2048]{0:T(1024)S(1)} fusion(f32[8192]{0:T(1024)S(1)} %bitcast.83, s32[2048]{0:T(1024)S(1)} %get-tuple-element.12), kind=kCustom, calls=%fused_computation.2 | custom fusion | bytes 24576 | tf_op jit(solution)/shard_map/gather | solution.py:124
  74.1 11.8 %gather_fusion.3 = f32[2048]{0:T(1024)S(1)} fusion(f32[8192]{0:T(1024)S(1)} %bitcast.84, s32[2048]{0:T(1024)S(1)} %get-tuple-element.11), kind=kCustom, calls=%fused_computation.3 | custom fusion | bytes 24576 | tf_op jit(solution)/shard_map/gather | solution.py:125
  88.5 16.1 %scatter_custom_fusion = s32[6144]{0:T(1024)S(1)} fusion(s32[4096]{0:T(1024)S(1)} %bitcast.104, s32[4096]{0:T(1024)S(1)} %pad_add_fusion.2, s32[]{:T(128)} %constant.58.clone.1), kind=kCustom, calls=%fused_computation.116 | custom fusion | bytes 24580 | tf_op jit(solution)/shard_map/scatter | solution.py:141
  104.6 8.6 %multiply_convert_fusion = (bf16[512,1024]{1,0:T(8,128)(2,1)S(1)}, bf16[512,1024]{1,0:T(8,128)(2,1)S(1)}) fusion(), kind=kLoop, calls=%fused_computation.21 | loop fusion | flops 9961472 | bytes 2097152 | tf_op jit(solution)/shard_map/convert.1
  114.7 3.6 iota_compare_fusion
  118.2 5.9 %all-gather.4.cloned.1.call-done = bf16[8192,1,1024]{2,0,1:T(8,128)(2,1)} async-done(((bf16[512,1,1024]{2,0,1:T(8,128)(2,1)}), bf16[8192,1,1024]{2,0,1:T(8,128)(2,1)}) %all-gather.4.cloned.1.call-update) | async-done | bytes 16777232 | tf_op jit(solution)/shard_map/all_gather | solution.py:111
  124.1 18.9 %gather_fusion = bf16[2048,1024]{1,0:T(8,128)(2,1)} fusion(bf16[8192,1024]{1,0:T(8,128)(2,1)} %bitcast.85, s32[2048]{0:T(1024)S(1)} %get-tuple-element.12), kind=kCustom, calls=%fused_computation | custom fusion | bytes 8396800 | tf_op jit(solution)/shard_map/gather | solution.py:122
  143.1 18.9 %gather_fusion.1 = bf16[2048,1024]{1,0:T(8,128)(2,1)} fusion(bf16[8192,1024]{1,0:T(8,128)(2,1)} %bitcast.86, s32[2048]{0:T(1024)S(1)} %get-tuple-element.11), kind=kCustom, calls=%fused_computation.1 | custom fusion | bytes 8396800 | tf_op jit(solution)/shard_map/gather | solution.py:123
  163.2 17.9 %shard_map.64 = bf16[2,2048,1024]{2,1,0:T(8,128)(2,1)} custom-call(bf16[2048,1024]{1,0:T(8,128)(2,1)} %gather_fusion, bf16[2048,1024]{1,0:T(8,128)(2,1)} %gather_fusion.1, f32[2048,1]{1,0:T(8,128)S(1)} %copy.11.ns_ref, f32[2048,1]{1,0:T(8,128)S(1)} %copy.12.fs_ref, bf16[2048,1024]{1,0:T(8,128)(2,1)} %bitcast.90, s32[2048,1]{1,0:T(8,128)S(1)} %copy.13.ws_ref, ...), custom_call_target="tpu_custom_call" | custom-call | tf_op jit(solution)/shard_map/pallas_call | solution.py:66
  181.1 26.7 %scatter_custom_fusion.1 = bf16[6144,1024]{1,0:T(8,128)(2,1)} fusion(s32[4096]{0:T(1024)S(1)} %bitcast.105, bf16[4096,1024]{1,0:T(8,128)(2,1)} %bitcast.89, bf16[]{:T(256)} %constant.68.clone.1), kind=kCustom, calls=%fused_computation.8 | custom fusion | bytes 12583424 | tf_op jit(solution)/shard_map/scatter | solution.py:146
  207.8 2.1 fusion.10
  210.2 2.6 fusion.11
  213.1 1.9 fusion.12
  215.4 2.9 fusion.13
  218.5 2.9 fusion.14
  221.7 2.9 fusion.15
  224.8 1.8 fusion.16
  235.0 3.2 copy-done.4
  238.2 9.7 %add_convert_fusion = bf16[8,512,1024]{2,1,0:T(8,128)(2,1)} fusion(bf16[8,512,1024]{2,1,0:T(8,128)(2,1)} %copy-done.4, bf16[8,384,1024]{2,1,0:T(8,128)(2,1)S(1)} %bitcast.87, s32[16,384]{1,0:T(8,128)S(1)} %eq.46), kind=kOutput, calls=%fused_computation.6 | convolution fusion | flops 3236954112 | bytes 23093248 | tf_op jit(solution)/shard_map/osk,okf->osf/dot_general | solution.py:162
  250.8 108.7 %reduce-scatter.2.cloned.1.call-done.summed_ref = bf16[512,1024]{1,0:T(8,128)(2,1)} async-done(((bf16[4096,1024]{1,0:T(8,128)(2,1)}), bf16[512,1024]{1,0:T(8,128)(2,1)}) %reduce-scatter.2.cloned.1.call-update) | async-done | bytes 1048592 | tf_op jit(solution)/shard_map/reduce_scatter | solution.py:166
  359.5 3.3 shard_map.65
  (65 shorter events, 22.5 us)
Async XLA Ops:
  6.5 117.6 %all-gather.4.cloned.1.call-start = ((), (), s32[]{:S(2)}) async-start(), calls=%async_computation.2 | async-start | bytes 17825792 | tf_op jit(solution)/shard_map/all_gather | solution.py:111
  7.3 352.3 %reduce-scatter.2.cloned.1.call-start = ((), (), s32[]{:S(2)}) async-start(), calls=%async_computation.1 | async-start | bytes 9437184 | tf_op jit(solution)/shard_map/reduce_scatter | solution.py:166
  74.0 12.2 %copy-start.5 = (s32[2048]{0:T(1024)S(1)}, s32[2048]{0:T(1024)}, u32[]{:S(2)}) copy-start(s32[2048]{0:T(1024)} %param.10) | copy-start | bytes 24580
  74.0 12.6 %copy-start.6 = (s32[2048]{0:T(1024)S(1)}, s32[2048]{0:T(1024)}, u32[]{:S(2)}) copy-start(s32[2048]{0:T(1024)} %param.11) | copy-start | bytes 24580
  162.0 1.2 copy-start
  181.1 26.7 %copy-start.3 = (pred[16,512,384]{2,1,0:T(32,128)(4,1)S(1)}, pred[16,512,384]{2,1,0:T(32,128)(4,1)}, u32[]{:S(2)}) copy-start(pred[16,512,384]{2,1,0:T(32,128)(4,1)} %iota_compare_fusion) | copy-start | bytes 9437188
  207.8 17.1 %copy-start.1 = (bf16[6144,1024]{1,0:T(8,128)(2,1)S(1)}, bf16[6144,1024]{1,0:T(8,128)(2,1)}, u32[]{:S(2)}) copy-start(bf16[6144,1024]{1,0:T(8,128)(2,1)} %scatter_custom_fusion.1) | copy-start | bytes 37748740
  209.8 14.7 %collective-permute-start = (bf16[1,512,1024]{2,1,0:T(8,128)(2,1)S(1)}, bf16[1,512,1024]{2,1,0:T(8,128)(2,1)S(1)}, u32[]{:S(2)}, u32[]{:S(2)}) collective-permute-start(bf16[1,512,1024]{2,1,0:T(8,128)(2,1)S(1)} %fusion.10), channel_id=1, source_target_pairs={{0,8},{8,0},{1,9},{9,1},{2,10},{10,2},{3,11},{11,3},{4,12},{12,4},... | collective-permute-start | bytes 3145736 | tf_op jit(solution)/shard_map/ppermute | solution.py:160
  212.8 13.8 %collective-permute-start.1 = (bf16[1,512,1024]{2,1,0:T(8,128)(2,1)S(1)}, bf16[1,512,1024]{2,1,0:T(8,128)(2,1)S(1)}, u32[]{:S(2)}, u32[]{:S(2)}) collective-permute-start(bf16[1,512,1024]{2,1,0:T(8,128)(2,1)S(1)} %fusion.11), channel_id=1, source_target_pairs={{0,8},{8,0},{1,9},{9,1},{2,10},{10,2},{3,11},{11,3},{4,12},{12,4},... | collective-permute-start | bytes 3145736 | tf_op jit(solution)/shard_map/ppermute | solution.py:160
  215.1 13.5 %collective-permute-start.2 = (bf16[1,512,1024]{2,1,0:T(8,128)(2,1)S(1)}, bf16[1,512,1024]{2,1,0:T(8,128)(2,1)}, u32[]{:S(2)}, u32[]{:S(2)}) collective-permute-start(bf16[1,512,1024]{2,1,0:T(8,128)(2,1)S(1)} %fusion.12), channel_id=1, source_target_pairs={{0,8},{8,0},{1,9},{9,1},{2,10},{10,2},{3,11},{11,3},{4,12},{12,4},... | collective-permute-start | bytes 3145736 | tf_op jit(solution)/shard_map/ppermute | solution.py:160
  218.3 12.2 %collective-permute-start.3 = (bf16[1,512,1024]{2,1,0:T(8,128)(2,1)}, bf16[1,512,1024]{2,1,0:T(8,128)(2,1)S(1)}, u32[]{:S(2)}, u32[]{:S(2)}) collective-permute-start(bf16[1,512,1024]{2,1,0:T(8,128)(2,1)} %fusion.13), channel_id=1, source_target_pairs={{0,8},{8,0},{1,9},{9,1},{2,10},{10,2},{3,11},{11,3},{4,12},{12,4},... | collective-permute-start | bytes 3145736 | tf_op jit(solution)/shard_map/ppermute | solution.py:160
  221.4 9.2 %collective-permute-start.4 = (bf16[1,512,1024]{2,1,0:T(8,128)(2,1)}, bf16[1,512,1024]{2,1,0:T(8,128)(2,1)}, u32[]{:S(2)}, u32[]{:S(2)}) collective-permute-start(bf16[1,512,1024]{2,1,0:T(8,128)(2,1)} %fusion.14), channel_id=1, source_target_pairs={{0,8},{8,0},{1,9},{9,1},{2,10},{10,2},{3,11},{11,3},{4,12},{12,4},... | collective-permute-start | bytes 3145736 | tf_op jit(solution)/shard_map/ppermute | solution.py:160
  224.6 7.5 %collective-permute-start.5 = (bf16[1,512,1024]{2,1,0:T(8,128)(2,1)}, bf16[1,512,1024]{2,1,0:T(8,128)(2,1)}, u32[]{:S(2)}, u32[]{:S(2)}) collective-permute-start(bf16[1,512,1024]{2,1,0:T(8,128)(2,1)} %fusion.15), channel_id=1, source_target_pairs={{0,8},{8,0},{1,9},{9,1},{2,10},{10,2},{3,11},{11,3},{4,12},{12,4},... | collective-permute-start | bytes 3145736 | tf_op jit(solution)/shard_map/ppermute | solution.py:160
  226.6 7.1 %collective-permute-start.6 = (bf16[1,512,1024]{2,1,0:T(8,128)(2,1)}, bf16[1,512,1024]{2,1,0:T(8,128)(2,1)}, u32[]{:S(2)}, u32[]{:S(2)}) collective-permute-start(bf16[1,512,1024]{2,1,0:T(8,128)(2,1)} %fusion.16), channel_id=1, source_target_pairs={{0,8},{8,0},{1,9},{9,1},{2,10},{10,2},{3,11},{11,3},{4,12},{12,4},... | collective-permute-start | bytes 3145736 | tf_op jit(solution)/shard_map/ppermute | solution.py:160
  228.5 6.4 %collective-permute-start.7 = (bf16[1,512,1024]{2,1,0:T(8,128)(2,1)}, bf16[1,512,1024]{2,1,0:T(8,128)(2,1)S(1)}, u32[]{:S(2)}, u32[]{:S(2)}) collective-permute-start(bf16[1,512,1024]{2,1,0:T(8,128)(2,1)} %fusion.17), channel_id=1, source_target_pairs={{0,8},{8,0},{1,9},{9,1},{2,10},{10,2},{3,11},{11,3},{4,12},{12,4},... | collective-permute-start | bytes 3145736 | tf_op jit(solution)/shard_map/ppermute | solution.py:160
  230.6 7.7 %slice-start = ((bf16[6144,1024]{1,0:T(8,128)(2,1)}), bf16[3072,1024]{1,0:T(8,128)(2,1)S(1)}, s32[]{:S(2)}) async-start(bf16[6144,1024]{1,0:T(8,128)(2,1)} %scatter_custom_fusion.1), calls=%async_computation.3 | async-start | bytes 12582912 | tf_op jit(solution)/shard_map/slice | solution.py:163
  235.0 3.2 copy-start.4
  247.9 1.2 copy-start.2
Sparse Core Ops, SparseCore 0:
  9.8 114.3 all-gather.3
  248.1 111.3 reduce-scatter.1

commit v17 on v15

--- a/solution.py
+++ b/solution.py
@@ -158,11 +158,16 @@
             preferred_element_type=jnp.float32,
         ).astype(jnp.bfloat16)
         taken.append(lax.ppermute(give, "core", perm=[(0, 1), (1, 0)]))
-    taken = jnp.concatenate(taken, axis=0)
-    keep = jnp.einsum(
-        "osk,okf->osf", onehot[:half], slotted[:half], preferred_element_type=jnp.float32
-    )
-    chip_sum = (keep + taken.astype(jnp.float32)).astype(jnp.bfloat16)
+    chip_sum = []
+    for part, start in enumerate(range(0, half, quarter)):
+        keep = jnp.einsum(
+            "osk,okf->osf",
+            onehot[start:start + quarter],
+            slotted[start:start + quarter],
+            preferred_element_type=jnp.float32,
+        )
+        chip_sum.append((keep + taken[part].astype(jnp.float32)).astype(jnp.bfloat16))
+    chip_sum = jnp.concatenate(chip_sum, axis=0)
     summed = lax.psum_scatter(
         chip_sum.reshape(owners // 2 * station_count, full_width),
         ("z_hi", "x"),

time: 357 us -> 359 us (level)
  matrix products: 16.7 us -> 10.3 us
  other arithmetic: 18.3 us -> 22.1 us
    dot_general x1 -> x0, matrix products: 8.8 us -> none  [shards(): jnp.einsum('osk,okf->osf', onehot[:half], slotted[:half], preferred_eleme...]
    concatenate x0 -> x1, other arithmetic: none -> 3.8 us  [shards(): chip_sum = jnp.concatenate(chip_sum, axis=0)]
    dot_general x4 -> x8, matrix products: 7.87 us -> 10.3 us  [shards(): jnp.einsum('osk,okf->osf', onehot[start:start + quarter], slotted[start:s...]
  transfers between devices with their start and end apart: 6 -> 6, of which waited for: 4 -> 5; matrix products, arithmetic and copies ran while one was open for 19% -> 19% of each run, Pallas kernels for 0% -> 0%
where the time goes in v17:
time: 359 us; the launch traced here: 355 us
  waiting for transfers between devices  125 us (35%)
  local copies, waits for them, and re-layouts  115 us (32%)
  blocking collectives  46.8 us (13%)
  other arithmetic  22.1 us (6%)
  Pallas kernels  21 us (6%)
  between operations  14.1 us (4%)
  matrix products  10.3 us (3%)
    reduce_scatter x1, waiting for transfers between devices, shards(): lax.psum_scatter(chip_sum.reshape(owners // 2 * station_count, full_width...  109 us
    all_gather x1, blocking collectives, shards(): lax.all_gather(scale, ('z_hi', 'x', 'core'), axis=0, tiled=True)  29 us
    scatter x1, local copies, waits for them, and re-layouts, shards(): slotted = jnp.zeros((owners * capacity, full_width), jnp.bfloat16).at[fla...  26.7 us
    gather x1, local copies, waits for them, and re-layouts, shards(): far_raw = panel_raw[rows1]  18.9 us
    gather x1, local copies, waits for them, and re-layouts, shards(): near_raw = panel_raw[rows0]  18.9 us
    psum x1, blocking collectives, shards(): total_power = lax.psum(local_power, ('y', 'z_lo'))  17.9 us
    pallas_call x1, Pallas kernels, pair_contributions(): pl.pallas_call(pair_kernel, grid=(pairs // block,), in_specs=[pl.BlockSpe...  17.7 us
    scatter x1, local copies, waits for them, and re-layouts, shards(): slot_station = jnp.full((owners * capacity,), station_count, jnp.int32).a...  15.7 us
  transfers between devices with their start and end apart: 6, of which 5 were waited for; matrix products, arithmetic and copies ran while one was open for 19% of the time, Pallas kernels for 0%

profile of v17, /device:TPU:1, one launch (start us, length us, event | category | flops | bytes accessed | tf_op | source)
XLA Modules:
  0.0 355.0 jit_solution(463061238071108144)
XLA Ops:
  8.2 4.6 %reduce-window.6 = s32[16,32,128]{2,1,0:T(8,128)S(1)} reduce-window(s32[16,32,128]{2,1,0:T(8,128)S(1)} %fusion.33, s32[]{:T(128)} %constant.59.clone.1), window={size=1x1x128 pad=0_0x0_0x127_0}, to_apply=%region_0.0 | reduce-window | flops 8323072 | bytes 524292 | tf_op jit(solution)/shard_map/reduce-window
  13.8 17.9 %psum.7 = f32[512]{0:T(512)S(1)} all-reduce(f32[512]{0:T(512)S(1)} %fusion.18), channel_id=1, replica_groups=mesh['z_hi'=2,'x'=4,'core'=2,'y'=4,'z_lo'=2] {'y','z_lo'}, use_global_device_ids=true, to_apply=%region_5.6 | all-reduce | flops 512 | bytes 4096 | tf_op jit(solution)/shard_map/psum | solution.py:114
  31.7 29.0 %all-gather.1 = f32[16,1,512]{2,1,0:T(1,128)S(1)} all-gather(f32[1,1,512]{2,1,0:T(1,128)S(1)} %bitcast.84), channel_id=1, replica_groups=mesh['z_hi'=2,'x'=4,'core'=2,'y'=4,'z_lo'=2] {'z_hi','x','core'}, dimensions={0}, use_global_device_ids=true | all-gather | bytes 34816 | tf_op jit(solution)/shard_map/all_gather | solution.py:118
  60.6 11.8 %gather_fusion.2 = f32[2048]{0:T(1024)S(1)} fusion(f32[8192]{0:T(1024)S(1)} %bitcast.57, s32[2048]{0:T(1024)S(1)} %broadcast_clamp_fusion.1), kind=kCustom, calls=%fused_computation.2 | custom fusion | bytes 24576 | tf_op jit(solution)/shard_map/gather | solution.py:124
  72.8 11.8 %gather_fusion.3 = f32[2048]{0:T(1024)S(1)} fusion(f32[8192]{0:T(1024)S(1)} %bitcast.58, s32[2048]{0:T(1024)S(1)} %broadcast_clamp_fusion), kind=kCustom, calls=%fused_computation.3 | custom fusion | bytes 24576 | tf_op jit(solution)/shard_map/gather | solution.py:125
  85.4 1.3 copy.14.we_ref
  87.3 15.7 %scatter_custom_fusion = s32[6144]{0:T(1024)S(1)} fusion(s32[4096]{0:T(1024)S(1)} %bitcast.85, s32[4096]{0:T(1024)S(1)} %pad_add_fusion.2, s32[]{:T(128)} %constant.58.clone.1), kind=kCustom, calls=%fused_computation.99 | custom fusion | bytes 24580 | tf_op jit(solution)/shard_map/scatter | solution.py:141
  103.0 8.6 %multiply_convert_fusion = (bf16[512,1024]{1,0:T(8,128)(2,1)S(1)}, bf16[512,1024]{1,0:T(8,128)(2,1)S(1)}) fusion(), kind=kLoop, calls=%fused_computation.41 | loop fusion | flops 9961472 | bytes 2097152 | tf_op jit(solution)/shard_map/convert.1
  111.6 1.5 pad_maximum_fusion.1.table_ref
  113.1 11.1 %all-gather.4.cloned.1.call-done = bf16[8192,1,1024]{2,0,1:T(8,128)(2,1)} async-done(((bf16[512,1,1024]{2,0,1:T(8,128)(2,1)}), bf16[8192,1,1024]{2,0,1:T(8,128)(2,1)}) %all-gather.4.cloned.1.call-update) | async-done | bytes 16777232 | tf_op jit(solution)/shard_map/all_gather | solution.py:111
  124.2 18.9 %gather_fusion = bf16[2048,1024]{1,0:T(8,128)(2,1)} fusion(bf16[8192,1024]{1,0:T(8,128)(2,1)} %bitcast.59, s32[2048]{0:T(1024)S(1)} %broadcast_clamp_fusion.1), kind=kCustom, calls=%fused_computation | custom fusion | bytes 8396800 | tf_op jit(solution)/shard_map/gather | solution.py:122
  143.1 18.9 %gather_fusion.1 = bf16[2048,1024]{1,0:T(8,128)(2,1)} fusion(bf16[8192,1024]{1,0:T(8,128)(2,1)} %bitcast.60, s32[2048]{0:T(1024)S(1)} %broadcast_clamp_fusion), kind=kCustom, calls=%fused_computation.1 | custom fusion | bytes 8396800 | tf_op jit(solution)/shard_map/gather | solution.py:123
  163.2 17.7 %shard_map.64 = bf16[2,2048,1024]{2,1,0:T(8,128)(2,1)} custom-call(bf16[2048,1024]{1,0:T(8,128)(2,1)} %gather_fusion, bf16[2048,1024]{1,0:T(8,128)(2,1)} %gather_fusion.1, f32[2048,1]{1,0:T(8,128)S(1)} %copy.11.ns_ref, f32[2048,1]{1,0:T(8,128)S(1)} %copy.12.fs_ref, bf16[2048,1024]{1,0:T(8,128)(2,1)} %bitcast.63, s32[2048,1]{1,0:T(8,128)S(1)} %copy.13.ws_ref, ...), custom_call_target="tpu_custom_call" | custom-call | tf_op jit(solution)/shard_map/pallas_call | solution.py:66
  181.0 26.7 %scatter_custom_fusion.1 = bf16[6144,1024]{1,0:T(8,128)(2,1)} fusion(s32[4096]{0:T(1024)S(1)} %bitcast.86, bf16[4096,1024]{1,0:T(8,128)(2,1)} %bitcast.62, bf16[]{:T(256)} %constant.68.clone.1), kind=kCustom, calls=%fused_computation.16 | custom fusion | bytes 12583424 | tf_op jit(solution)/shard_map/scatter | solution.py:146
  207.7 5.4 %fusion.53 = (bf16[768,1024]{1,0:T(8,128)(2,1)S(1)}, bf16[768,1024]{1,0:T(8,128)(2,1)S(1)}, bf16[768,1024]{1,0:T(8,128)(2,1)S(1)}, bf16[768,1024]{1,0:T(8,128)(2...) fusion(bf16[6144,1024]{1,0:T(8,128)(2,1)} %scatter_custom_fusion.1), kind=kLoop, calls=%fused_computation.104 | loop fusion | bytes 25165824 | tf_op jit(solution)/shard_map/slice | solution.py:157
  213.1 1.3 fusion.29
  214.7 1.3 fusion.28
  222.9 1.7 collective-permute-done.1
  225.9 1.7 collective-permute-done
  227.6 1.3 add_convert_fusion.3
  228.9 3.8 %pad_maximum_fusion = bf16[8,512,1024]{2,1,0:T(8,128)(2,1)} fusion(bf16[2,512,1024]{2,1,0:T(8,128)(2,1)S(1)} %add_convert_fusion, bf16[2,512,1024]{2,1,0:T(8,128)(2,1)S(1)} %add_convert_fusion.1, bf16[2,512,1024]{2,1,0:T(8,128)(2,1)S(1)} %add_convert_fusion.2, bf16[2,512,1024]{2,1,0:T(8,128)(2,1)S(1)} %add_convert_fusion.3), kind=kLoop, calls=%fused_computation.15 | loop fusion | flops 12582912 | bytes 16777216 | tf_op jit(solution)/shard_map/concatenate | solution.py:170
  234.0 1.7 fusion.19.own_ref
  235.6 108.8 %reduce-scatter.2.cloned.1.call-done.summed_ref = bf16[512,1024]{1,0:T(8,128)(2,1)} async-done(((bf16[4096,1024]{1,0:T(8,128)(2,1)}), bf16[512,1024]{1,0:T(8,128)(2,1)}) %reduce-scatter.2.cloned.1.call-update) | async-done | bytes 1048592 | tf_op jit(solution)/shard_map/reduce_scatter | solution.py:171
  344.5 3.3 shard_map.65
  (44 shorter events, 15.1 us)
Async XLA Ops:
  6.5 7.0 %copy-start.1 = (bf16[512,1,1024]{2,0,1:T(8,128)(2,1)S(1)}, bf16[512,1,1024]{2,0,1:T(8,128)(2,1)}, u32[]{:S(2)}) copy-start(bf16[512,1,1024]{2,0,1:T(8,128)(2,1)} %param.6) | copy-start | bytes 3145732
  6.5 117.6 %all-gather.4.cloned.1.call-start = ((), (), s32[]{:S(2)}) async-start(), calls=%async_computation.2 | async-start | bytes 17825792 | tf_op jit(solution)/shard_map/all_gather | solution.py:111
  7.3 337.2 %reduce-scatter.2.cloned.1.call-start = ((), (), s32[]{:S(2)}) async-start(), calls=%async_computation.1 | async-start | bytes 9437184 | tf_op jit(solution)/shard_map/reduce_scatter | solution.py:171
  72.8 12.2 %copy-start.3 = (s32[2048]{0:T(1024)S(1)}, s32[2048]{0:T(1024)}, u32[]{:S(2)}) copy-start(s32[2048]{0:T(1024)} %param.10) | copy-start | bytes 24580
  84.6 0.8 copy-start.4
  162.0 1.2 copy-start
  214.4 5.4 %collective-permute-start.3 = (bf16[2,512,1024]{2,1,0:T(8,128)(2,1)S(1)}, bf16[2,512,1024]{2,1,0:T(8,128)(2,1)S(1)}, u32[]{:S(2)}, u32[]{:S(2)}) collective-permute-start(bf16[2,512,1024]{2,1,0:T(8,128)(2,1)S(1)} %fusion.29), channel_id=1, source_target_pairs={{0,8},{8,0},{1,9},{9,1},{2,10},{10,2},{3,11},{11,3},{4,12},{12,4},... | collective-permute-start | bytes 6291464 | tf_op jit(solution)/shard_map/ppermute | solution.py:160
  216.0 5.6 %collective-permute-start.2 = (bf16[2,512,1024]{2,1,0:T(8,128)(2,1)S(1)}, bf16[2,512,1024]{2,1,0:T(8,128)(2,1)S(1)}, u32[]{:S(2)}, u32[]{:S(2)}) collective-permute-start(bf16[2,512,1024]{2,1,0:T(8,128)(2,1)S(1)} %fusion.28), channel_id=1, source_target_pairs={{0,8},{8,0},{1,9},{9,1},{2,10},{10,2},{3,11},{11,3},{4,12},{12,4},... | collective-permute-start | bytes 6291464 | tf_op jit(solution)/shard_map/ppermute | solution.py:160
  217.9 6.7 %collective-permute-start.1 = (bf16[2,512,1024]{2,1,0:T(8,128)(2,1)S(1)}, bf16[2,512,1024]{2,1,0:T(8,128)(2,1)S(1)}, u32[]{:S(2)}, u32[]{:S(2)}) collective-permute-start(bf16[2,512,1024]{2,1,0:T(8,128)(2,1)S(1)} %fusion.27), channel_id=1, source_target_pairs={{0,8},{8,0},{1,9},{9,1},{2,10},{10,2},{3,11},{11,3},{4,12},{12,4},... | collective-permute-start | bytes 6291464 | tf_op jit(solution)/shard_map/ppermute | solution.py:160
  219.5 8.1 %collective-permute-start = (bf16[2,512,1024]{2,1,0:T(8,128)(2,1)S(1)}, bf16[2,512,1024]{2,1,0:T(8,128)(2,1)S(1)}, u32[]{:S(2)}, u32[]{:S(2)}) collective-permute-start(bf16[2,512,1024]{2,1,0:T(8,128)(2,1)S(1)} %fusion.26), channel_id=1, source_target_pairs={{0,8},{8,0},{1,9},{9,1},{2,10},{10,2},{3,11},{11,3},{4,12},{12,4},... | collective-permute-start | bytes 6291464 | tf_op jit(solution)/shard_map/ppermute | solution.py:160
  232.8 1.2 copy-start.2
Sparse Core Ops, SparseCore 0:
  9.8 114.3 all-gather.3
  232.9 111.5 reduce-scatter.1

commit v18 on v17

--- a/solution.py
+++ b/solution.py
@@ -159,14 +159,15 @@
         ).astype(jnp.bfloat16)
         taken.append(lax.ppermute(give, "core", perm=[(0, 1), (1, 0)]))
     chip_sum = []
-    for part, start in enumerate(range(0, half, quarter)):
+    for part, start in enumerate(range(0, half, 2 * quarter)):
         keep = jnp.einsum(
             "osk,okf->osf",
-            onehot[start:start + quarter],
-            slotted[start:start + quarter],
+            onehot[start:start + 2 * quarter],
+            slotted[start:start + 2 * quarter],
             preferred_element_type=jnp.float32,
         )
-        chip_sum.append((keep + taken[part].astype(jnp.float32)).astype(jnp.bfloat16))
+        arrived = jnp.concatenate(taken[2 * part:2 * part + 2], axis=0)
+        chip_sum.append((keep + arrived.astype(jnp.float32)).astype(jnp.bfloat16))
     chip_sum = jnp.concatenate(chip_sum, axis=0)
     summed = lax.psum_scatter(
         chip_sum.reshape(owners // 2 * station_count, full_width),

time: 359 us -> 363 us (1.011)
  matrix products: 10.3 us -> 20.1 us
  waiting for transfers between devices: 125 us -> 119 us
  other arithmetic: 22.1 us -> 27 us
    dot_general x0 -> x2, matrix products: none -> 10.9 us  [shards(): jnp.einsum('osk,okf->osf', onehot[start:start + 2 * quarter], slotted[sta...]
    ppermute x4, waiting for transfers between devices: 3.95 us -> 0.01 us  [shards(): taken.append(lax.ppermute(give, 'core', perm=[(0, 1), (1, 0)]))]
    concatenate x1, other arithmetic: 3.8 us -> 7.52 us  [shards(): chip_sum = jnp.concatenate(chip_sum, axis=0)]
    dot_general x8 -> x4, matrix products: 10.3 us -> 9.15 us  [shards(): jnp.einsum('osk,okf->osf', onehot[start:start + quarter], slotted[start:s...]
  transfers between devices with their start and end apart: 6 -> 6, of which waited for: 5 -> 2; matrix products, arithmetic and copies ran while one was open for 19% -> 21% of each run, Pallas kernels for 0% -> 0%
where the time goes in v18:
time: 363 us; the launch traced here: 362 us
  waiting for transfers between devices  119 us (33%)
  local copies, waits for them, and re-layouts  113 us (31%)
  blocking collectives  46.9 us (13%)
  other arithmetic  27 us (7%)
  Pallas kernels  21 us (6%)
  matrix products  20.1 us (6%)
  between operations  13.6 us (4%)
    reduce_scatter x1, waiting for transfers between devices, shards(): lax.psum_scatter(chip_sum.reshape(owners // 2 * station_count, full_width...  109 us
    all_gather x1, blocking collectives, shards(): lax.all_gather(scale, ('z_hi', 'x', 'core'), axis=0, tiled=True)  28.9 us
    scatter x1, local copies, waits for them, and re-layouts, shards(): slotted = jnp.zeros((owners * capacity, full_width), jnp.bfloat16).at[fla...  26.7 us
    gather x1, local copies, waits for them, and re-layouts, shards(): near_raw = panel_raw[rows0]  18.9 us
    gather x1, local copies, waits for them, and re-layouts, shards(): far_raw = panel_raw[rows1]  18.9 us
    psum x1, blocking collectives, shards(): total_power = lax.psum(local_power, ('y', 'z_lo'))  18 us
    pallas_call x1, Pallas kernels, pair_contributions(): pl.pallas_call(pair_kernel, grid=(pairs // block,), in_specs=[pl.BlockSpe...  17.7 us
    scatter x1, local copies, waits for them, and re-layouts, shards(): slot_station = jnp.full((owners * capacity,), station_count, jnp.int32).a...  15.7 us
  transfers between devices with their start and end apart: 6, of which 2 were waited for; matrix products, arithmetic and copies ran while one was open for 21% of the time, Pallas kernels for 0%

profile of v18, /device:TPU:1, one launch (start us, length us, event | category | flops | bytes accessed | tf_op | source)
XLA Modules:
  0.0 362.4 jit_solution(14593155664250980033)
XLA Ops:
  8.2 4.6 %reduce-window.6 = s32[16,32,128]{2,1,0:T(8,128)S(1)} reduce-window(s32[16,32,128]{2,1,0:T(8,128)S(1)} %fusion.29, s32[]{:T(128)} %constant.59.clone.1), window={size=1x1x128 pad=0_0x0_0x127_0}, to_apply=%region_0.0 | reduce-window | flops 8323072 | bytes 524292 | tf_op jit(solution)/shard_map/reduce-window
  13.5 1.5 fusion.14
  15.0 18.0 %psum.7 = f32[512]{0:T(512)S(1)} all-reduce(f32[512]{0:T(512)S(1)} %fusion.14), channel_id=1, replica_groups=mesh['z_hi'=2,'x'=4,'core'=2,'y'=4,'z_lo'=2] {'y','z_lo'}, use_global_device_ids=true, to_apply=%region_5.6 | all-reduce | flops 512 | bytes 4096 | tf_op jit(solution)/shard_map/psum | solution.py:114
  33.0 28.9 %all-gather.1 = f32[16,1,512]{2,1,0:T(1,128)S(1)} all-gather(f32[1,1,512]{2,1,0:T(1,128)S(1)} %bitcast.80), channel_id=1, replica_groups=mesh['z_hi'=2,'x'=4,'core'=2,'y'=4,'z_lo'=2] {'z_hi','x','core'}, dimensions={0}, use_global_device_ids=true | all-gather | bytes 34816 | tf_op jit(solution)/shard_map/all_gather | solution.py:118
  61.9 11.8 %gather_fusion.2 = f32[2048]{0:T(1024)S(1)} fusion(f32[8192]{0:T(1024)S(1)} %bitcast.53, s32[2048]{0:T(1024)S(1)} %broadcast_clamp_fusion.1), kind=kCustom, calls=%fused_computation.2 | custom fusion | bytes 24576 | tf_op jit(solution)/shard_map/gather | solution.py:124
  74.1 11.8 %gather_fusion.3 = f32[2048]{0:T(1024)S(1)} fusion(f32[8192]{0:T(1024)S(1)} %bitcast.54, s32[2048]{0:T(1024)S(1)} %broadcast_clamp_fusion), kind=kCustom, calls=%fused_computation.3 | custom fusion | bytes 24576 | tf_op jit(solution)/shard_map/gather | solution.py:125
  88.5 15.7 %scatter_custom_fusion = s32[6144]{0:T(1024)S(1)} fusion(s32[4096]{0:T(1024)S(1)} %bitcast.81, s32[4096]{0:T(1024)S(1)} %pad_add_fusion.2, s32[]{:T(128)} %constant.58.clone.1), kind=kCustom, calls=%fused_computation.93 | custom fusion | bytes 24580 | tf_op jit(solution)/shard_map/scatter | solution.py:141
  104.3 8.6 %multiply_convert_fusion = (bf16[512,1024]{1,0:T(8,128)(2,1)S(1)}, bf16[512,1024]{1,0:T(8,128)(2,1)S(1)}) fusion(), kind=kLoop, calls=%fused_computation.35 | loop fusion | flops 9961472 | bytes 2097152 | tf_op jit(solution)/shard_map/convert.1
  112.8 1.6 pad_maximum_fusion.1.table_ref
  114.4 9.7 %all-gather.4.cloned.1.call-done = bf16[8192,1,1024]{2,0,1:T(8,128)(2,1)} async-done(((bf16[512,1,1024]{2,0,1:T(8,128)(2,1)}), bf16[8192,1,1024]{2,0,1:T(8,128)(2,1)}) %all-gather.4.cloned.1.call-update) | async-done | bytes 16777232 | tf_op jit(solution)/shard_map/all_gather | solution.py:111
  124.1 18.9 %gather_fusion = bf16[2048,1024]{1,0:T(8,128)(2,1)} fusion(bf16[8192,1024]{1,0:T(8,128)(2,1)} %bitcast.55, s32[2048]{0:T(1024)S(1)} %broadcast_clamp_fusion.1), kind=kCustom, calls=%fused_computation | custom fusion | bytes 8396800 | tf_op jit(solution)/shard_map/gather | solution.py:122
  143.0 18.9 %gather_fusion.1 = bf16[2048,1024]{1,0:T(8,128)(2,1)} fusion(bf16[8192,1024]{1,0:T(8,128)(2,1)} %bitcast.56, s32[2048]{0:T(1024)S(1)} %broadcast_clamp_fusion), kind=kCustom, calls=%fused_computation.1 | custom fusion | bytes 8396800 | tf_op jit(solution)/shard_map/gather | solution.py:123
  163.1 17.7 %shard_map.64 = bf16[2,2048,1024]{2,1,0:T(8,128)(2,1)} custom-call(bf16[2048,1024]{1,0:T(8,128)(2,1)} %gather_fusion, bf16[2048,1024]{1,0:T(8,128)(2,1)} %gather_fusion.1, f32[2048,1]{1,0:T(8,128)S(1)} %copy.11.ns_ref, f32[2048,1]{1,0:T(8,128)S(1)} %copy.12.fs_ref, bf16[2048,1024]{1,0:T(8,128)(2,1)} %bitcast.61, s32[2048,1]{1,0:T(8,128)S(1)} %copy.13.ws_ref, ...), custom_call_target="tpu_custom_call" | custom-call | tf_op jit(solution)/shard_map/pallas_call | solution.py:66
  180.8 26.7 %scatter_custom_fusion.1 = bf16[6144,1024]{1,0:T(8,128)(2,1)} fusion(s32[4096]{0:T(1024)S(1)} %bitcast.82, bf16[4096,1024]{1,0:T(8,128)(2,1)} %bitcast.60, bf16[]{:T(256)} %constant.68.clone.1), kind=kCustom, calls=%fused_computation.16 | custom fusion | bytes 12583424 | tf_op jit(solution)/shard_map/scatter | solution.py:146
  207.6 3.6 fusion.49
  212.8 2.6 fusion.24
  215.6 2.6 fusion.23
  218.5 2.6 fusion.22
  222.1 5.4 %add_convert_fusion = bf16[4,512,1024]{2,1,0:T(8,128)(2,1)} fusion(bf16[2,512,1024]{2,1,0:T(8,128)(2,1)S(1)} %collective-permute-done.3, bf16[2,512,1024]{2,1,0:T(8,128)(2,1)} %collective-permute-done.2, bf16[4,384,1024]{2,1,0:T(8,128)(2,1)S(1)} %bitcast.63, s32[16,384]{1,0:T(8,128)S(1)} %eq.46), kind=kOutput, calls=%fused_computation.14 | convolution fusion | flops 1622147072 | bytes 11558912 | tf_op jit(solution)/shard_map/osk,okf->osf/dot_general | solution.py:163
  227.6 5.5 %add_convert_fusion.1 = bf16[4,512,1024]{2,1,0:T(8,128)(2,1)} fusion(bf16[2,512,1024]{2,1,0:T(8,128)(2,1)S(1)} %collective-permute-done.1, bf16[2,512,1024]{2,1,0:T(8,128)(2,1)} %collective-permute-done, bf16[4,384,1024]{2,1,0:T(8,128)(2,1)S(1)} %bitcast.62, s32[16,384]{1,0:T(8,128)S(1)} %eq.46), kind=kOutput, calls=%fused_computation.15 | convolution fusion | flops 1622147072 | bytes 11558912 | tf_op jit(solution)/shard_map/osk,okf->osf/dot_general | solution.py:163
  233.1 7.5 %pad_maximum_fusion = bf16[8,512,1024]{2,1,0:T(8,128)(2,1)} fusion(bf16[4,512,1024]{2,1,0:T(8,128)(2,1)} %add_convert_fusion, bf16[4,512,1024]{2,1,0:T(8,128)(2,1)} %add_convert_fusion.1), kind=kLoop, calls=%fused_computation.13 | loop fusion | flops 4194304 | bytes 16777216 | tf_op jit(solution)/shard_map/concatenate | solution.py:171
  241.8 1.6 fusion.15.own_ref
  243.4 108.9 %reduce-scatter.2.cloned.1.call-done.summed_ref = bf16[512,1024]{1,0:T(8,128)(2,1)} async-done(((bf16[4096,1024]{1,0:T(8,128)(2,1)}), bf16[512,1024]{1,0:T(8,128)(2,1)}) %reduce-scatter.2.cloned.1.call-update) | async-done | bytes 1048592 | tf_op jit(solution)/shard_map/reduce_scatter | solution.py:172
  352.3 3.3 shard_map.65
  (48 shorter events, 10.8 us)
Async XLA Ops:
  6.5 117.5 %all-gather.4.cloned.1.call-start = ((), (), s32[]{:S(2)}) async-start(), calls=%async_computation.2 | async-start | bytes 17825792 | tf_op jit(solution)/shard_map/all_gather | solution.py:111
  7.3 345.1 %reduce-scatter.2.cloned.1.call-start = ((), (), s32[]{:S(2)}) async-start(), calls=%async_computation.1 | async-start | bytes 9437184 | tf_op jit(solution)/shard_map/reduce_scatter | solution.py:172
  74.0 12.2 %copy-start.2 = (s32[2048]{0:T(1024)S(1)}, s32[2048]{0:T(1024)}, u32[]{:S(2)}) copy-start(s32[2048]{0:T(1024)} %param.10) | copy-start | bytes 24580
  74.1 12.6 %copy-start.3 = (s32[2048]{0:T(1024)S(1)}, s32[2048]{0:T(1024)}, u32[]{:S(2)}) copy-start(s32[2048]{0:T(1024)} %param.11) | copy-start | bytes 24580
  161.9 1.2 copy-start
  212.4 9.7 %collective-permute-start.3 = (bf16[2,512,1024]{2,1,0:T(8,128)(2,1)S(1)}, bf16[2,512,1024]{2,1,0:T(8,128)(2,1)S(1)}, u32[]{:S(2)}, u32[]{:S(2)}) collective-permute-start(bf16[2,512,1024]{2,1,0:T(8,128)(2,1)S(1)} %fusion.25), channel_id=1, source_target_pairs={{0,8},{8,0},{1,9},{9,1},{2,10},{10,2},{3,11},{11,3},{4,12},{12,4},... | collective-permute-start | bytes 6291464 | tf_op jit(solution)/shard_map/ppermute | solution.py:160
  212.8 8.6 %slice-start = ((s8[12582912]{0:T(1024)(128)(4,1)}), s8[4194304]{0:T(1024)(128)(4,1)S(1)}, s32[]{:S(2)}) async-start(s8[12582912]{0:T(1024)(128)(4,1)} %bitcast.57), calls=%async_computation.3 | async-start | bytes 8388608
  215.4 6.8 %collective-permute-start.2 = (bf16[2,512,1024]{2,1,0:T(8,128)(2,1)}, bf16[2,512,1024]{2,1,0:T(8,128)(2,1)}, u32[]{:S(2)}, u32[]{:S(2)}) collective-permute-start(bf16[2,512,1024]{2,1,0:T(8,128)(2,1)} %fusion.24), channel_id=1, source_target_pairs={{0,8},{8,0},{1,9},{9,1},{2,10},{10,2},{3,11},{11,3},{4,12},{12,4},... | collective-permute-start | bytes 6291464 | tf_op jit(solution)/shard_map/ppermute | solution.py:160
  215.6 5.8 %slice-start.1 = ((s8[12582912]{0:T(1024)(128)(4,1)}), s8[4194304]{0:T(1024)(128)(4,1)S(1)}, s32[]{:S(2)}) async-start(s8[12582912]{0:T(1024)(128)(4,1)} %bitcast.57), calls=%async_computation.4 | async-start | bytes 8388608
  218.3 3.1 slice-start.2
  218.3 9.3 %collective-permute-start.1 = (bf16[2,512,1024]{2,1,0:T(8,128)(2,1)}, bf16[2,512,1024]{2,1,0:T(8,128)(2,1)S(1)}, u32[]{:S(2)}, u32[]{:S(2)}) collective-permute-start(bf16[2,512,1024]{2,1,0:T(8,128)(2,1)} %fusion.23), channel_id=1, source_target_pairs={{0,8},{8,0},{1,9},{9,1},{2,10},{10,2},{3,11},{11,3},{4,12},{12,4},... | collective-permute-start | bytes 6291464 | tf_op jit(solution)/shard_map/ppermute | solution.py:160
  221.1 6.5 %collective-permute-start = (bf16[2,512,1024]{2,1,0:T(8,128)(2,1)}, bf16[2,512,1024]{2,1,0:T(8,128)(2,1)}, u32[]{:S(2)}, u32[]{:S(2)}) collective-permute-start(bf16[2,512,1024]{2,1,0:T(8,128)(2,1)} %fusion.22), channel_id=1, source_target_pairs={{0,8},{8,0},{1,9},{9,1},{2,10},{10,2},{3,11},{11,3},{4,12},{12,4},... | collective-permute-start | bytes 6291464 | tf_op jit(solution)/shard_map/ppermute | solution.py:160
  240.6 1.2 copy-start.1
Sparse Core Ops, SparseCore 0:
  9.8 114.2 all-gather.3
  240.7 111.5 reduce-scatter.1
